TPU v7x, 256 devices: a whole 4x4x8 slice. The times are simulated.
256 devices in a mesh: batch: 8 (over z), replica: 32 (over y, x, core).
Axes of the slice: x: 4, y: 4, z: 8, core: 2. Of those that a mesh axis runs over, the one named last changes fastest.
Arguments:
- patches: bfloat16 [32, 64, 64, 1024], P('replica', 'batch'), may hold values from -6 to 6
- visible_order: int32 [32, 64, 64], P('replica', 'batch'), may hold values from 0 to 63, each once within a row
- visible_counts: int32 [32, 64], P('replica'), may hold values from 1 to 32, as said below
- dest_rows: int32 [32, 64], P('replica'), may hold values from 0 to 1023, as said below
- qkv_weight: bfloat16 [1024, 3072], P('replica')
- out_weight: bfloat16 [1024, 1024], P('replica'), may hold values from -0.1875 to 0.1875
- norm_gain: bfloat16 [1024], P('replica'), may hold values from 0.5 to 1.5
- upstream: bfloat16 [32, 1024, 1024], P('replica', 'batch'), may hold values from -6 to 6
Outputs:
- layer_out: bfloat16 [32, 1024, 1024], P('replica', 'batch')
- d_packed: bfloat16 [32, 1024, 1024], P('replica', 'batch')
- grad_qkv: float32 [1024, 3072], P('replica')
- grad_out: float32 [1024, 1024], P('replica')
- grad_gain: float32 [1024], P('replica')
Inputs may be any that keep to these rules, and one draw needn't show every extreme that they name: `visible_counts`: in every replica index, each batch index b packs exactly 128 rows: the volumes with dest_rows // 128 == b, one from every device of the batch axis, in order of that device's batch index, without gaps; one of them has 32 visible patches. `dest_rows`: the 8 volumes of one device go to 8 different batch indices; a volume's rows never cross a multiple of 128.
All inputs are finite; a program needn't handle non-finite values.
Results may differ from a plain program's by a relative error of at most 0.033.
Values may be sent and summed in bfloat16 or wider, within the bound.
No kernel may reach another device: no remote copies, remote signals or barrier semaphores. Data moves between devices by JAX's collectives and lax.ppermute only.
A program may use at most 128 MiB of HBM per device.

v0:
```python
import jax
import jax.numpy as jnp
from jax import lax
from jax.sharding import PartitionSpec as P

HEADS = 16
MAXVIS = 32
MEANVIS = 16


EPS = 1e-06
NEG = -1e30


def layer_core(tokens, upward, allowed, wqkv, wout, gain):
    groups, length, width = tokens.shape
    rows = groups * length
    head_dim = width // HEADS
    scale = head_dim ** (-0.5)
    x32 = tokens.astype(jnp.float32).reshape(rows, width)
    row_average = jnp.mean(x32, axis=1, keepdims=True)
    centered_rows = x32 - row_average
    inverse_deviation = lax.rsqrt(
        jnp.mean(centered_rows * centered_rows, axis=1, keepdims=True) + EPS
    )
    standardized_rows = centered_rows * inverse_deviation
    gain_float32 = gain.astype(jnp.float32)
    layernorm_output = (standardized_rows * gain_float32).astype(jnp.bfloat16)
    qkv = jnp.dot(layernorm_output, wqkv, preferred_element_type=jnp.float32).astype(jnp.bfloat16)
    query = qkv[:, :width].reshape(groups, length, HEADS, head_dim)
    keys = qkv[:, width : 2 * width].reshape(groups, length, HEADS, head_dim)
    values = qkv[:, 2 * width :].reshape(groups, length, HEADS, head_dim)
    scores = jnp.einsum("gqhd,gkhd->ghqk", query, keys, preferred_element_type=jnp.float32) * scale
    scores = jnp.where(allowed[:, None], scores, NEG)
    top = jnp.max(scores, axis=-1, keepdims=True)
    expd = jnp.exp(scores - top)
    probs = expd / jnp.sum(expd, axis=-1, keepdims=True)
    weights = probs.astype(jnp.bfloat16)
    context = (
        jnp.einsum("ghqk,gkhd->gqhd", weights, values, preferred_element_type=jnp.float32)
        .astype(jnp.bfloat16)
        .reshape(rows, width)
    )
    result = (x32 + jnp.dot(context, wout, preferred_element_type=jnp.float32)).astype(jnp.bfloat16)
    up_rows = upward.reshape(rows, width)
    d_context = lax.dot_general(
        up_rows, wout, (((1,), (1,)), ((), ())), preferred_element_type=jnp.float32
    ).astype(jnp.bfloat16)
    d_context = d_context.reshape(groups, length, HEADS, head_dim)
    d_values = jnp.einsum(
        "ghqk,gqhd->gkhd", weights, d_context, preferred_element_type=jnp.float32
    ).astype(jnp.bfloat16)
    d_weights = jnp.einsum("gqhd,gkhd->ghqk", d_context, values, preferred_element_type=jnp.float32)
    d_scores = (
        probs * (d_weights - jnp.sum(d_weights * probs, axis=-1, keepdims=True)) * scale
    ).astype(jnp.bfloat16)
    d_query = jnp.einsum(
        "ghqk,gkhd->gqhd", d_scores, keys, preferred_element_type=jnp.float32
    ).astype(jnp.bfloat16)
    d_keys = jnp.einsum(
        "ghqk,gqhd->gkhd", d_scores, query, preferred_element_type=jnp.float32
    ).astype(jnp.bfloat16)
    d_qkv = jnp.concatenate(
        [d_query.reshape(rows, width), d_keys.reshape(rows, width), d_values.reshape(rows, width)],
        axis=1,
    )
    layernorm_gradient = lax.dot_general(
        d_qkv, wqkv, (((1,), (1,)), ((), ())), preferred_element_type=jnp.float32
    )
    gain_products = jnp.sum(layernorm_gradient * standardized_rows, axis=0)
    normalized_gradient = layernorm_gradient * gain_float32
    input_gradient = inverse_deviation * (
        normalized_gradient
        - jnp.mean(normalized_gradient, axis=1, keepdims=True)
        - standardized_rows
        * jnp.mean(normalized_gradient * standardized_rows, axis=1, keepdims=True)
    )
    d_tokens = (up_rows.astype(jnp.float32) + input_gradient).astype(jnp.bfloat16)
    return (
        result.reshape(tokens.shape),
        d_tokens.reshape(tokens.shape),
        layernorm_output,
        context,
        d_qkv,
        up_rows,
        gain_products,
    )


def left_product(left, right):
    return lax.dot_general(
        left, right, (((0,), (0,)), ((), ())), preferred_element_type=jnp.float32
    )


def on_device(
    patches, visible_order, visible_counts, dest_rows, qkv_weight, out_weight, norm_gain, upstream
):
    wqkv, wout, gain = (
        lax.all_gather(qkv_weight, "replica", axis=0, tiled=True),
        lax.all_gather(out_weight, "replica", axis=0, tiled=True),
        lax.all_gather(norm_gain, "replica", axis=0, tiled=True),
    )
    batches = lax.axis_size("batch")
    me_index = lax.axis_index("batch")
    cap = MEANVIS * batches
    width = wout.shape[1]
    slot = jnp.arange(MAXVIS, dtype=jnp.int32)
    sources = jnp.arange(batches, dtype=jnp.int32)
    counts_all = visible_counts[0].reshape(batches, batches)
    rows_all = dest_rows[0].reshape(batches, batches)
    mine = rows_all // cap == me_index
    src_count = jnp.sum(jnp.where(mine, counts_all, 0), axis=1)
    src_start = jnp.sum(jnp.where(mine, rows_all % cap, 0), axis=1)
    position = jnp.arange(cap, dtype=jnp.int32)
    hit = (position[:, None] >= src_start[None, :]) & (
        position[:, None] < (src_start + src_count)[None, :]
    )
    segment = jnp.sum(jnp.where(hit, sources[None, :], 0), axis=1)
    inside = jnp.sum(jnp.where(hit, position[:, None] - src_start[None, :], 0), axis=1)
    flat_rows = segment * MAXVIS + inside
    my_targets = jnp.take(rows_all, me_index, axis=0) // cap
    to_target = jnp.sum(
        jnp.where(my_targets[None, :] == sources[:, None], sources[None, :], 0), axis=1
    )
    my_counts = jnp.take(counts_all, me_index, axis=0)
    local_rows = jnp.take_along_axis(patches[0], visible_order[0, :, :MAXVIS, None], axis=1)
    live = slot[None, :] < src_count[:, None]
    pick = jnp.clip(src_start[:, None] + slot[None, :], 0, cap - 1)
    fetched = jnp.take(upstream[0], pick.reshape(-1), axis=0).reshape(batches, MAXVIS, width)
    backward_rows = jnp.where(live[..., None], fetched, jnp.zeros_like(fetched))
    returned = lax.all_to_all(backward_rows, "batch", split_axis=0, concat_axis=0, tiled=True)
    upward = jnp.take(returned, my_targets, axis=0)
    valid = slot[None, :] < my_counts[:, None]
    allowed = jnp.broadcast_to(valid[:, None, :], (batches, MAXVIS, MAXVIS))
    result, d_tokens, layernorm_output, context, d_qkv, up_rows, gain_products = layer_core(
        local_rows, upward, allowed, wqkv, wout, gain
    )
    came_out, came_grad = (
        lax.all_to_all(
            jnp.take(result, to_target, axis=0), "batch", split_axis=0, concat_axis=0, tiled=True
        ),
        lax.all_to_all(
            jnp.take(d_tokens, to_target, axis=0), "batch", split_axis=0, concat_axis=0, tiled=True
        ),
    )
    layer_out = jnp.take(came_out.reshape(batches * MAXVIS, width), flat_rows, axis=0)
    d_packed = jnp.take(came_grad.reshape(batches * MAXVIS, width), flat_rows, axis=0)
    grad_q = lax.psum_scatter(
        left_product(layernorm_output, d_qkv).astype(jnp.bfloat16),
        "replica",
        scatter_dimension=0,
        tiled=True,
    ).astype(jnp.float32)
    grad_o, grad_g = (
        lax.psum_scatter(
            left_product(context, up_rows).astype(jnp.bfloat16),
            "replica",
            scatter_dimension=0,
            tiled=True,
        ).astype(jnp.float32),
        lax.psum_scatter(
            gain_products.astype(jnp.bfloat16), "replica", scatter_dimension=0, tiled=True
        ).astype(jnp.float32),
    )
    grad_q, grad_o, grad_g = (
        lax.psum(grad_q.astype(jnp.bfloat16), "batch").astype(jnp.float32),
        lax.psum(grad_o.astype(jnp.bfloat16), "batch").astype(jnp.float32),
        lax.psum(grad_g.astype(jnp.bfloat16), "batch").astype(jnp.float32),
    )
    return (layer_out[None], d_packed[None], grad_q, grad_o, grad_g)


def solution(mesh):
    placed = (
        P("replica", "batch", None, None),
        P("replica", "batch", None),
        P("replica", None),
        P("replica", None),
        P("replica", None),
        P("replica", None),
        P("replica"),
        P("replica", "batch", None),
    )
    return jax.shard_map(
        on_device,
        mesh=mesh,
        in_specs=placed,
        out_specs=(
            P("replica", "batch", None),
            P("replica", "batch", None),
            P("replica", None),
            P("replica", None),
            P("replica"),
        ),
        check_vma=False,
    )
```

profile of v0, /device:TPU:2, one launch (start us, length us, event | category | flops | bytes accessed | tf_op | source)
XLA Modules:
  0.0 393.7 jit_solution(1787826674265752297)
XLA Ops:
  8.4 1.3 reduce.8
  9.8 1.3 reduce.9
  11.6 2.5 gather_fusion
  14.2 1.0 select_select_fusion
  15.2 8.5 %all-to-all-start.1 = ((bf16[8,32,1024]{2,1,0:T(8,128)(2,1)}), bf16[8,32,1024]{2,1,0:T(8,128)(2,1)S(1)}, u32[]{:S(2)}, u32[]{:S(2)}) async-start(bf16[8,32,1024]{2,1,0:T(8,128)(2,1)} %select_select_fusion), calls=%async_computation.1 | async-start | bytes 1048576 | tf_op jit(solution)/shard_map/all_to_all | solution.py:132
  23.7 0.7 all-gather.5.cloned.1.call-update
  24.5 2.8 gather_fusion.1
  29.6 62.8 %all-reduce = bf16[1024]{0:T(1024)(128)(2,1)S(1)} all-reduce(bf16[1024]{0:T(1024)(128)(2,1)S(1)} %dynamic-update-slice.1), channel_id=1, replica_groups=mesh['batch'=8,'replica'=32] {'replica'}, use_global_device_ids=true, to_apply=%add | all-reduce | flops 1024 | bytes 4096
  93.4 4.7 %convolution_convert_fusion.1 = bf16[256,3072]{1,0:T(8,128)(2,1)S(1)} fusion(bf16[1024,3072]{1,0:T(8,128)(2,1)} %all-gather.3.cloned.1.call-done, f32[1024]{0:T(1024)S(1)} %convert_element_type.85, f32[256]{0:T(256)S(1)} %rsqrt.12, f32[256]{0:T(256)S(1)} %div.47, bf16[256,1024]{1,0:T(8,128)(2,1)S(1)} %gather_fusion.1, pred[256]{0:T(512)(128)(4,1)S(1)} %compare_and_fusion.5), kind=kOutput, calls=%fused_computation.10 | convolution fusion | flops 1612972032 | bytes 8395008 | tf_op jit(solution)/shard_map/dot_general | solution.py:29
  98.1 0.9 fusion.89
  99.1 1.7 reshape.245
  100.7 1.6 reshape.246
  102.4 1.8 reshape.244
  104.1 4.4 %fusion.91 = (f32[8,16,32]{2,1,0:T(8,128)S(1)}, f32[8,16,32,32]{2,3,1,0:T(8,128)}) fusion(pred[8,32]{1,0:T(8,128)(4,1)S(1)} %iota_compare_fusion.4, bf16[8,32,16,64]{3,2,1,0:T(8,128)(2,1)} %reshape.246, bf16[8,32,16,64]{3,2,1,0:T(8,128)(2,1)} %reshape.245), kind=kOutput, calls=%fused_computation.141 | convolution fusion | flops 17301536 | bytes 1589504 | tf_op jit(solution)/shard_map/sub | solution.py:36
  108.5 2.3 fusion.18
  111.2 1.5 reshape.247
  112.7 3.1 convolution_convert_fusion.2
  115.9 1.3 all-gather.5.cloned.1.call-done
  117.2 3.1 convolution_convert_fusion.5
  120.4 2.5 reshape.251
  122.8 3.3 fusion.47
  126.1 5.7 %fusion.20 = bf16[8,32,16,64]{3,1,2,0:T(8,128)(2,1)} fusion(f32[8,16,32,32]{2,3,1,0:T(8,128)} %fusion.47, bf16[8,32,16,64]{3,2,1,0:T(8,128)(2,1)} %reshape.245, f32[8,16,32,32]{2,3,1,0:T(8,128)} %get-tuple-element.42, f32[8,16,32]{2,1,0:T(8,128)S(1)} %get-tuple-element.41), kind=kOutput, calls=%fused_computation.26 | convolution fusion | flops 17960992 | bytes 2113536 | tf_op jit(solution)/shard_map/ghqk,gqhd->gkhd/dot_general | solution.py:60
  131.8 1.6 copy.62
  133.5 1.5 reshape.253
  135.0 6.0 %fusion.23 = bf16[8,32,16,64]{3,1,2,0:T(8,128)(2,1)} fusion(f32[8,16,32,32]{2,3,1,0:T(8,128)} %fusion.47, bf16[8,32,16,64]{3,2,1,0:T(8,128)(2,1)} %reshape.246, f32[8,16,32,32]{2,3,1,0:T(8,128)} %get-tuple-element.42, f32[8,16,32]{2,1,0:T(8,128)S(1)} %get-tuple-element.41), kind=kOutput, calls=%fused_computation.27 | convolution fusion | flops 17960992 | bytes 2113536 | tf_op jit(solution)/shard_map/ghqk,gkhd->gqhd/dot_general | solution.py:57
  141.0 1.6 copy.60
  142.6 1.5 reshape.252
  144.2 2.4 fusion.19
  147.0 1.5 reshape.254
  148.5 1.1 constant_dynamic-update-slice_fusion.2
  149.6 1.1 constant_dynamic-update-slice_fusion.1
  150.8 1.1 copy-done.3
  151.9 4.7 %convolution_convert_fusion = bf16[1024,3072]{1,0:T(8,128)(2,1)} fusion(bf16[256,3072]{1,0:T(8,128)(2,1)S(1)} %constant_dynamic-update-slice_fusion, f32[1024]{0:T(1024)S(1)} %convert_element_type.85, f32[256]{0:T(256)S(1)} %rsqrt.12, f32[256]{0:T(256)S(1)} %div.47, bf16[256,1024]{1,0:T(8,128)(2,1)S(1)} %gather_fusion.1, pred[256]{0:T(512)(128)(4,1)S(1)} %compare_and_fusion.5), kind=kOutput, calls=%fused_computation.9 | convolution fusion | flops 1615331328 | bytes 8395008 | tf_op jit(solution)/shard_map/dot_general | solution.py:91
  156.8 0.9 copy-done.5
  157.7 2.3 fusion.26
  160.6 5.4 %fusion.38 = (bf16[1024]{0:T(1024)(128)(2,1)S(1)}, f32[256]{0:T(256)S(1)}, f32[256]{0:T(256)S(1)}, f32[256,1024]{1,0:T(8,128)S(1)}) fusion(f32[256]{0:T(256)S(1)} %rsqrt.12, f32[256]{0:T(256)S(1)} %div.47, bf16[256,1024]{1,0:T(8,128)(2,1)S(1)} %gather_fusion.1, pred[256]{0:T(512)(128)(4,1)S(1)} %compare_and_fusion.5, f32[1024]{0:T(1024)S(1)} %convert_element_type.85, ...), kind=kOutput, calls=%fused_computation.45 | convolution fusion | flops 1613232640 | bytes 9447680 | tf_op jit(solution)/shard_map/dot_general | solution.py:67
  167.0 1.0 broadcast_select_fusion.1
  168.0 24.7 %all_to_all.15 = bf16[8,32,1024]{2,1,0:T(8,128)(2,1)S(1)} all-to-all(bf16[8,32,1024]{2,1,0:T(8,128)(2,1)S(1)} %get-tuple-element.39), channel_id=1, replica_groups=mesh['batch'=8,'replica'=32] {'batch'}, dimensions={0} | all-to-all | bytes 1048576 | tf_op jit(solution)/shard_map/all_to_all | solution.py:143
  192.7 3.5 all-to-all-start
  196.4 10.7 %reduce-scatter.5.cloned.1.call-done = bf16[32,1024]{1,0:T(8,128)(2,1)} async-done(((bf16[1024,1024]{1,0:T(8,128)(2,1)}), bf16[32,1024]{1,0:T(8,128)(2,1)}) %reduce-scatter.5.cloned.1.call-update) | async-done | bytes 65552 | tf_op jit(solution)/shard_map/reduce_scatter | solution.py:156
  207.1 97.2 %reduce-scatter.3.cloned.1.call-done = bf16[32,3072]{1,0:T(8,128)(2,1)} async-done(((bf16[1024,3072]{1,0:T(8,128)(2,1)}), bf16[32,3072]{1,0:T(8,128)(2,1)}) %reduce-scatter.3.cloned.1.call-update) | async-done | bytes 196624 | tf_op jit(solution)/shard_map/reduce_scatter | solution.py:149
  304.9 58.4 %all-reduce.1 = bf16[1024]{0:T(1024)(128)(2,1)S(1)} all-reduce(bf16[1024]{0:T(1024)(128)(2,1)S(1)} %get-tuple-element.19), channel_id=4, replica_groups=mesh['batch'=8,'replica'=32] {'replica'}, use_global_device_ids=true, to_apply=%region_17.21.clone | all-reduce | flops 1024 | bytes 4096
  363.4 17.5 %psum.23 = bf16[32]{0:T(256)(128)(2,1)S(1)} all-reduce(bf16[32]{0:T(256)(128)(2,1)S(1)} %dynamic-slice.9), channel_id=1, replica_groups=mesh['batch'=8,'replica'=32] {'batch'}, use_global_device_ids=true, to_apply=%region_18.22 | all-reduce | flops 32 | bytes 128 | tf_op jit(solution)/shard_map/psum | solution.py:169
  381.4 0.9 gather_fusion.6
  382.2 0.9 gather_fusion.3
  383.1 0.9 select_bitcast_fusion
  384.0 1.5 convert_element_type.105
  385.5 1.7 convert_element_type.103
  (78 shorter events, 8.0 us)
Async XLA Ops:
  7.2 17.4 %copy-start = (bf16[1,8,64,1024]{3,2,1,0:T(8,128)(2,1)S(1)}, bf16[1,8,64,1024]{3,2,1,0:T(8,128)(2,1)}, u32[]{:S(2)}) copy-start(bf16[1,8,64,1024]{3,2,1,0:T(8,128)(2,1)} %param.14) | copy-start | bytes 3145732
  7.2 86.2 %all-gather.3.cloned.1.call-start = ((), (), s32[]{:S(2)}) async-start(), calls=%async_computation.5 | async-start | bytes 6488064 | tf_op jit(solution)/shard_map/all_gather | solution.py:100
  14.1 10.3 %copy-start.6 = (s32[1,8,64]{2,1,0:T(8,128)S(1)}, s32[1,8,64]{2,1,0:T(8,128)}, u32[]{:S(2)}) copy-start(s32[1,8,64]{2,1,0:T(8,128)} %param.15) | copy-start | bytes 6148
  15.2 77.5 %all-to-all-start.1 = ((bf16[8,32,1024]{2,1,0:T(8,128)(2,1)}), bf16[8,32,1024]{2,1,0:T(8,128)(2,1)S(1)}, u32[]{:S(2)}, u32[]{:S(2)}) async-start(bf16[8,32,1024]{2,1,0:T(8,128)(2,1)} %select_select_fusion), calls=%async_computation.1 | async-start | bytes 1048576 | tf_op jit(solution)/shard_map/all_to_all | solution.py:132
  23.6 93.6 %all-gather.5.cloned.1.call-start = ((), (), s32[]{:S(2)}) async-start(), calls=%async_computation.6 | async-start | bytes 2162688 | tf_op jit(solution)/shard_map/all_gather | solution.py:101
  24.4 182.7 %reduce-scatter.5.cloned.1.call-start = ((), (), s32[]{:S(2)}) async-start(), calls=%async_computation.8 | async-start | bytes 2162688 | tf_op jit(solution)/shard_map/reduce_scatter | solution.py:156
  24.5 3.6 copy-start.7
  24.5 4.8 %copy-start.8 = (bf16[32]{0:T(256)(128)(2,1)S(1)}, bf16[32]{0:T(256)(128)(2,1)}, u32[]{:S(2)}) copy-start(bf16[32]{0:T(256)(128)(2,1)} %param.20) | copy-start | bytes 196
  104.1 4.4 %copy-start.1 = (bf16[8,32,16,64]{3,2,1,0:T(8,128)(2,1)}, bf16[8,32,16,64]{3,2,1,0:T(8,128)(2,1)S(1)}, u32[]{:S(2)}) copy-start(bf16[8,32,16,64]{3,2,1,0:T(8,128)(2,1)S(1)} %reshape.244) | copy-start | bytes 1572868
  115.9 7.0 %copy-start.2 = (bf16[8,32,16,64]{3,2,1,0:T(8,128)(2,1)S(1)}, bf16[8,32,16,64]{3,2,1,0:T(8,128)(2,1)}, u32[]{:S(2)}) copy-start(bf16[8,32,16,64]{3,2,1,0:T(8,128)(2,1)} %copy-done.1) | copy-start | bytes 1572868
  115.9 188.3 %reduce-scatter.3.cloned.1.call-start = ((), (), s32[]{:S(2)}) async-start(), calls=%async_computation.7 | async-start | bytes 6488064 | tf_op jit(solution)/shard_map/reduce_scatter | solution.py:149
  148.5 2.2 copy-start.4
  150.8 1.2 copy-start.3
  156.6 1.0 copy-start.5
  192.7 189.5 %all-to-all-start = ((bf16[8,32,1024]{2,1,0:T(8,128)(2,1)}), bf16[8,32,1024]{2,1,0:T(8,128)(2,1)S(1)}, u32[]{:S(2)}, u32[]{:S(2)}) async-start(bf16[8,32,1024]{2,1,0:T(8,128)(2,1)} %get-tuple-element.40), calls=%async_computation | async-start | bytes 1048576 | tf_op jit(solution)/shard_map/all_to_all | solution.py:140
  196.2 187.8 %all-reduce.5.cloned.1.call-start = ((), (), s32[]{:S(2)}) async-start(), calls=%async_computation.9 | async-start | bytes 524288 | tf_op jit(solution)/shard_map/psum | solution.py:167
Sparse Core Ops, SparseCore 0:
  10.5 56.0 all-gather.2
  69.1 48.0 all-gather.4
  121.1 85.9 reduce-scatter.4
  211.0 93.2 reduce-scatter.2
  306.5 72.7 all-reduce.4
where the time goes:
time: 398 us; the launch traced here: 394 us
  blocking collectives  163 us (41%)
  waiting for transfers between devices  111 us (28%)
  matrix products  47.4 us (12%)
  local copies, waits for them, and re-layouts  33.7 us (8%)
  between operations  15.4 us (4%)
  starting transfers between devices  12.2 us (3%)
  other arithmetic  11.1 us (3%)
    unnamed x2, blocking collectives  121 us
    reduce_scatter x1, waiting for transfers between devices, on_device(): lax.psum_scatter(left_product(layernorm_output, d_qkv).astype(jnp.bfloat1...  97.2 us
    all_to_all x1, blocking collectives, on_device(): lax.all_to_all(jnp.take(d_tokens, to_target, axis=0), 'batch', split_axis...  24.7 us
    psum x1, blocking collectives, on_device(): lax.psum(grad_g.astype(jnp.bfloat16), 'batch').astype(jnp.float32)  17.5 us
    reduce_scatter x1, waiting for transfers between devices, on_device(): lax.psum_scatter(left_product(context, up_rows).astype(jnp.bfloat16), 're...  10.7 us
    all_to_all x1, starting transfers between devices, on_device(): lax.all_to_all(backward_rows, 'batch', split_axis=0, concat_axis=0, tiled...  8.47 us
  transfers between devices with their start and end apart: 7, of which 3 were waited for; matrix products, arithmetic and copies ran while one was open for 22% of the time, Pallas kernels for 0%

commit v1 on v0

--- a/solution.py
+++ b/solution.py
@@ -96,11 +96,15 @@
 def on_device(
     patches, visible_order, visible_counts, dest_rows, qkv_weight, out_weight, norm_gain, upstream
 ):
-    wqkv, wout, gain = (
-        lax.all_gather(qkv_weight, "replica", axis=0, tiled=True),
-        lax.all_gather(out_weight, "replica", axis=0, tiled=True),
-        lax.all_gather(norm_gain, "replica", axis=0, tiled=True),
+    qkv_cols = qkv_weight.shape[1]
+    out_cols = out_weight.shape[1]
+    gain_block = jnp.broadcast_to(norm_gain[:, None], (norm_gain.shape[0], 128))
+    gathered = lax.all_gather(
+        jnp.concatenate([qkv_weight, out_weight, gain_block], axis=1), "replica", axis=0, tiled=True
     )
+    wqkv = gathered[:, :qkv_cols]
+    wout = gathered[:, qkv_cols : qkv_cols + out_cols]
+    gain = gathered[:, qkv_cols + out_cols]
     batches = lax.axis_size("batch")
     me_index = lax.axis_index("batch")
     cap = MEANVIS * batches
@@ -136,38 +140,30 @@
     result, d_tokens, layernorm_output, context, d_qkv, up_rows, gain_products = layer_core(
         local_rows, upward, allowed, wqkv, wout, gain
     )
-    came_out, came_grad = (
-        lax.all_to_all(
-            jnp.take(result, to_target, axis=0), "batch", split_axis=0, concat_axis=0, tiled=True
-        ),
-        lax.all_to_all(
-            jnp.take(d_tokens, to_target, axis=0), "batch", split_axis=0, concat_axis=0, tiled=True
-        ),
+    came = lax.all_to_all(
+        jnp.take(jnp.concatenate([result, d_tokens], axis=-1), to_target, axis=0),
+        "batch",
+        split_axis=0,
+        concat_axis=0,
+        tiled=True,
     )
+    came_out = came[..., :width]
+    came_grad = came[..., width:]
     layer_out = jnp.take(came_out.reshape(batches * MAXVIS, width), flat_rows, axis=0)
     d_packed = jnp.take(came_grad.reshape(batches * MAXVIS, width), flat_rows, axis=0)
-    grad_q = lax.psum_scatter(
-        left_product(layernorm_output, d_qkv).astype(jnp.bfloat16),
-        "replica",
-        scatter_dimension=0,
-        tiled=True,
-    ).astype(jnp.float32)
-    grad_o, grad_g = (
-        lax.psum_scatter(
+    partial = jnp.concatenate(
+        [
+            left_product(layernorm_output, d_qkv).astype(jnp.bfloat16),
             left_product(context, up_rows).astype(jnp.bfloat16),
-            "replica",
-            scatter_dimension=0,
-            tiled=True,
-        ).astype(jnp.float32),
-        lax.psum_scatter(
-            gain_products.astype(jnp.bfloat16), "replica", scatter_dimension=0, tiled=True
-        ).astype(jnp.float32),
+            jnp.broadcast_to(gain_products.astype(jnp.bfloat16)[:, None], (width, 128)),
+        ],
+        axis=1,
     )
-    grad_q, grad_o, grad_g = (
-        lax.psum(grad_q.astype(jnp.bfloat16), "batch").astype(jnp.float32),
-        lax.psum(grad_o.astype(jnp.bfloat16), "batch").astype(jnp.float32),
-        lax.psum(grad_g.astype(jnp.bfloat16), "batch").astype(jnp.float32),
-    )
+    summed = lax.psum_scatter(partial, "replica", scatter_dimension=0, tiled=True)
+    summed = lax.psum(summed, "batch").astype(jnp.float32)
+    grad_q = summed[:, :qkv_cols]
+    grad_o = summed[:, qkv_cols : qkv_cols + out_cols]
+    grad_g = summed[:, qkv_cols + out_cols]
     return (layer_out[None], d_packed[None], grad_q, grad_o, grad_g)
 
 

time: 398 us -> 336 us (0.84)
  blocking collectives: 163 us -> 0 us
  waiting for transfers between devices: 111 us -> 203 us
  local copies, waits for them, and re-layouts: 33.7 us -> 41.1 us
  other arithmetic: 11.1 us -> 17.3 us
    unnamed x2 -> x0, blocking collectives: 121 us -> none
    psum x1, waiting for transfers between devices: 0.01 us -> 72.4 us  [on_device(): summed = lax.psum(summed, 'batch').astype(jnp.float32)]
    all_gather x2 -> x1, waiting for transfers between devices: 1.3 us -> 29.1 us  [on_device(): lax.all_gather(jnp.concatenate([qkv_weight, out_weight, gain_block], axis...]
    all_to_all x1 -> x0, blocking collectives: 24.7 us -> none  [on_device(): lax.all_to_all(jnp.take(d_tokens, to_target, axis=0), 'batch', split_axis...]
    reduce_scatter x2 -> x1, waiting for transfers between devices: 108 us -> 87.6 us  [on_device(): lax.psum_scatter(partial, 'replica', scatter_dimension=0, tiled=True)]
    psum x1 -> x0, blocking collectives: 17.5 us -> none  [on_device(): lax.psum(grad_g.astype(jnp.bfloat16), 'batch').astype(jnp.float32)]
    all_to_all x1, waiting for transfers between devices: 0.01 us -> 13.4 us  [on_device(): lax.all_to_all(backward_rows, 'batch', split_axis=0, concat_axis=0, tiled...]
    concatenate x0 -> x3, other arithmetic: none -> 5.48 us  [the longest x1 3.71 us: on_device(): jnp.concatenate([left_product(layernorm_output, d_qkv).astype(jnp.bfloat1...]
  transfers between devices with their start and end apart: 7 -> 5, of which waited for: 3 -> 4; matrix products, arithmetic and copies ran while one was open for 22% -> 6% of each run, Pallas kernels for 0% -> 0%
where the time goes in v1:
time: 336 us; the launch traced here: 335 us
  waiting for transfers between devices  203 us (60%)
  matrix products  44 us (13%)
  local copies, waits for them, and re-layouts  41.1 us (12%)
  other arithmetic  17.3 us (5%)
  starting transfers between devices  15.6 us (5%)
  between operations  14.1 us (4%)
    reduce_scatter x1, waiting for transfers between devices, on_device(): lax.psum_scatter(partial, 'replica', scatter_dimension=0, tiled=True)  87.6 us
    psum x1, waiting for transfers between devices, on_device(): summed = lax.psum(summed, 'batch').astype(jnp.float32)  72.4 us
    all_gather x1, waiting for transfers between devices, on_device(): lax.all_gather(jnp.concatenate([qkv_weight, out_weight, gain_block], axis...  29.1 us
    all_to_all x1, waiting for transfers between devices, on_device(): lax.all_to_all(backward_rows, 'batch', split_axis=0, concat_axis=0, tiled...  13.4 us
    all_to_all x1, starting transfers between devices, on_device(): lax.all_to_all(backward_rows, 'batch', split_axis=0, concat_axis=0, tiled...  8.47 us
    all_to_all x1, starting transfers between devices, on_device(): lax.all_to_all(jnp.take(jnp.concatenate([result, d_tokens], axis=-1), to_...  7.02 us
  transfers between devices with their start and end apart: 5, of which 4 were waited for; matrix products, arithmetic and copies ran while one was open for 6% of the time, Pallas kernels for 0%

profile of v1, /device:TPU:2, one launch (start us, length us, event | category | flops | bytes accessed | tf_op | source)
XLA Modules:
  0.0 334.6 jit_solution(9900112664250814567)
XLA Ops:
  8.1 1.7 pad_maximum_fusion.2
  10.3 1.3 reduce.13
  11.7 1.3 reduce.12
  13.5 1.2 gather_fusion
  14.7 1.0 select_select_fusion
  15.7 8.5 %all-to-all-start = ((bf16[8,32,1024]{2,1,0:T(8,128)(2,1)}), bf16[8,32,1024]{2,1,0:T(8,128)(2,1)S(1)}, u32[]{:S(2)}, u32[]{:S(2)}) async-start(bf16[8,32,1024]{2,1,0:T(8,128)(2,1)} %select_select_fusion), calls=%async_computation | async-start | bytes 1048576 | tf_op jit(solution)/shard_map/all_to_all | solution.py:136
  24.3 2.8 gather_fusion.3
  28.2 13.4 %all-to-all-done = bf16[8,32,1024]{2,1,0:T(8,128)(2,1)S(1)} async-done(((bf16[8,32,1024]{2,1,0:T(8,128)(2,1)}), bf16[8,32,1024]{2,1,0:T(8,128)(2,1)S(1)}, u32[]{:S(2)}, u32[]{:S(2)}) %all-to-all-start) | async-done | bytes 524320 | tf_op jit(solution)/shard_map/all_to_all | solution.py:136
  42.2 0.9 broadcast_select_fusion.1
  43.3 29.1 %all-gather.2.cloned.1.call-done = bf16[1024,4224]{1,0:T(8,128)(2,1)} async-done(((bf16[32,4224]{1,0:T(8,128)(2,1)}), bf16[1024,4224]{1,0:T(8,128)(2,1)}) %all-gather.2.cloned.1.call-update) | async-done | bytes 8650768 | tf_op jit(solution)/shard_map/all_gather | solution.py:102
  72.4 3.2 fusion.43
  75.6 1.8 reshape.307
  77.3 1.1 convert_reduce_fusion.1
  78.4 4.7 %fusion.6 = bf16[256,3072]{1,0:T(8,128)(2,1)S(1)} fusion(bf16[1024,4224]{1,0:T(8,128)(2,1)} %all-gather.2.cloned.1.call-done, f32[1024]{0:T(1024)S(1)} %convert_reduce_fusion.1, f32[256]{0:T(256)S(1)} %rsqrt.12, f32[256]{0:T(256)S(1)} %div.51, bf16[256,1024]{1,0:T(8,128)(2,1)S(1)} %gather_fusion.3, pred[256]{0:T(512)(128)(4,1)S(1)} %compare_and_fusion.4), kind=kOutput, calls=%fused_computation.14 | convolution fusion | flops 1612972032 | bytes 8395008 | tf_op jit(solution)/shard_map/dot_general | solution.py:29
  83.2 1.2 fusion.109
  84.4 2.5 reshape.302
  86.9 2.5 reshape.304
  89.4 2.5 reshape.303
  91.9 3.2 fusion.66
  95.1 4.1 %fusion.111 = (f32[8,16,32]{2,1,0:T(8,128)S(1)}, f32[8,16,32,32]{2,3,1,0:T(8,128)}) fusion(pred[8,32]{1,0:T(8,128)(4,1)S(1)} %iota_compare_fusion.3, bf16[8,32,16,64]{3,2,1,0:T(8,128)(2,1)} %reshape.304, bf16[8,32,16,64]{3,2,1,0:T(8,128)(2,1)} %reshape.303), kind=kOutput, calls=%fused_computation.155 | convolution fusion | flops 17301536 | bytes 1589504 | tf_op jit(solution)/shard_map/sub | solution.py:36
  99.2 5.8 %fusion.34 = bf16[8,32,16,64]{3,1,2,0:T(8,128)(2,1)} fusion(f32[8,16,32,32]{2,3,1,0:T(8,128)} %fusion.66, bf16[8,32,16,64]{3,2,1,0:T(8,128)(2,1)} %reshape.304, f32[8,16,32,32]{2,3,1,0:T(8,128)} %get-tuple-element.37, f32[8,16,32]{2,1,0:T(8,128)S(1)} %get-tuple-element.36), kind=kOutput, calls=%fused_computation.35 | convolution fusion | flops 17960992 | bytes 2113536 | tf_op jit(solution)/shard_map/ghqk,gkhd->gqhd/dot_general | solution.py:57
  104.9 5.6 %fusion.31 = bf16[8,32,16,64]{3,1,2,0:T(8,128)(2,1)} fusion(f32[8,16,32,32]{2,3,1,0:T(8,128)} %fusion.66, bf16[8,32,16,64]{3,2,1,0:T(8,128)(2,1)} %reshape.303, f32[8,16,32,32]{2,3,1,0:T(8,128)} %get-tuple-element.37, f32[8,16,32]{2,1,0:T(8,128)S(1)} %get-tuple-element.36), kind=kOutput, calls=%fused_computation.34 | convolution fusion | flops 17960992 | bytes 2113536 | tf_op jit(solution)/shard_map/ghqk,gqhd->gkhd/dot_general | solution.py:60
  110.6 3.2 fusion.30
  113.8 1.6 fusion.29
  115.8 1.5 reshape.308
  117.3 1.9 constant_dynamic-update-slice_fusion.2
  119.2 1.6 copy.50
  120.9 1.5 reshape.309
  122.4 1.6 copy.52
  124.1 1.5 reshape.310
  125.6 1.6 copy.43
  127.2 1.5 reshape.305
  128.7 1.9 constant_dynamic-update-slice_fusion.1
  130.7 1.9 constant_dynamic-update-slice_fusion
  132.6 3.5 %convolution_convert_fusion = bf16[1024,3072]{1,0:T(8,128)(2,1)S(1)} fusion(bf16[256,3072]{1,0:T(8,128)(2,1)} %constant_dynamic-update-slice_fusion, f32[1024]{0:T(1024)S(1)} %convert_reduce_fusion.1, f32[256]{0:T(256)S(1)} %rsqrt.12, f32[256]{0:T(256)S(1)} %div.51, bf16[256,1024]{1,0:T(8,128)(2,1)S(1)} %gather_fusion.3, pred[256]{0:T(512)(128)(4,1)S(1)} %compare_and_fusion.4), kind=kOutput, calls=%fused_computation.9 | convolution fusion | flops 1615331328 | bytes 8395008 | tf_op jit(solution)/shard_map/dot_general | solution.py:91
  136.1 1.0 convolution_convert_fusion.1
  137.5 5.8 %fusion.57 = (bf16[1024]{0:T(1024)(128)(2,1)S(1)}, f32[256]{0:T(256)S(1)}, f32[256]{0:T(256)S(1)}, f32[256,1024]{1,0:T(8,128)}) fusion(f32[256]{0:T(256)S(1)} %rsqrt.12, f32[256]{0:T(256)S(1)} %div.51, bf16[256,1024]{1,0:T(8,128)(2,1)S(1)} %gather_fusion.3, pred[256]{0:T(512)(128)(4,1)S(1)} %compare_and_fusion.4, f32[1024]{0:T(1024)S(1)} %convert_reduce_fusion.1, ...), kind=kOutput, calls=%fused_computation.53 | convolution fusion | flops 1613232640 | bytes 9447680 | tf_op jit(solution)/shard_map/dot_general | solution.py:67
  143.5 3.7 %pad_maximum_fusion = bf16[1024,4224]{1,0:T(8,128)(2,1)} fusion(bf16[1024,128]{1,0:T(8,128)(2,1)S(1)} %broadcast_in_dim.181, bf16[1024,1024]{1,0:T(8,128)(2,1)S(1)} %convolution_convert_fusion.1, bf16[1024,3072]{1,0:T(8,128)(2,1)S(1)} %convolution_convert_fusion), kind=kLoop, calls=%fused_computation.8 | loop fusion | flops 25952256 | bytes 17301504 | tf_op jit(solution)/shard_map/concatenate | solution.py:154
  147.5 1.7 fusion.56
  149.2 2.3 fusion.40
  152.3 1.2 broadcast_select_fusion
  153.4 7.0 %all-to-all-start.1 = ((bf16[8,32,2048]{2,1,0:T(8,128)(2,1)}), bf16[8,32,2048]{2,1,0:T(8,128)(2,1)S(1)}, u32[]{:S(2)}, u32[]{:S(2)}) async-start(bf16[8,32,2048]{2,1,0:T(8,128)(2,1)} %broadcast_select_fusion), calls=%async_computation.1 | async-start | bytes 2097152 | tf_op jit(solution)/shard_map/all_to_all | solution.py:143
  160.5 87.6 %reduce-scatter.2.cloned.1.call-done = bf16[32,4224]{1,0:T(8,128)(2,1)} async-done(((bf16[1024,4224]{1,0:T(8,128)(2,1)}), bf16[32,4224]{1,0:T(8,128)(2,1)}) %reduce-scatter.2.cloned.1.call-update) | async-done | bytes 270352 | tf_op jit(solution)/shard_map/reduce_scatter | solution.py:162
  249.9 0.9 select_bitcast_fusion
  250.8 72.4 %all-reduce.2.cloned.1.call-done = bf16[32,4224]{1,0:T(8,128)(2,1)} async-done(((bf16[32,4224]{1,0:T(8,128)(2,1)}), bf16[32,4224]{1,0:T(8,128)(2,1)}) %all-reduce.2.cloned.1.call-update) | async-done | bytes 270352 | tf_op jit(solution)/shard_map/psum | solution.py:163
  323.3 1.0 convert_element_type.105
  324.9 1.7 slice.75
  326.6 1.5 slice.76
  (72 shorter events, 8.4 us)
Async XLA Ops:
  7.2 17.1 %copy-start = (bf16[1,8,64,1024]{3,2,1,0:T(8,128)(2,1)S(1)}, bf16[1,8,64,1024]{3,2,1,0:T(8,128)(2,1)}, u32[]{:S(2)}) copy-start(bf16[1,8,64,1024]{3,2,1,0:T(8,128)(2,1)} %param.12) | copy-start | bytes 3145732
  7.2 6.3 %copy-start.1 = (bf16[1,128,1024]{2,1,0:T(8,128)(2,1)S(1)}, bf16[1,128,1024]{2,1,0:T(8,128)(2,1)}, u32[]{:S(2)}) copy-start(bf16[1,128,1024]{2,1,0:T(8,128)(2,1)} %param.19) | copy-start | bytes 786436
  7.2 65.2 %all-gather.2.cloned.1.call-start = ((), (), s32[]{:S(2)}) async-start(), calls=%async_computation.3 | async-start | bytes 8921088 | tf_op jit(solution)/shard_map/all_gather | solution.py:102
  14.6 9.6 %copy-start.7 = (s32[1,8,64]{2,1,0:T(8,128)S(1)}, s32[1,8,64]{2,1,0:T(8,128)}, u32[]{:S(2)}) copy-start(s32[1,8,64]{2,1,0:T(8,128)} %param.13) | copy-start | bytes 6148
  15.7 26.0 %all-to-all-start = ((bf16[8,32,1024]{2,1,0:T(8,128)(2,1)}), bf16[8,32,1024]{2,1,0:T(8,128)(2,1)S(1)}, u32[]{:S(2)}, u32[]{:S(2)}) async-start(bf16[8,32,1024]{2,1,0:T(8,128)(2,1)} %select_select_fusion), calls=%async_computation | async-start | bytes 1048576 | tf_op jit(solution)/shard_map/all_to_all | solution.py:136
  24.2 223.9 %reduce-scatter.2.cloned.1.call-start = ((), (), s32[]{:S(2)}) async-start(), calls=%async_computation.4 | async-start | bytes 8921088 | tf_op jit(solution)/shard_map/reduce_scatter | solution.py:162
  110.6 3.2 copy-start.2
  110.6 3.2 copy-start.8
  113.8 1.6 copy-start.6
  132.6 3.6 %copy-start.4 = (bf16[256,1024]{1,0:T(8,128)(2,1)S(1)}, bf16[256,1024]{1,0:T(8,128)(2,1)}, u32[]{:S(2)}) copy-start(bf16[256,1024]{1,0:T(8,128)(2,1)} %reshape.305) | copy-start | bytes 1572868
  132.6 3.6 %copy-start.5 = (bf16[8,32,1024]{2,1,0:T(8,128)(2,1)S(1)}, bf16[8,32,1024]{2,1,0:T(8,128)(2,1)}, u32[]{:S(2)}) copy-start(bf16[8,32,1024]{2,1,0:T(8,128)(2,1)} %broadcast_select_fusion.1) | copy-start | bytes 1572868
  136.1 1.4 copy-start.3
  153.4 94.7 %all-to-all-start.1 = ((bf16[8,32,2048]{2,1,0:T(8,128)(2,1)}), bf16[8,32,2048]{2,1,0:T(8,128)(2,1)S(1)}, u32[]{:S(2)}, u32[]{:S(2)}) async-start(bf16[8,32,2048]{2,1,0:T(8,128)(2,1)} %broadcast_select_fusion), calls=%async_computation.1 | async-start | bytes 2097152 | tf_op jit(solution)/shard_map/all_to_all | solution.py:143
  160.4 162.8 %all-reduce.2.cloned.1.call-start = ((), (), s32[]{:S(2)}) async-start(), calls=%async_computation.5 | async-start | bytes 540672 | tf_op jit(solution)/shard_map/psum | solution.py:163
Sparse Core Ops, SparseCore 0:
  11.1 61.2 all-gather.1
  147.3 100.6 reduce-scatter.1
  250.4 72.8 all-reduce.1

commit v2 on v1

--- a/solution.py
+++ b/solution.py
@@ -160,7 +160,18 @@
         axis=1,
     )
     summed = lax.psum_scatter(partial, "replica", scatter_dimension=0, tiled=True)
-    summed = lax.psum(summed, "batch").astype(jnp.float32)
+    pieces = lax.all_to_all(
+        summed.reshape(batches, -1, summed.shape[1]), "batch", split_axis=0, concat_axis=0, tiled=True
+    )
+    reduced = jnp.sum(pieces.astype(jnp.float32), axis=0).astype(jnp.bfloat16)
+    summed = lax.all_to_all(
+        jnp.broadcast_to(reduced[None], (batches,) + reduced.shape),
+        "batch",
+        split_axis=0,
+        concat_axis=0,
+        tiled=True,
+    )
+    summed = summed.reshape(-1, summed.shape[2]).astype(jnp.float32)
     grad_q = summed[:, :qkv_cols]
     grad_o = summed[:, qkv_cols : qkv_cols + out_cols]
     grad_g = summed[:, qkv_cols + out_cols]

time: 336 us -> 321 us (0.955)
  waiting for transfers between devices: 203 us -> 181 us
  starting transfers between devices: 15.6 us -> 22.5 us
    psum x1 -> x0, waiting for transfers between devices: 72.4 us -> none  [on_device(): summed = lax.psum(summed, 'batch').astype(jnp.float32)]
    all_to_all x1, waiting for transfers between devices: 0.01 us -> 25.4 us  [on_device(): lax.all_to_all(jnp.take(jnp.concatenate([result, d_tokens], axis=-1), to_...]
    all_to_all x0 -> x2, waiting for transfers between devices: none -> 17.2 us  [the longest x1 9.42 us: on_device(): lax.all_to_all(summed.reshape(batches, -1, summed.shape[1]), 'batch', spl...]
    all_to_all x0 -> x2, starting transfers between devices: none -> 10.4 us  [the longest x1 7 us: on_device(): lax.all_to_all(summed.reshape(batches, -1, summed.shape[1]), 'batch', spl...]
    reduce_scatter x1, waiting for transfers between devices: 87.6 us -> 95.8 us  [on_device(): lax.psum_scatter(partial, 'replica', scatter_dimension=0, tiled=True)]
    all_to_all x1, starting transfers between devices: 7.02 us -> 3.56 us  [on_device(): lax.all_to_all(jnp.take(jnp.concatenate([result, d_tokens], axis=-1), to_...]
  transfers between devices with their start and end apart: 5 -> 6, of which waited for: 4 -> 6; matrix products, arithmetic and copies ran while one was open for 6% -> 6% of each run, Pallas kernels for 0% -> 0%
where the time goes in v2:
time: 321 us; the launch traced here: 320 us
  waiting for transfers between devices  181 us (56%)
  matrix products  44 us (14%)
  local copies, waits for them, and re-layouts  41.8 us (13%)
  starting transfers between devices  22.5 us (7%)
  other arithmetic  16.4 us (5%)
  between operations  14.4 us (4%)
    reduce_scatter x1, waiting for transfers between devices, on_device(): lax.psum_scatter(partial, 'replica', scatter_dimension=0, tiled=True)  95.8 us
    all_gather x1, waiting for transfers between devices, on_device(): lax.all_gather(jnp.concatenate([qkv_weight, out_weight, gain_block], axis...  29.1 us
    all_to_all x1, waiting for transfers between devices, on_device(): lax.all_to_all(jnp.take(jnp.concatenate([result, d_tokens], axis=-1), to_...  25.4 us
    all_to_all x1, waiting for transfers between devices, on_device(): lax.all_to_all(backward_rows, 'batch', split_axis=0, concat_axis=0, tiled...  13.4 us
    all_to_all x1, waiting for transfers between devices, on_device(): lax.all_to_all(summed.reshape(batches, -1, summed.shape[1]), 'batch', spl...  9.42 us
    all_to_all x1, starting transfers between devices, on_device(): lax.all_to_all(backward_rows, 'batch', split_axis=0, concat_axis=0, tiled...  8.47 us
    all_to_all x1, waiting for transfers between devices, on_device(): lax.all_to_all(jnp.broadcast_to(reduced[None], (batches,) + reduced.shape...  7.75 us
    all_to_all x1, starting transfers between devices, on_device(): lax.all_to_all(summed.reshape(batches, -1, summed.shape[1]), 'batch', spl...  7 us
  transfers between devices with their start and end apart: 6, of which 6 were waited for; matrix products, arithmetic and copies ran while one was open for 6% of the time, Pallas kernels for 0%

profile of v2, /device:TPU:2, one launch (start us, length us, event | category | flops | bytes accessed | tf_op | source)
XLA Modules:
  0.0 320.1 jit_solution(12907240663164983671)
XLA Ops:
  8.1 1.7 pad_maximum_fusion.2
  10.3 1.3 reduce.14
  11.7 1.3 reduce.13
  13.5 1.2 gather_fusion
  14.7 1.0 select_select_fusion
  15.7 8.5 %all-to-all-start = ((bf16[8,32,1024]{2,1,0:T(8,128)(2,1)}), bf16[8,32,1024]{2,1,0:T(8,128)(2,1)S(1)}, u32[]{:S(2)}, u32[]{:S(2)}) async-start(bf16[8,32,1024]{2,1,0:T(8,128)(2,1)} %select_select_fusion), calls=%async_computation | async-start | bytes 1048576 | tf_op jit(solution)/shard_map/all_to_all | solution.py:136
  24.3 2.8 gather_fusion.3
  28.2 13.4 %all-to-all-done = bf16[8,32,1024]{2,1,0:T(8,128)(2,1)S(1)} async-done(((bf16[8,32,1024]{2,1,0:T(8,128)(2,1)}), bf16[8,32,1024]{2,1,0:T(8,128)(2,1)S(1)}, u32[]{:S(2)}, u32[]{:S(2)}) %all-to-all-start) | async-done | bytes 524320 | tf_op jit(solution)/shard_map/all_to_all | solution.py:136
  43.3 29.1 %all-gather.2.cloned.1.call-done = bf16[1024,4224]{1,0:T(8,128)(2,1)} async-done(((bf16[32,4224]{1,0:T(8,128)(2,1)}), bf16[1024,4224]{1,0:T(8,128)(2,1)}) %all-gather.2.cloned.1.call-update) | async-done | bytes 8650768 | tf_op jit(solution)/shard_map/all_gather | solution.py:102
  72.4 3.2 fusion.43
  75.6 1.8 reshape.314
  77.3 1.1 convert_reduce_fusion.1
  78.4 4.7 %fusion.6 = bf16[256,3072]{1,0:T(8,128)(2,1)S(1)} fusion(bf16[1024,4224]{1,0:T(8,128)(2,1)} %all-gather.2.cloned.1.call-done, f32[1024]{0:T(1024)S(1)} %convert_reduce_fusion.1, f32[256]{0:T(256)S(1)} %rsqrt.12, f32[256]{0:T(256)S(1)} %div.51, bf16[256,1024]{1,0:T(8,128)(2,1)S(1)} %gather_fusion.3, pred[256]{0:T(512)(128)(4,1)S(1)} %compare_and_fusion.4), kind=kOutput, calls=%fused_computation.14 | convolution fusion | flops 1612972032 | bytes 8395008 | tf_op jit(solution)/shard_map/dot_general | solution.py:29
  83.2 1.2 fusion.109
  84.4 2.5 reshape.309
  86.9 2.5 reshape.311
  89.4 2.5 reshape.310
  91.9 3.2 %fusion.66 = f32[8,16,32,32]{2,3,1,0:T(8,128)} fusion(bf16[8,32,16,64]{3,2,1,0:T(8,128)(2,1)S(1)} %reshape.314, bf16[8,32,16,64]{3,2,1,0:T(8,128)(2,1)} %reshape.309), kind=kOutput, calls=%fused_computation.65 | convolution fusion | flops 16777216 | bytes 1572864 | tf_op jit(solution)/shard_map/gqhd,gkhd->ghqk/dot_general | solution.py:53
  95.1 4.1 %fusion.111 = (f32[8,16,32]{2,1,0:T(8,128)S(1)}, f32[8,16,32,32]{2,3,1,0:T(8,128)}) fusion(pred[8,32]{1,0:T(8,128)(4,1)S(1)} %iota_compare_fusion.3, bf16[8,32,16,64]{3,2,1,0:T(8,128)(2,1)} %reshape.311, bf16[8,32,16,64]{3,2,1,0:T(8,128)(2,1)} %reshape.310), kind=kOutput, calls=%fused_computation.155 | convolution fusion | flops 17301536 | bytes 1589504 | tf_op jit(solution)/shard_map/sub | solution.py:36
  99.2 5.8 %fusion.34 = bf16[8,32,16,64]{3,1,2,0:T(8,128)(2,1)} fusion(f32[8,16,32,32]{2,3,1,0:T(8,128)} %fusion.66, bf16[8,32,16,64]{3,2,1,0:T(8,128)(2,1)} %reshape.311, f32[8,16,32,32]{2,3,1,0:T(8,128)} %get-tuple-element.37, f32[8,16,32]{2,1,0:T(8,128)S(1)} %get-tuple-element.36), kind=kOutput, calls=%fused_computation.35 | convolution fusion | flops 17960992 | bytes 2113536 | tf_op jit(solution)/shard_map/ghqk,gkhd->gqhd/dot_general | solution.py:57
  104.9 5.6 %fusion.31 = bf16[8,32,16,64]{3,1,2,0:T(8,128)(2,1)} fusion(f32[8,16,32,32]{2,3,1,0:T(8,128)} %fusion.66, bf16[8,32,16,64]{3,2,1,0:T(8,128)(2,1)} %reshape.310, f32[8,16,32,32]{2,3,1,0:T(8,128)} %get-tuple-element.37, f32[8,16,32]{2,1,0:T(8,128)S(1)} %get-tuple-element.36), kind=kOutput, calls=%fused_computation.34 | convolution fusion | flops 17960992 | bytes 2113536 | tf_op jit(solution)/shard_map/ghqk,gqhd->gkhd/dot_general | solution.py:60
  110.6 3.2 fusion.30
  113.8 1.6 fusion.29
  115.8 1.5 reshape.315
  117.3 1.9 constant_dynamic-update-slice_fusion.2
  119.2 1.6 copy.50
  120.9 1.5 reshape.316
  122.4 1.6 copy.52
  124.1 1.5 reshape.317
  125.6 1.6 copy.43
  127.2 1.5 reshape.312
  128.7 1.9 constant_dynamic-update-slice_fusion.1
  130.7 1.9 constant_dynamic-update-slice_fusion
  132.6 3.5 %convolution_convert_fusion = bf16[1024,3072]{1,0:T(8,128)(2,1)S(1)} fusion(bf16[256,3072]{1,0:T(8,128)(2,1)} %constant_dynamic-update-slice_fusion, f32[1024]{0:T(1024)S(1)} %convert_reduce_fusion.1, f32[256]{0:T(256)S(1)} %rsqrt.12, f32[256]{0:T(256)S(1)} %div.51, bf16[256,1024]{1,0:T(8,128)(2,1)S(1)} %gather_fusion.3, pred[256]{0:T(512)(128)(4,1)S(1)} %compare_and_fusion.4), kind=kOutput, calls=%fused_computation.9 | convolution fusion | flops 1615331328 | bytes 8395008 | tf_op jit(solution)/shard_map/dot_general | solution.py:91
  136.1 1.0 convolution_convert_fusion.1
  137.5 5.8 %fusion.57 = (bf16[1024]{0:T(1024)(128)(2,1)S(1)}, f32[256]{0:T(256)S(1)}, f32[256]{0:T(256)S(1)}, f32[256,1024]{1,0:T(8,128)}) fusion(f32[256]{0:T(256)S(1)} %rsqrt.12, f32[256]{0:T(256)S(1)} %div.51, bf16[256,1024]{1,0:T(8,128)(2,1)S(1)} %gather_fusion.3, pred[256]{0:T(512)(128)(4,1)S(1)} %compare_and_fusion.4, f32[1024]{0:T(1024)S(1)} %convert_reduce_fusion.1, ...), kind=kOutput, calls=%fused_computation.53 | convolution fusion | flops 1613232640 | bytes 9447680 | tf_op jit(solution)/shard_map/dot_general | solution.py:67
  143.5 3.7 %pad_maximum_fusion = bf16[1024,4224]{1,0:T(8,128)(2,1)} fusion(bf16[1024,128]{1,0:T(8,128)(2,1)S(1)} %broadcast_in_dim.187, bf16[1024,1024]{1,0:T(8,128)(2,1)S(1)} %convolution_convert_fusion.1, bf16[1024,3072]{1,0:T(8,128)(2,1)S(1)} %convolution_convert_fusion), kind=kLoop, calls=%fused_computation.8 | loop fusion | flops 25952256 | bytes 17301504 | tf_op jit(solution)/shard_map/concatenate | solution.py:154
  147.5 1.7 fusion.56
  149.2 2.3 fusion.40
  152.3 95.8 %reduce-scatter.2.cloned.1.call-done = bf16[32,4224]{1,0:T(8,128)(2,1)} async-done(((bf16[1024,4224]{1,0:T(8,128)(2,1)}), bf16[32,4224]{1,0:T(8,128)(2,1)}) %reduce-scatter.2.cloned.1.call-update) | async-done | bytes 270352 | tf_op jit(solution)/shard_map/reduce_scatter | solution.py:162
  248.1 1.7 reshape.321
  249.8 7.0 %all-to-all-start.2 = ((bf16[8,4,4224]{2,1,0:T(4,128)(2,1)}), bf16[8,4,4224]{2,1,0:T(4,128)(2,1)S(1)}, u32[]{:S(2)}, u32[]{:S(2)}) async-start(bf16[8,4,4224]{2,1,0:T(4,128)(2,1)} %reshape.321), calls=%async_computation.3 | async-start | bytes 540672 | tf_op jit(solution)/shard_map/all_to_all | solution.py:163
  256.8 1.2 broadcast_select_fusion
  257.9 9.4 %all-to-all-done.2 = bf16[8,4,4224]{2,1,0:T(4,128)(2,1)S(1)} async-done(((bf16[8,4,4224]{2,1,0:T(4,128)(2,1)}), bf16[8,4,4224]{2,1,0:T(4,128)(2,1)S(1)}, u32[]{:S(2)}, u32[]{:S(2)}) %all-to-all-start.2) | async-done | bytes 270368 | tf_op jit(solution)/shard_map/all_to_all | solution.py:163
  267.4 3.6 %all-to-all-start.1 = ((bf16[8,32,2048]{2,1,0:T(8,128)(2,1)}), bf16[8,32,2048]{2,1,0:T(8,128)(2,1)S(1)}, u32[]{:S(2)}, u32[]{:S(2)}) async-start(bf16[8,32,2048]{2,1,0:T(8,128)(2,1)} %broadcast_select_fusion), calls=%async_computation.1 | async-start | bytes 2097152 | tf_op jit(solution)/shard_map/all_to_all | solution.py:143
  271.1 25.4 %all-to-all-done.1 = bf16[8,32,2048]{2,1,0:T(8,128)(2,1)S(1)} async-done(((bf16[8,32,2048]{2,1,0:T(8,128)(2,1)}), bf16[8,32,2048]{2,1,0:T(8,128)(2,1)S(1)}, u32[]{:S(2)}, u32[]{:S(2)}) %all-to-all-start.1) | async-done | bytes 1048608 | tf_op jit(solution)/shard_map/all_to_all | solution.py:143
  297.2 3.4 %all-to-all-start.3 = ((bf16[8,4,4224]{2,1,0:T(4,128)(2,1)}), bf16[8,4,4224]{2,1,0:T(4,128)(2,1)S(1)}, u32[]{:S(2)}, u32[]{:S(2)}) async-start(bf16[8,4,4224]{2,1,0:T(4,128)(2,1)} %broadcast_in_dim.188), calls=%async_computation.4 | async-start | bytes 540672 | tf_op jit(solution)/shard_map/all_to_all | solution.py:167
  303.4 7.8 %all-to-all-done.3 = bf16[8,4,4224]{2,1,0:T(4,128)(2,1)S(1)} async-done(((bf16[8,4,4224]{2,1,0:T(4,128)(2,1)}), bf16[8,4,4224]{2,1,0:T(4,128)(2,1)S(1)}, u32[]{:S(2)}, u32[]{:S(2)}) %all-to-all-start.3) | async-done | bytes 270368 | tf_op jit(solution)/shard_map/all_to_all | solution.py:167
  (76 shorter events, 12.5 us)
Async XLA Ops:
  7.2 17.1 %copy-start = (bf16[1,8,64,1024]{3,2,1,0:T(8,128)(2,1)S(1)}, bf16[1,8,64,1024]{3,2,1,0:T(8,128)(2,1)}, u32[]{:S(2)}) copy-start(bf16[1,8,64,1024]{3,2,1,0:T(8,128)(2,1)} %param.12) | copy-start | bytes 3145732
  7.2 6.3 %copy-start.1 = (bf16[1,128,1024]{2,1,0:T(8,128)(2,1)S(1)}, bf16[1,128,1024]{2,1,0:T(8,128)(2,1)}, u32[]{:S(2)}) copy-start(bf16[1,128,1024]{2,1,0:T(8,128)(2,1)} %param.19) | copy-start | bytes 786436
  7.2 65.2 %all-gather.2.cloned.1.call-start = ((), (), s32[]{:S(2)}) async-start(), calls=%async_computation.5 | async-start | bytes 8921088 | tf_op jit(solution)/shard_map/all_gather | solution.py:102
  14.6 9.6 %copy-start.7 = (s32[1,8,64]{2,1,0:T(8,128)S(1)}, s32[1,8,64]{2,1,0:T(8,128)}, u32[]{:S(2)}) copy-start(s32[1,8,64]{2,1,0:T(8,128)} %param.13) | copy-start | bytes 6148
  15.7 26.0 %all-to-all-start = ((bf16[8,32,1024]{2,1,0:T(8,128)(2,1)}), bf16[8,32,1024]{2,1,0:T(8,128)(2,1)S(1)}, u32[]{:S(2)}, u32[]{:S(2)}) async-start(bf16[8,32,1024]{2,1,0:T(8,128)(2,1)} %select_select_fusion), calls=%async_computation | async-start | bytes 1048576 | tf_op jit(solution)/shard_map/all_to_all | solution.py:136
  24.2 223.9 %reduce-scatter.2.cloned.1.call-start = ((), (), s32[]{:S(2)}) async-start(), calls=%async_computation.6 | async-start | bytes 8921088 | tf_op jit(solution)/shard_map/reduce_scatter | solution.py:162
  110.6 3.2 copy-start.2
  110.6 3.2 copy-start.8
  113.8 1.6 copy-start.6
  132.6 3.6 %copy-start.4 = (bf16[256,1024]{1,0:T(8,128)(2,1)S(1)}, bf16[256,1024]{1,0:T(8,128)(2,1)}, u32[]{:S(2)}) copy-start(bf16[256,1024]{1,0:T(8,128)(2,1)} %reshape.312) | copy-start | bytes 1572868
  132.6 3.6 %copy-start.5 = (bf16[8,32,1024]{2,1,0:T(8,128)(2,1)S(1)}, bf16[8,32,1024]{2,1,0:T(8,128)(2,1)}, u32[]{:S(2)}) copy-start(bf16[8,32,1024]{2,1,0:T(8,128)(2,1)} %broadcast_select_fusion.1) | copy-start | bytes 1572868
  136.1 1.4 copy-start.3
  249.8 17.6 %all-to-all-start.2 = ((bf16[8,4,4224]{2,1,0:T(4,128)(2,1)}), bf16[8,4,4224]{2,1,0:T(4,128)(2,1)S(1)}, u32[]{:S(2)}, u32[]{:S(2)}) async-start(bf16[8,4,4224]{2,1,0:T(4,128)(2,1)} %reshape.321), calls=%async_computation.3 | async-start | bytes 540672 | tf_op jit(solution)/shard_map/all_to_all | solution.py:163
  267.4 29.1 %all-to-all-start.1 = ((bf16[8,32,2048]{2,1,0:T(8,128)(2,1)}), bf16[8,32,2048]{2,1,0:T(8,128)(2,1)S(1)}, u32[]{:S(2)}, u32[]{:S(2)}) async-start(bf16[8,32,2048]{2,1,0:T(8,128)(2,1)} %broadcast_select_fusion), calls=%async_computation.1 | async-start | bytes 2097152 | tf_op jit(solution)/shard_map/all_to_all | solution.py:143
  297.2 13.9 %all-to-all-start.3 = ((bf16[8,4,4224]{2,1,0:T(4,128)(2,1)}), bf16[8,4,4224]{2,1,0:T(4,128)(2,1)S(1)}, u32[]{:S(2)}, u32[]{:S(2)}) async-start(bf16[8,4,4224]{2,1,0:T(4,128)(2,1)} %broadcast_in_dim.188), calls=%async_computation.4 | async-start | bytes 540672 | tf_op jit(solution)/shard_map/all_to_all | solution.py:167
Sparse Core Ops, SparseCore 0:
  11.1 61.2 all-gather.1
  147.3 100.6 reduce-scatter.1

commit v3 on v2

--- a/solution.py
+++ b/solution.py
@@ -17,6 +17,7 @@
     rows = groups * length
     head_dim = width // HEADS
     scale = head_dim ** (-0.5)
+    f32 = jnp.float32
     x32 = tokens.astype(jnp.float32).reshape(rows, width)
     row_average = jnp.mean(x32, axis=1, keepdims=True)
     centered_rows = x32 - row_average
@@ -26,47 +27,45 @@
     standardized_rows = centered_rows * inverse_deviation
     gain_float32 = gain.astype(jnp.float32)
     layernorm_output = (standardized_rows * gain_float32).astype(jnp.bfloat16)
-    qkv = jnp.dot(layernorm_output, wqkv, preferred_element_type=jnp.float32).astype(jnp.bfloat16)
-    query = qkv[:, :width].reshape(groups, length, HEADS, head_dim)
-    keys = qkv[:, width : 2 * width].reshape(groups, length, HEADS, head_dim)
-    values = qkv[:, 2 * width :].reshape(groups, length, HEADS, head_dim)
-    scores = jnp.einsum("gqhd,gkhd->ghqk", query, keys, preferred_element_type=jnp.float32) * scale
-    scores = jnp.where(allowed[:, None], scores, NEG)
+    w3 = wqkv.reshape(width, 3, HEADS, head_dim)
+    qkv = jnp.einsum("rc,cjhd->jhrd", layernorm_output, w3, preferred_element_type=f32).astype(
+        jnp.bfloat16
+    )
+    qkv = qkv.reshape(3, HEADS, groups, length, head_dim)
+    query, keys, values = qkv[0], qkv[1], qkv[2]
+    scores = jnp.einsum("hgqd,hgkd->hgqk", query, keys, preferred_element_type=f32) * scale
+    scores = jnp.where(allowed[None], scores, NEG)
     top = jnp.max(scores, axis=-1, keepdims=True)
     expd = jnp.exp(scores - top)
     probs = expd / jnp.sum(expd, axis=-1, keepdims=True)
     weights = probs.astype(jnp.bfloat16)
-    context = (
-        jnp.einsum("ghqk,gkhd->gqhd", weights, values, preferred_element_type=jnp.float32)
-        .astype(jnp.bfloat16)
-        .reshape(rows, width)
-    )
-    result = (x32 + jnp.dot(context, wout, preferred_element_type=jnp.float32)).astype(jnp.bfloat16)
-    up_rows = upward.reshape(rows, width)
-    d_context = lax.dot_general(
-        up_rows, wout, (((1,), (1,)), ((), ())), preferred_element_type=jnp.float32
-    ).astype(jnp.bfloat16)
-    d_context = d_context.reshape(groups, length, HEADS, head_dim)
+    context = jnp.einsum("hgqk,hgkd->hgqd", weights, values, preferred_element_type=f32).astype(
+        jnp.bfloat16
+    )
+    wout3 = wout.reshape(HEADS, head_dim, width)
+    projected = jnp.einsum("hgqd,hde->gqe", context, wout3, preferred_element_type=f32)
+    result = (x32 + projected.reshape(rows, width)).astype(jnp.bfloat16)
+    up3 = upward.reshape(groups, length, width)
+    d_context = jnp.einsum("gqe,hde->hgqd", up3, wout3, preferred_element_type=f32).astype(
+        jnp.bfloat16
+    )
     d_values = jnp.einsum(
-        "ghqk,gqhd->gkhd", weights, d_context, preferred_element_type=jnp.float32
-    ).astype(jnp.bfloat16)
-    d_weights = jnp.einsum("gqhd,gkhd->ghqk", d_context, values, preferred_element_type=jnp.float32)
+        "hgqk,hgqd->hgkd", weights, d_context, preferred_element_type=f32
+    ).astype(jnp.bfloat16)
+    d_weights = jnp.einsum("hgqd,hgkd->hgqk", d_context, values, preferred_element_type=f32)
     d_scores = (
         probs * (d_weights - jnp.sum(d_weights * probs, axis=-1, keepdims=True)) * scale
     ).astype(jnp.bfloat16)
     d_query = jnp.einsum(
-        "ghqk,gkhd->gqhd", d_scores, keys, preferred_element_type=jnp.float32
+        "hgqk,hgkd->hgqd", d_scores, keys, preferred_element_type=f32
     ).astype(jnp.bfloat16)
     d_keys = jnp.einsum(
-        "ghqk,gqhd->gkhd", d_scores, query, preferred_element_type=jnp.float32
-    ).astype(jnp.bfloat16)
-    d_qkv = jnp.concatenate(
-        [d_query.reshape(rows, width), d_keys.reshape(rows, width), d_values.reshape(rows, width)],
-        axis=1,
-    )
-    layernorm_gradient = lax.dot_general(
-        d_qkv, wqkv, (((1,), (1,)), ((), ())), preferred_element_type=jnp.float32
-    )
+        "hgqk,hgqd->hgkd", d_scores, query, preferred_element_type=f32
+    ).astype(jnp.bfloat16)
+    d_qkv = jnp.stack([d_query, d_keys, d_values])
+    layernorm_gradient = jnp.einsum(
+        "jhgqd,cjhd->gqc", d_qkv, w3, preferred_element_type=f32
+    ).reshape(rows, width)
     gain_products = jnp.sum(layernorm_gradient * standardized_rows, axis=0)
     normalized_gradient = layernorm_gradient * gain_float32
     input_gradient = inverse_deviation * (
@@ -75,21 +74,23 @@
         - standardized_rows
         * jnp.mean(normalized_gradient * standardized_rows, axis=1, keepdims=True)
     )
+    up_rows = upward.reshape(rows, width)
     d_tokens = (up_rows.astype(jnp.float32) + input_gradient).astype(jnp.bfloat16)
+    grad_qkv_part = jnp.einsum(
+        "gqc,jhgqd->cjhd",
+        layernorm_output.reshape(groups, length, width),
+        d_qkv,
+        preferred_element_type=f32,
+    ).reshape(width, 3 * width)
+    grad_out_part = jnp.einsum(
+        "hgqd,gqe->hde", context, up3, preferred_element_type=f32
+    ).reshape(width, width)
     return (
         result.reshape(tokens.shape),
         d_tokens.reshape(tokens.shape),
-        layernorm_output,
-        context,
-        d_qkv,
-        up_rows,
+        grad_qkv_part,
+        grad_out_part,
         gain_products,
-    )
-
-
-def left_product(left, right):
-    return lax.dot_general(
-        left, right, (((0,), (0,)), ((), ())), preferred_element_type=jnp.float32
     )
 
 
@@ -137,7 +138,7 @@
     upward = jnp.take(returned, my_targets, axis=0)
     valid = slot[None, :] < my_counts[:, None]
     allowed = jnp.broadcast_to(valid[:, None, :], (batches, MAXVIS, MAXVIS))
-    result, d_tokens, layernorm_output, context, d_qkv, up_rows, gain_products = layer_core(
+    result, d_tokens, grad_qkv_part, grad_out_part, gain_products = layer_core(
         local_rows, upward, allowed, wqkv, wout, gain
     )
     came = lax.all_to_all(
@@ -153,8 +154,8 @@
     d_packed = jnp.take(came_grad.reshape(batches * MAXVIS, width), flat_rows, axis=0)
     partial = jnp.concatenate(
         [
-            left_product(layernorm_output, d_qkv).astype(jnp.bfloat16),
-            left_product(context, up_rows).astype(jnp.bfloat16),
+            grad_qkv_part.astype(jnp.bfloat16),
+            grad_out_part.astype(jnp.bfloat16),
             jnp.broadcast_to(gain_products.astype(jnp.bfloat16)[:, None], (width, 128)),
         ],
         axis=1,
@@ -189,6 +190,7 @@
         P("replica"),
         P("replica", "batch", None),
     )
+
     return jax.shard_map(
         on_device,
         mesh=mesh,

time: 321 us -> 320 us (level)
  matrix products: 44 us -> 39.2 us
    slice x1 -> x7, local copies, waits for them, and re-layouts: 1.19 us -> 21.4 us  [the longest x2 14.5 us: on_device(): wqkv = gathered[:, :qkv_cols]]
    reshape x8 -> x0, local copies, waits for them, and re-layouts: 15.3 us -> none  [the longest x1 2.54 us: layer_core(): values = qkv[:, 2 * width:].reshape(groups, length, HEADS, head_dim)]
    dot_general x0 -> x2, local copies, waits for them, and re-layouts: none -> 7.79 us  [layer_core(): jnp.einsum('gqc,jhgqd->cjhd', layernorm_output.reshape(groups, length, wi...]
    convert_element_type x4 -> x0, local copies, waits for them, and re-layouts: 5.32 us -> none  [the longest x1 1.64 us: layer_core(): d_values = jnp.einsum('ghqk,gqhd->gkhd', weights, d_context, preferred_el...]
    dot_general x11, matrix products: 39.9 us -> 35.3 us  [the longest x1 5.54 us: layer_core(): jnp.einsum('hgqk,hgqd->hgkd', d_scores, query, preferred_element_type=f32)]
    unnamed x21 -> x25, local copies, waits for them, and re-layouts: 4.79 us -> 0.61 us
where the time goes in v3:
time: 320 us; the launch traced here: 318 us
  waiting for transfers between devices  183 us (57%)
  local copies, waits for them, and re-layouts  43 us (13%)
  matrix products  39.2 us (12%)
  starting transfers between devices  22.5 us (7%)
  other arithmetic  16.5 us (5%)
  between operations  14.5 us (5%)
    reduce_scatter x1, waiting for transfers between devices, on_device(): lax.psum_scatter(partial, 'replica', scatter_dimension=0, tiled=True)  96.6 us
    all_gather x1, waiting for transfers between devices, on_device(): lax.all_gather(jnp.concatenate([qkv_weight, out_weight, gain_block], axis...  30.2 us
    all_to_all x1, waiting for transfers between devices, on_device(): lax.all_to_all(jnp.take(jnp.concatenate([result, d_tokens], axis=-1), to_...  25.2 us
    slice x2, local copies, waits for them, and re-layouts, on_device(): wqkv = gathered[:, :qkv_cols]  14.5 us
    all_to_all x1, waiting for transfers between devices, on_device(): lax.all_to_all(backward_rows, 'batch', split_axis=0, concat_axis=0, tiled...  13.6 us
    all_to_all x1, waiting for transfers between devices, on_device(): lax.all_to_all(summed.reshape(batches, -1, summed.shape[1]), 'batch', spl...  9.42 us
    all_to_all x1, starting transfers between devices, on_device(): lax.all_to_all(backward_rows, 'batch', split_axis=0, concat_axis=0, tiled...  8.47 us
    dot_general x2, local copies, waits for them, and re-layouts, layer_core(): jnp.einsum('gqc,jhgqd->cjhd', layernorm_output.reshape(groups, length, wi...  7.79 us
  transfers between devices with their start and end apart: 6, of which 6 were waited for; matrix products, arithmetic and copies ran while one was open for 6% of the time, Pallas kernels for 0%

profile of v3, /device:TPU:2, one launch (start us, length us, event | category | flops | bytes accessed | tf_op | source)
XLA Modules:
  0.0 318.4 jit_solution(15735185377165815285)
XLA Ops:
  7.2 0.8 broadcast_in_dim.170
  8.1 1.7 pad_maximum_fusion.3
  10.3 1.3 reduce.14
  11.6 1.3 reduce.13
  13.5 1.2 gather_fusion
  14.7 1.0 select_select_fusion
  15.7 8.5 %all-to-all-start = ((bf16[8,32,1024]{2,1,0:T(8,128)(2,1)}), bf16[8,32,1024]{2,1,0:T(8,128)(2,1)S(1)}, u32[]{:S(2)}, u32[]{:S(2)}) async-start(bf16[8,32,1024]{2,1,0:T(8,128)(2,1)} %select_select_fusion), calls=%async_computation | async-start | bytes 1048576 | tf_op jit(solution)/shard_map/all_to_all | solution.py:137
  24.3 2.8 gather_fusion.3
  28.1 13.6 %all-to-all-done = bf16[8,32,1024]{2,1,0:T(8,128)(2,1)S(1)} async-done(((bf16[8,32,1024]{2,1,0:T(8,128)(2,1)}), bf16[8,32,1024]{2,1,0:T(8,128)(2,1)S(1)}, u32[]{:S(2)}, u32[]{:S(2)}) %all-to-all-start) | async-done | bytes 524320 | tf_op jit(solution)/shard_map/all_to_all | solution.py:137
  42.2 30.2 %all-gather.2.cloned.1.call-done = bf16[1024,4224]{1,0:T(8,128)(2,1)} async-done(((bf16[32,4224]{1,0:T(8,128)(2,1)}), bf16[1024,4224]{1,0:T(8,128)(2,1)}) %all-gather.2.cloned.1.call-update) | async-done | bytes 8650768 | tf_op jit(solution)/shard_map/all_gather | solution.py:103
  72.4 1.1 convert_reduce_fusion.1
  73.8 6.0 %slice.70 = bf16[1024,3072]{1,0:T(8,128)(2,1)} slice(bf16[1024,4224]{1,0:T(8,128)(2,1)} %all-gather.2.cloned.1.call-done), slice={[0:1024], [0:3072]} | slice | bytes 12582912 | tf_op jit(solution)/shard_map/slice | solution.py:106
  79.8 8.5 %copy.35 = bf16[1024,3072]{0,1:T(8,128)(2,1)} copy(bf16[1024,3072]{1,0:T(8,128)(2,1)} %slice.70) | data formatting | bytes 12582912 | tf_op jit(solution)/shard_map/slice | solution.py:106
  88.3 4.6 %fusion.21 = bf16[3,16,256,64]{2,3,1,0:T(8,128)(2,1)S(1)} fusion(bf16[1024,3,16,64]{0,3,2,1:T(8,128)(2,1)} %bitcast.118, bf16[256,1024,1,1]{1,0,3,2:T(8,128)(2,1)S(1)} %bitcast.132), kind=kOutput, calls=%fused_computation.27 | convolution fusion | flops 1611399168 | bytes 8388608 | tf_op jit(solution)/shard_map/rc,cjhd->jhrd/dot_general | solution.py:31
  92.9 0.9 fusion.83
  93.8 1.5 copy.38
  95.4 1.3 copy.37
  96.7 1.3 copy.36
  98.0 1.8 slice.75
  99.8 1.3 fusion.34
  101.1 2.0 fusion.86
  103.1 3.8 %fusion.85 = (f32[16,8,32]{2,1,0:T(8,128)S(1)}, f32[16,8,32,32]{2,3,1,0:T(8,128)}) fusion(pred[8,32]{1,0:T(8,128)(4,1)S(1)} %iota_compare_fusion.3, bf16[16,8,32,64]{3,2,1,0:T(8,128)(2,1)} %bitcast.129, bf16[16,8,32,64]{3,2,1,0:T(8,128)(2,1)} %bitcast.127), kind=kOutput, calls=%fused_computation.148 | convolution fusion | flops 17301536 | bytes 1589504 | tf_op jit(solution)/shard_map/sub | solution.py:39
  107.0 3.1 convolution_convert_fusion.3
  110.0 4.6 %fusion.26 = bf16[1,16,8,32,64]{4,3,2,1,0:T(8,128)(2,1)S(1)} fusion(bf16[16,8,32,64]{3,2,1,0:T(8,128)(2,1)} %bitcast.128, f32[16,8,32,32]{2,3,1,0:T(8,128)} %fusion.86, f32[16,8,32,32]{2,3,1,0:T(8,128)} %get-tuple-element.39, f32[16,8,32]{2,1,0:T(8,128)S(1)} %get-tuple-element.38), kind=kOutput, calls=%fused_computation.32 | convolution fusion | flops 17960992 | bytes 2113536 | tf_op jit(solution)/shard_map/hgqk,hgkd->hgqd/dot_general | solution.py:59
  114.7 5.5 %fusion.23 = bf16[1,16,8,32,64]{4,3,2,1,0:T(8,128)(2,1)} fusion(bf16[16,8,32,64]{3,2,1,0:T(8,128)(2,1)} %bitcast.130, f32[16,8,32,32]{2,3,1,0:T(8,128)} %fusion.86, f32[16,8,32,32]{2,3,1,0:T(8,128)} %get-tuple-element.39, f32[16,8,32]{2,1,0:T(8,128)S(1)} %get-tuple-element.38), kind=kOutput, calls=%fused_computation.31 | convolution fusion | flops 17960992 | bytes 2113536 | tf_op jit(solution)/shard_map/hgqk,hgqd->hgkd/dot_general | solution.py:62
  120.2 2.4 fusion.22
  122.6 2.1 bitcast_convert_fusion.1
  124.8 2.1 fusion.82
  126.9 3.7 %copy.44 = bf16[3,16,64,8,32]{2,1,0,4,3:T(8,128)(2,1)} copy(bf16[3,16,64,8,32]{2,4,3,1,0:T(8,128)(2,1)S(1)} %get-tuple-element.29) | data formatting | bytes 3145728 | tf_op jit(solution)/shard_map/gqc,jhgqd->cjhd/dot_general | solution.py:79
  130.6 4.1 %dot_general.60 = bf16[3072,8,32]{0,2,1:T(8,128)(2,1)S(1)} reshape(bf16[3,16,64,8,32]{2,1,0,4,3:T(8,128)(2,1)} %copy.44) | data formatting | bytes 3145728 | tf_op jit(solution)/shard_map/gqc,jhgqd->cjhd/dot_general | solution.py:79
  134.7 1.8 bitcast_convert_fusion
  136.6 5.1 %fusion.50 = (bf16[1024]{0:T(1024)(128)(2,1)S(1)}, f32[256]{0:T(256)S(1)}, f32[256]{0:T(256)S(1)}, f32[256,1024]{1,0:T(8,128)S(1)}) fusion(f32[256]{0:T(256)S(1)} %div.59, f32[256]{0:T(256)S(1)} %rsqrt.13, bf16[256,1024]{1,0:T(8,128)(2,1)S(1)} %gather_fusion.3, pred[256]{0:T(512)(128)(4,1)S(1)} %compare_and_fusion.4, f32[1024]{0:T(1024)S(1)} %convert_reduce_fusion.1, ...), kind=kOutput, calls=%fused_computation.55 | convolution fusion | flops 1613232640 | bytes 9447680 | tf_op jit(solution)/shard_map/jhgqd,cjhd->gqc/dot_general | solution.py:66
  141.9 3.7 %pad_maximum_fusion = bf16[1024,4224]{1,0:T(8,128)(2,1)} fusion(bf16[1024,128]{1,0:T(8,128)(2,1)S(1)} %broadcast_in_dim.187, bf16[1024,1024]{1,0:T(8,128)(2,1)S(1)} %bitcast.117, bf16[1024,3072]{1,0:T(8,128)(2,1)S(1)} %bitcast_convert_fusion), kind=kLoop, calls=%fused_computation.9 | loop fusion | flops 25952256 | bytes 17301504 | tf_op jit(solution)/shard_map/concatenate | solution.py:155
  146.5 2.7 fusion.35
  149.9 96.6 %reduce-scatter.2.cloned.1.call-done = bf16[32,4224]{1,0:T(8,128)(2,1)} async-done(((bf16[1024,4224]{1,0:T(8,128)(2,1)}), bf16[32,4224]{1,0:T(8,128)(2,1)}) %reduce-scatter.2.cloned.1.call-update) | async-done | bytes 270352 | tf_op jit(solution)/shard_map/reduce_scatter | solution.py:163
  246.5 1.7 reshape.406
  248.2 7.0 %all-to-all-start.2 = ((bf16[8,4,4224]{2,1,0:T(4,128)(2,1)}), bf16[8,4,4224]{2,1,0:T(4,128)(2,1)S(1)}, u32[]{:S(2)}, u32[]{:S(2)}) async-start(bf16[8,4,4224]{2,1,0:T(4,128)(2,1)} %reshape.406), calls=%async_computation.3 | async-start | bytes 540672 | tf_op jit(solution)/shard_map/all_to_all | solution.py:164
  255.2 1.2 broadcast_select_fusion
  256.4 9.4 %all-to-all-done.2 = bf16[8,4,4224]{2,1,0:T(4,128)(2,1)S(1)} async-done(((bf16[8,4,4224]{2,1,0:T(4,128)(2,1)}), bf16[8,4,4224]{2,1,0:T(4,128)(2,1)S(1)}, u32[]{:S(2)}, u32[]{:S(2)}) %all-to-all-start.2) | async-done | bytes 270368 | tf_op jit(solution)/shard_map/all_to_all | solution.py:164
  265.8 3.6 %all-to-all-start.1 = ((bf16[8,32,2048]{2,1,0:T(8,128)(2,1)}), bf16[8,32,2048]{2,1,0:T(8,128)(2,1)S(1)}, u32[]{:S(2)}, u32[]{:S(2)}) async-start(bf16[8,32,2048]{2,1,0:T(8,128)(2,1)} %broadcast_select_fusion), calls=%async_computation.1 | async-start | bytes 2097152 | tf_op jit(solution)/shard_map/all_to_all | solution.py:144
  269.6 25.2 %all-to-all-done.1 = bf16[8,32,2048]{2,1,0:T(8,128)(2,1)S(1)} async-done(((bf16[8,32,2048]{2,1,0:T(8,128)(2,1)}), bf16[8,32,2048]{2,1,0:T(8,128)(2,1)S(1)}, u32[]{:S(2)}, u32[]{:S(2)}) %all-to-all-start.1) | async-done | bytes 1048608 | tf_op jit(solution)/shard_map/all_to_all | solution.py:144
  294.8 0.8 broadcast_in_dim.188
  295.6 3.4 %all-to-all-start.3 = ((bf16[8,4,4224]{2,1,0:T(4,128)(2,1)}), bf16[8,4,4224]{2,1,0:T(4,128)(2,1)S(1)}, u32[]{:S(2)}, u32[]{:S(2)}) async-start(bf16[8,4,4224]{2,1,0:T(4,128)(2,1)} %broadcast_in_dim.188), calls=%async_computation.4 | async-start | bytes 540672 | tf_op jit(solution)/shard_map/all_to_all | solution.py:168
  299.1 0.9 gather_fusion.5
  300.0 0.9 gather_fusion.4
  300.8 0.9 select_bitcast_fusion
  301.7 7.8 %all-to-all-done.3 = bf16[8,4,4224]{2,1,0:T(4,128)(2,1)S(1)} async-done(((bf16[8,4,4224]{2,1,0:T(4,128)(2,1)}), bf16[8,4,4224]{2,1,0:T(4,128)(2,1)S(1)}, u32[]{:S(2)}, u32[]{:S(2)}) %all-to-all-start.3) | async-done | bytes 270368 | tf_op jit(solution)/shard_map/all_to_all | solution.py:168
  310.8 0.8 slice.78
  (76 shorter events, 6.5 us)
Async XLA Ops:
  7.2 17.2 %copy-start = (bf16[1,8,64,1024]{3,2,1,0:T(8,128)(2,1)S(1)}, bf16[1,8,64,1024]{3,2,1,0:T(8,128)(2,1)}, u32[]{:S(2)}) copy-start(bf16[1,8,64,1024]{3,2,1,0:T(8,128)(2,1)} %param.12) | copy-start | bytes 3145732
  7.2 6.3 %copy-start.2 = (bf16[1,128,1024]{2,1,0:T(8,128)(2,1)S(1)}, bf16[1,128,1024]{2,1,0:T(8,128)(2,1)}, u32[]{:S(2)}) copy-start(bf16[1,128,1024]{2,1,0:T(8,128)(2,1)} %param.19) | copy-start | bytes 786436
  7.2 65.2 %all-gather.2.cloned.1.call-start = ((), (), s32[]{:S(2)}) async-start(), calls=%async_computation.5 | async-start | bytes 8921088 | tf_op jit(solution)/shard_map/all_gather | solution.py:103
  14.6 9.6 %copy-start.11 = (s32[1,8,64]{2,1,0:T(8,128)S(1)}, s32[1,8,64]{2,1,0:T(8,128)}, u32[]{:S(2)}) copy-start(s32[1,8,64]{2,1,0:T(8,128)} %param.13) | copy-start | bytes 6148
  15.7 26.0 %all-to-all-start = ((bf16[8,32,1024]{2,1,0:T(8,128)(2,1)}), bf16[8,32,1024]{2,1,0:T(8,128)(2,1)S(1)}, u32[]{:S(2)}, u32[]{:S(2)}) async-start(bf16[8,32,1024]{2,1,0:T(8,128)(2,1)} %select_select_fusion), calls=%async_computation | async-start | bytes 1048576 | tf_op jit(solution)/shard_map/all_to_all | solution.py:137
  24.2 222.3 %reduce-scatter.2.cloned.1.call-start = ((), (), s32[]{:S(2)}) async-start(), calls=%async_computation.6 | async-start | bytes 8921088 | tf_op jit(solution)/shard_map/reduce_scatter | solution.py:163
  73.8 14.5 %copy-start.9 = (bf16[8,32,1024]{2,1,0:T(8,128)(2,1)}, bf16[8,32,1024]{2,1,0:T(8,128)(2,1)S(1)}, u32[]{:S(2)}) copy-start(bf16[8,32,1024]{2,1,0:T(8,128)(2,1)S(1)} %fusion.40) | copy-start | bytes 1572868
  99.8 1.3 copy-start.5
  101.1 2.0 copy-start.8
  120.2 2.4 copy-start.7
  122.6 2.2 copy-start.6
  130.6 4.1 %copy-start.10 = (bf16[8,32,1024]{2,1,0:T(8,128)(2,1)S(1)}, bf16[8,32,1024]{2,1,0:T(8,128)(2,1)}, u32[]{:S(2)}) copy-start(bf16[8,32,1024]{2,1,0:T(8,128)(2,1)} %copy-done.9) | copy-start | bytes 1572868
  134.7 1.9 copy-start.4
  136.6 5.3 %copy-start.3 = (bf16[16,64,1024]{2,1,0:T(8,128)(2,1)S(1)}, bf16[16,64,1024]{2,1,0:T(8,128)(2,1)}, u32[]{:S(2)}) copy-start(bf16[16,64,1024]{2,1,0:T(8,128)(2,1)} %bitcast_convert_fusion.1) | copy-start | bytes 6291460
  248.2 17.6 %all-to-all-start.2 = ((bf16[8,4,4224]{2,1,0:T(4,128)(2,1)}), bf16[8,4,4224]{2,1,0:T(4,128)(2,1)S(1)}, u32[]{:S(2)}, u32[]{:S(2)}) async-start(bf16[8,4,4224]{2,1,0:T(4,128)(2,1)} %reshape.406), calls=%async_computation.3 | async-start | bytes 540672 | tf_op jit(solution)/shard_map/all_to_all | solution.py:164
  265.8 29.0 %all-to-all-start.1 = ((bf16[8,32,2048]{2,1,0:T(8,128)(2,1)}), bf16[8,32,2048]{2,1,0:T(8,128)(2,1)S(1)}, u32[]{:S(2)}, u32[]{:S(2)}) async-start(bf16[8,32,2048]{2,1,0:T(8,128)(2,1)} %broadcast_select_fusion), calls=%async_computation.1 | async-start | bytes 2097152 | tf_op jit(solution)/shard_map/all_to_all | solution.py:144
  295.6 13.9 %all-to-all-start.3 = ((bf16[8,4,4224]{2,1,0:T(4,128)(2,1)}), bf16[8,4,4224]{2,1,0:T(4,128)(2,1)S(1)}, u32[]{:S(2)}, u32[]{:S(2)}) async-start(bf16[8,4,4224]{2,1,0:T(4,128)(2,1)} %broadcast_in_dim.188), calls=%async_computation.4 | async-start | bytes 540672 | tf_op jit(solution)/shard_map/all_to_all | solution.py:168
  300.0 11.6 %copy-start.1 = (bf16[1,8,64,1024]{3,2,1,0:T(8,128)(2,1)S(1)}, bf16[1,8,64,1024]{3,2,1,0:T(8,128)(2,1)}, u32[]{:S(2)}) copy-start(bf16[1,8,64,1024]{3,2,1,0:T(8,128)(2,1)} %param.12) | copy-start | bytes 3145732
Sparse Core Ops, SparseCore 0:
  11.1 61.2 all-gather.1
  145.7 100.6 reduce-scatter.1

commit v4 on v3

--- a/solution.py
+++ b/solution.py
@@ -27,11 +27,8 @@
     standardized_rows = centered_rows * inverse_deviation
     gain_float32 = gain.astype(jnp.float32)
     layernorm_output = (standardized_rows * gain_float32).astype(jnp.bfloat16)
-    w3 = wqkv.reshape(width, 3, HEADS, head_dim)
-    qkv = jnp.einsum("rc,cjhd->jhrd", layernorm_output, w3, preferred_element_type=f32).astype(
-        jnp.bfloat16
-    )
-    qkv = qkv.reshape(3, HEADS, groups, length, head_dim)
+    qkv = jnp.dot(layernorm_output, wqkv, preferred_element_type=f32).astype(jnp.bfloat16)
+    qkv = jnp.transpose(qkv.reshape(groups, length, 3, HEADS, head_dim), (2, 3, 0, 1, 4))
     query, keys, values = qkv[0], qkv[1], qkv[2]
     scores = jnp.einsum("hgqd,hgkd->hgqk", query, keys, preferred_element_type=f32) * scale
     scores = jnp.where(allowed[None], scores, NEG)
@@ -62,10 +59,12 @@
     d_keys = jnp.einsum(
         "hgqk,hgqd->hgkd", d_scores, query, preferred_element_type=f32
     ).astype(jnp.bfloat16)
-    d_qkv = jnp.stack([d_query, d_keys, d_values])
-    layernorm_gradient = jnp.einsum(
-        "jhgqd,cjhd->gqc", d_qkv, w3, preferred_element_type=f32
-    ).reshape(rows, width)
+    d_qkv = jnp.transpose(jnp.stack([d_query, d_keys, d_values]), (2, 3, 0, 1, 4)).reshape(
+        rows, 3 * width
+    )
+    layernorm_gradient = lax.dot_general(
+        d_qkv, wqkv, (((1,), (1,)), ((), ())), preferred_element_type=f32
+    )
     gain_products = jnp.sum(layernorm_gradient * standardized_rows, axis=0)
     normalized_gradient = layernorm_gradient * gain_float32
     input_gradient = inverse_deviation * (
@@ -76,12 +75,7 @@
     )
     up_rows = upward.reshape(rows, width)
     d_tokens = (up_rows.astype(jnp.float32) + input_gradient).astype(jnp.bfloat16)
-    grad_qkv_part = jnp.einsum(
-        "gqc,jhgqd->cjhd",
-        layernorm_output.reshape(groups, length, width),
-        d_qkv,
-        preferred_element_type=f32,
-    ).reshape(width, 3 * width)
+    grad_qkv_part = left_product(layernorm_output, d_qkv)
     grad_out_part = jnp.einsum(
         "hgqd,gqe->hde", context, up3, preferred_element_type=f32
     ).reshape(width, width)
@@ -91,6 +85,12 @@
         grad_qkv_part,
         grad_out_part,
         gain_products,
+    )
+
+
+def left_product(left, right):
+    return lax.dot_general(
+        left, right, (((0,), (0,)), ((), ())), preferred_element_type=jnp.float32
     )
 
 

time: 320 us -> 310 us (0.969)
  local copies, waits for them, and re-layouts: 43 us -> 33.1 us
    slice x6 -> x0, local copies, waits for them, and re-layouts: 19.6 us -> none  [the longest x2 14.5 us: on_device(): wqkv = gathered[:, :qkv_cols]]
    reshape x0 -> x3, local copies, waits for them, and re-layouts: none -> 10.5 us  [the longest x2 6.26 us: layer_core(): qkv.reshape(groups, length, 3, HEADS, head_dim)]
    dot_general x2 -> x0, local copies, waits for them, and re-layouts: 7.79 us -> none  [layer_core(): jnp.einsum('gqc,jhgqd->cjhd', layernorm_output.reshape(groups, length, wi...]
    transpose x0 -> x1, local copies, waits for them, and re-layouts: none -> 3.74 us  [layer_core(): jnp.transpose(jnp.stack([d_query, d_keys, d_values]), (2, 3, 0, 1, 4))]
where the time goes in v4:
time: 310 us; the launch traced here: 309 us
  waiting for transfers between devices  182 us (59%)
  matrix products  40.6 us (13%)
  local copies, waits for them, and re-layouts  33.1 us (11%)
  starting transfers between devices  22.5 us (7%)
  other arithmetic  16.7 us (5%)
  between operations  14.4 us (5%)
    reduce_scatter x1, waiting for transfers between devices, on_device(): lax.psum_scatter(partial, 'replica', scatter_dimension=0, tiled=True)  95.8 us
    all_gather x1, waiting for transfers between devices, on_device(): lax.all_gather(jnp.concatenate([qkv_weight, out_weight, gain_block], axis...  30.2 us
    all_to_all x1, waiting for transfers between devices, on_device(): lax.all_to_all(jnp.take(jnp.concatenate([result, d_tokens], axis=-1), to_...  25.2 us
    all_to_all x1, waiting for transfers between devices, on_device(): lax.all_to_all(backward_rows, 'batch', split_axis=0, concat_axis=0, tiled...  13.6 us
    all_to_all x1, waiting for transfers between devices, on_device(): lax.all_to_all(summed.reshape(batches, -1, summed.shape[1]), 'batch', spl...  9.42 us
    all_to_all x1, starting transfers between devices, on_device(): lax.all_to_all(backward_rows, 'batch', split_axis=0, concat_axis=0, tiled...  8.47 us
    all_to_all x1, waiting for transfers between devices, on_device(): lax.all_to_all(jnp.broadcast_to(reduced[None], (batches,) + reduced.shape...  7.74 us
    all_to_all x1, starting transfers between devices, on_device(): lax.all_to_all(summed.reshape(batches, -1, summed.shape[1]), 'batch', spl...  7.01 us
  transfers between devices with their start and end apart: 6, of which 6 were waited for; matrix products, arithmetic and copies ran while one was open for 6% of the time, Pallas kernels for 0%

profile of v4, /device:TPU:2, one launch (start us, length us, event | category | flops | bytes accessed | tf_op | source)
XLA Modules:
  0.0 309.2 jit_solution(14856552765534479517)
XLA Ops:
  7.2 0.8 broadcast_in_dim.172
  8.1 1.7 pad_maximum_fusion.2
  10.3 1.3 reduce.14
  11.6 1.3 reduce.13
  13.5 1.2 gather_fusion
  14.7 1.0 select_select_fusion
  15.7 8.5 %all-to-all-start = ((bf16[8,32,1024]{2,1,0:T(8,128)(2,1)}), bf16[8,32,1024]{2,1,0:T(8,128)(2,1)S(1)}, u32[]{:S(2)}, u32[]{:S(2)}) async-start(bf16[8,32,1024]{2,1,0:T(8,128)(2,1)} %select_select_fusion), calls=%async_computation | async-start | bytes 1048576 | tf_op jit(solution)/shard_map/all_to_all | solution.py:137
  24.3 2.8 gather_fusion.3
  28.1 13.6 %all-to-all-done = bf16[8,32,1024]{2,1,0:T(8,128)(2,1)S(1)} async-done(((bf16[8,32,1024]{2,1,0:T(8,128)(2,1)}), bf16[8,32,1024]{2,1,0:T(8,128)(2,1)S(1)}, u32[]{:S(2)}, u32[]{:S(2)}) %all-to-all-start) | async-done | bytes 524320 | tf_op jit(solution)/shard_map/all_to_all | solution.py:137
  42.2 30.2 %all-gather.2.cloned.1.call-done = bf16[1024,4224]{1,0:T(8,128)(2,1)} async-done(((bf16[32,4224]{1,0:T(8,128)(2,1)}), bf16[1024,4224]{1,0:T(8,128)(2,1)}) %all-gather.2.cloned.1.call-update) | async-done | bytes 8650768 | tf_op jit(solution)/shard_map/all_gather | solution.py:103
  72.4 1.1 convert_reduce_fusion.1
  73.8 4.7 %fusion.6 = bf16[256,3072]{1,0:T(8,128)(2,1)S(1)} fusion(bf16[1024,4224]{1,0:T(8,128)(2,1)} %all-gather.2.cloned.1.call-done, f32[1024]{0:T(1024)S(1)} %convert_reduce_fusion.1, f32[256]{0:T(256)S(1)} %rsqrt.13, f32[256]{0:T(256)S(1)} %div.51, bf16[256,1024]{1,0:T(8,128)(2,1)S(1)} %gather_fusion.3, pred[256]{0:T(512)(128)(4,1)S(1)} %compare_and_fusion.4), kind=kOutput, calls=%fused_computation.15 | convolution fusion | flops 1612972032 | bytes 8395008 | tf_op jit(solution)/shard_map/dot_general | solution.py:30
  78.5 3.6 %reshape.361 = bf16[8,32,3,16,64]{4,3,2,1,0:T(8,128)(2,1)} reshape(bf16[256,3072]{1,0:T(8,128)(2,1)S(1)} %fusion.6) | data formatting | bytes 3145728 | tf_op jit(solution)/shard_map/reshape | solution.py:31
  82.1 2.7 copy.33
  84.8 2.9 slice.72
  87.7 1.3 fusion.32
  89.2 1.0 copy-done.6
  90.2 2.0 fusion.57
  92.2 3.8 %fusion.87 = (f32[16,8,32]{2,1,0:T(8,128)S(1)}, f32[16,8,32,32]{2,3,1,0:T(8,128)}) fusion(pred[8,32]{1,0:T(8,128)(4,1)S(1)} %iota_compare_fusion.3, bf16[3,16,8,32,64]{4,3,2,1,0:T(8,128)(2,1)} %bitcast.122), kind=kOutput, calls=%fused_computation.155 | convolution fusion | flops 17301536 | bytes 2638080 | tf_op jit(solution)/shard_map/sub | solution.py:36
  95.9 2.4 fusion.25
  98.5 2.8 convolution_convert_fusion.3
  101.3 5.6 %fusion.29 = bf16[1,16,8,32,64]{4,3,2,1,0:T(8,128)(2,1)} fusion(f32[16,8,32,32]{2,3,1,0:T(8,128)} %fusion.57, bf16[3,16,8,32,64]{4,3,2,1,0:T(8,128)(2,1)} %bitcast.124, f32[16,8,32,32]{2,3,1,0:T(8,128)} %get-tuple-element.34, f32[16,8,32]{2,1,0:T(8,128)S(1)} %get-tuple-element.33), kind=kOutput, calls=%fused_computation.33 | convolution fusion | flops 17960992 | bytes 10092544 | tf_op jit(solution)/shard_map/hgqk,hgkd->hgqd/dot_general | solution.py:56
  106.9 5.6 %fusion.26 = bf16[1,16,8,32,64]{4,3,2,1,0:T(8,128)(2,1)} fusion(f32[16,8,32,32]{2,3,1,0:T(8,128)} %fusion.57, bf16[3,16,8,32,64]{4,3,2,1,0:T(8,128)(2,1)} %bitcast.125, f32[16,8,32,32]{2,3,1,0:T(8,128)} %get-tuple-element.34, f32[16,8,32]{2,1,0:T(8,128)S(1)} %get-tuple-element.33), kind=kOutput, calls=%fused_computation.32 | convolution fusion | flops 17960992 | bytes 10092544 | tf_op jit(solution)/shard_map/hgqk,hgqd->hgkd/dot_general | solution.py:59
  112.5 2.3 maximum_bitcast_fusion
  114.8 3.7 %copy.26 = bf16[8,32,3,16,64]{4,3,2,1,0:T(8,128)(2,1)} copy(bf16[8,32,3,16,64]{4,1,0,3,2:T(8,128)(2,1)S(1)} %maximum_bitcast_fusion) | data formatting | bytes 3145728 | tf_op jit(solution)/shard_map/transpose | solution.py:62
  118.5 4.2 %reshape.364 = bf16[256,3072]{1,0:T(8,128)(2,1)S(1)} reshape(bf16[8,32,3,16,64]{4,3,2,1,0:T(8,128)(2,1)} %copy.26) | data formatting | bytes 3145728 | tf_op jit(solution)/shard_map/reshape | solution.py:62
  122.7 2.0 bitcast_convert_fusion
  124.8 1.8 convolution_convert_fusion
  126.6 5.9 %fusion.50 = (bf16[1024]{0:T(1024)(128)(2,1)S(1)}, f32[256]{0:T(256)S(1)}, f32[256]{0:T(256)S(1)}, f32[256,1024]{1,0:T(8,128)}) fusion(f32[256]{0:T(256)S(1)} %rsqrt.13, f32[256]{0:T(256)S(1)} %div.51, bf16[256,1024]{1,0:T(8,128)(2,1)S(1)} %gather_fusion.3, pred[256]{0:T(512)(128)(4,1)S(1)} %compare_and_fusion.4, f32[1024]{0:T(1024)S(1)} %convert_reduce_fusion.1, ...), kind=kOutput, calls=%fused_computation.57 | convolution fusion | flops 1613232640 | bytes 9447680 | tf_op jit(solution)/shard_map/dot_general | solution.py:65
  132.7 3.7 %pad_maximum_fusion = bf16[1024,4224]{1,0:T(8,128)(2,1)} fusion(bf16[1024,128]{1,0:T(8,128)(2,1)S(1)} %broadcast_in_dim.187, bf16[1024,1024]{1,0:T(8,128)(2,1)S(1)} %bitcast.120, bf16[1024,3072]{1,0:T(8,128)(2,1)S(1)} %convolution_convert_fusion), kind=kLoop, calls=%fused_computation.8 | loop fusion | flops 25952256 | bytes 17301504 | tf_op jit(solution)/shard_map/concatenate | solution.py:155
  136.7 0.9 copy-done.5
  138.1 2.7 fusion.33
  141.5 95.8 %reduce-scatter.2.cloned.1.call-done = bf16[32,4224]{1,0:T(8,128)(2,1)} async-done(((bf16[1024,4224]{1,0:T(8,128)(2,1)}), bf16[32,4224]{1,0:T(8,128)(2,1)}) %reduce-scatter.2.cloned.1.call-update) | async-done | bytes 270352 | tf_op jit(solution)/shard_map/reduce_scatter | solution.py:163
  237.2 1.7 reshape.368
  239.0 7.0 %all-to-all-start.2 = ((bf16[8,4,4224]{2,1,0:T(4,128)(2,1)}), bf16[8,4,4224]{2,1,0:T(4,128)(2,1)S(1)}, u32[]{:S(2)}, u32[]{:S(2)}) async-start(bf16[8,4,4224]{2,1,0:T(4,128)(2,1)} %reshape.368), calls=%async_computation.3 | async-start | bytes 540672 | tf_op jit(solution)/shard_map/all_to_all | solution.py:164
  246.0 1.2 broadcast_select_fusion
  247.1 9.4 %all-to-all-done.2 = bf16[8,4,4224]{2,1,0:T(4,128)(2,1)S(1)} async-done(((bf16[8,4,4224]{2,1,0:T(4,128)(2,1)}), bf16[8,4,4224]{2,1,0:T(4,128)(2,1)S(1)}, u32[]{:S(2)}, u32[]{:S(2)}) %all-to-all-start.2) | async-done | bytes 270368 | tf_op jit(solution)/shard_map/all_to_all | solution.py:164
  256.5 3.6 %all-to-all-start.1 = ((bf16[8,32,2048]{2,1,0:T(8,128)(2,1)}), bf16[8,32,2048]{2,1,0:T(8,128)(2,1)S(1)}, u32[]{:S(2)}, u32[]{:S(2)}) async-start(bf16[8,32,2048]{2,1,0:T(8,128)(2,1)} %broadcast_select_fusion), calls=%async_computation.1 | async-start | bytes 2097152 | tf_op jit(solution)/shard_map/all_to_all | solution.py:144
  260.3 25.2 %all-to-all-done.1 = bf16[8,32,2048]{2,1,0:T(8,128)(2,1)S(1)} async-done(((bf16[8,32,2048]{2,1,0:T(8,128)(2,1)}), bf16[8,32,2048]{2,1,0:T(8,128)(2,1)S(1)}, u32[]{:S(2)}, u32[]{:S(2)}) %all-to-all-start.1) | async-done | bytes 1048608 | tf_op jit(solution)/shard_map/all_to_all | solution.py:144
  285.6 0.8 broadcast_in_dim.188
  286.4 3.4 %all-to-all-start.3 = ((bf16[8,4,4224]{2,1,0:T(4,128)(2,1)}), bf16[8,4,4224]{2,1,0:T(4,128)(2,1)S(1)}, u32[]{:S(2)}, u32[]{:S(2)}) async-start(bf16[8,4,4224]{2,1,0:T(4,128)(2,1)} %broadcast_in_dim.188), calls=%async_computation.4 | async-start | bytes 540672 | tf_op jit(solution)/shard_map/all_to_all | solution.py:168
  289.9 0.9 gather_fusion.5
  290.7 0.9 gather_fusion.4
  291.6 0.9 select_bitcast_fusion
  292.5 7.7 %all-to-all-done.3 = bf16[8,4,4224]{2,1,0:T(4,128)(2,1)S(1)} async-done(((bf16[8,4,4224]{2,1,0:T(4,128)(2,1)}), bf16[8,4,4224]{2,1,0:T(4,128)(2,1)S(1)}, u32[]{:S(2)}, u32[]{:S(2)}) %all-to-all-start.3) | async-done | bytes 270368 | tf_op jit(solution)/shard_map/all_to_all | solution.py:168
  300.3 0.6 slice_reduce_fusion
  300.9 0.7 slice.76
  301.6 0.8 slice.75
  (66 shorter events, 5.4 us)
Async XLA Ops:
  7.2 17.2 %copy-start = (bf16[1,8,64,1024]{3,2,1,0:T(8,128)(2,1)S(1)}, bf16[1,8,64,1024]{3,2,1,0:T(8,128)(2,1)}, u32[]{:S(2)}) copy-start(bf16[1,8,64,1024]{3,2,1,0:T(8,128)(2,1)} %param.12) | copy-start | bytes 3145732
  7.2 6.3 %copy-start.2 = (bf16[1,128,1024]{2,1,0:T(8,128)(2,1)S(1)}, bf16[1,128,1024]{2,1,0:T(8,128)(2,1)}, u32[]{:S(2)}) copy-start(bf16[1,128,1024]{2,1,0:T(8,128)(2,1)} %param.19) | copy-start | bytes 786436
  7.2 65.2 %all-gather.2.cloned.1.call-start = ((), (), s32[]{:S(2)}) async-start(), calls=%async_computation.5 | async-start | bytes 8921088 | tf_op jit(solution)/shard_map/all_gather | solution.py:103
  14.6 9.6 %copy-start.7 = (s32[1,8,64]{2,1,0:T(8,128)S(1)}, s32[1,8,64]{2,1,0:T(8,128)}, u32[]{:S(2)}) copy-start(s32[1,8,64]{2,1,0:T(8,128)} %param.13) | copy-start | bytes 6148
  15.7 26.0 %all-to-all-start = ((bf16[8,32,1024]{2,1,0:T(8,128)(2,1)}), bf16[8,32,1024]{2,1,0:T(8,128)(2,1)S(1)}, u32[]{:S(2)}, u32[]{:S(2)}) async-start(bf16[8,32,1024]{2,1,0:T(8,128)(2,1)} %select_select_fusion), calls=%async_computation | async-start | bytes 1048576 | tf_op jit(solution)/shard_map/all_to_all | solution.py:137
  24.2 213.1 %reduce-scatter.2.cloned.1.call-start = ((), (), s32[]{:S(2)}) async-start(), calls=%async_computation.6 | async-start | bytes 8921088 | tf_op jit(solution)/shard_map/reduce_scatter | solution.py:163
  84.8 4.4 %copy-start.3 = (bf16[8,32,3,16,64]{4,1,0,3,2:T(8,128)(2,1)}, bf16[8,32,3,16,64]{4,1,0,3,2:T(8,128)(2,1)S(1)}, u32[]{:S(2)}) copy-start(bf16[8,32,3,16,64]{4,1,0,3,2:T(8,128)(2,1)S(1)} %copy.33) | copy-start | bytes 4718596
  87.7 1.5 copy-start.4
  89.2 1.0 copy-start.6
  95.9 2.5 copy-start.8
  136.3 1.2 copy-start.5
  239.0 17.6 %all-to-all-start.2 = ((bf16[8,4,4224]{2,1,0:T(4,128)(2,1)}), bf16[8,4,4224]{2,1,0:T(4,128)(2,1)S(1)}, u32[]{:S(2)}, u32[]{:S(2)}) async-start(bf16[8,4,4224]{2,1,0:T(4,128)(2,1)} %reshape.368), calls=%async_computation.3 | async-start | bytes 540672 | tf_op jit(solution)/shard_map/all_to_all | solution.py:164
  256.5 29.0 %all-to-all-start.1 = ((bf16[8,32,2048]{2,1,0:T(8,128)(2,1)}), bf16[8,32,2048]{2,1,0:T(8,128)(2,1)S(1)}, u32[]{:S(2)}, u32[]{:S(2)}) async-start(bf16[8,32,2048]{2,1,0:T(8,128)(2,1)} %broadcast_select_fusion), calls=%async_computation.1 | async-start | bytes 2097152 | tf_op jit(solution)/shard_map/all_to_all | solution.py:144
  286.4 13.9 %all-to-all-start.3 = ((bf16[8,4,4224]{2,1,0:T(4,128)(2,1)}), bf16[8,4,4224]{2,1,0:T(4,128)(2,1)S(1)}, u32[]{:S(2)}, u32[]{:S(2)}) async-start(bf16[8,4,4224]{2,1,0:T(4,128)(2,1)} %broadcast_in_dim.188), calls=%async_computation.4 | async-start | bytes 540672 | tf_op jit(solution)/shard_map/all_to_all | solution.py:168
  290.7 11.6 %copy-start.1 = (bf16[1,8,64,1024]{3,2,1,0:T(8,128)(2,1)S(1)}, bf16[1,8,64,1024]{3,2,1,0:T(8,128)(2,1)}, u32[]{:S(2)}) copy-start(bf16[1,8,64,1024]{3,2,1,0:T(8,128)(2,1)} %param.12) | copy-start | bytes 3145732
Sparse Core Ops, SparseCore 0:
  11.1 61.2 all-gather.1
  136.5 100.6 reduce-scatter.1

commit v5 on v4

--- a/solution.py
+++ b/solution.py
@@ -152,15 +152,22 @@
     came_grad = came[..., width:]
     layer_out = jnp.take(came_out.reshape(batches * MAXVIS, width), flat_rows, axis=0)
     d_packed = jnp.take(came_grad.reshape(batches * MAXVIS, width), flat_rows, axis=0)
-    partial = jnp.concatenate(
+    side = jnp.concatenate(
         [
-            grad_qkv_part.astype(jnp.bfloat16),
             grad_out_part.astype(jnp.bfloat16),
             jnp.broadcast_to(gain_products.astype(jnp.bfloat16)[:, None], (width, 128)),
         ],
         axis=1,
     )
-    summed = lax.psum_scatter(partial, "replica", scatter_dimension=0, tiled=True)
+    replicas = lax.axis_size("replica")
+    side = lax.all_to_all(
+        side.reshape(replicas, -1, side.shape[1]), "replica", split_axis=0, concat_axis=0, tiled=True
+    )
+    side = jnp.sum(side.astype(jnp.float32), axis=0).astype(jnp.bfloat16)
+    summed = lax.psum_scatter(
+        grad_qkv_part.astype(jnp.bfloat16), "replica", scatter_dimension=0, tiled=True
+    )
+    summed = jnp.concatenate([summed, side], axis=1)
     pieces = lax.all_to_all(
         summed.reshape(batches, -1, summed.shape[1]), "batch", split_axis=0, concat_axis=0, tiled=True
     )

time: 310 us -> 296 us (0.955)
  waiting for transfers between devices: 182 us -> 155 us
  starting transfers between devices: 22.5 us -> 28.5 us
  matrix products: 40.6 us -> 44.9 us
    reduce_scatter x1, waiting for transfers between devices: 95.8 us -> 42.4 us  [on_device(): lax.psum_scatter(grad_qkv_part.astype(jnp.bfloat16), 'replica', scatter_d...]
    all_to_all x0 -> x1, waiting for transfers between devices: none -> 26.3 us  [on_device(): lax.all_to_all(side.reshape(replicas, -1, side.shape[1]), 'replica', spli...]
    all_to_all x0 -> x1, starting transfers between devices: none -> 5.95 us  [on_device(): lax.all_to_all(side.reshape(replicas, -1, side.shape[1]), 'replica', spli...]
    dot_general x1, matrix products: 1.84 us -> 5.57 us  [left_product(): lax.dot_general(left, right, (((0,), (0,)), ((), ())), preferred_element_...]
  transfers between devices with their start and end apart: 6 -> 7, of which waited for: 6 -> 7; matrix products, arithmetic and copies ran while one was open for 6% -> 10% of each run, Pallas kernels for 0% -> 0%
where the time goes in v5:
time: 296 us; the launch traced here: 295 us
  waiting for transfers between devices  155 us (52%)
  matrix products  44.9 us (15%)
  local copies, waits for them, and re-layouts  33.5 us (11%)
  starting transfers between devices  28.5 us (10%)
  other arithmetic  18.7 us (6%)
  between operations  14.4 us (5%)
    reduce_scatter x1, waiting for transfers between devices, on_device(): lax.psum_scatter(grad_qkv_part.astype(jnp.bfloat16), 'replica', scatter_d...  42.4 us
    all_gather x1, waiting for transfers between devices, on_device(): lax.all_gather(jnp.concatenate([qkv_weight, out_weight, gain_block], axis...  30.2 us
    all_to_all x1, waiting for transfers between devices, on_device(): lax.all_to_all(side.reshape(replicas, -1, side.shape[1]), 'replica', spli...  26.3 us
    all_to_all x1, waiting for transfers between devices, on_device(): lax.all_to_all(jnp.take(jnp.concatenate([result, d_tokens], axis=-1), to_...  25.2 us
    all_to_all x1, waiting for transfers between devices, on_device(): lax.all_to_all(backward_rows, 'batch', split_axis=0, concat_axis=0, tiled...  13.6 us
    all_to_all x1, waiting for transfers between devices, on_device(): lax.all_to_all(summed.reshape(batches, -1, summed.shape[1]), 'batch', spl...  9.42 us
    all_to_all x1, starting transfers between devices, on_device(): lax.all_to_all(backward_rows, 'batch', split_axis=0, concat_axis=0, tiled...  8.47 us
    all_to_all x1, waiting for transfers between devices, on_device(): lax.all_to_all(jnp.broadcast_to(reduced[None], (batches,) + reduced.shape...  7.75 us
  transfers between devices with their start and end apart: 7, of which 7 were waited for; matrix products, arithmetic and copies ran while one was open for 10% of the time, Pallas kernels for 0%

profile of v5, /device:TPU:2, one launch (start us, length us, event | category | flops | bytes accessed | tf_op | source)
XLA Modules:
  0.0 294.8 jit_solution(14275897134374259080)
XLA Ops:
  7.2 0.8 broadcast_in_dim.172
  8.1 1.7 pad_maximum_fusion.2
  10.3 1.3 reduce.15
  11.6 1.3 reduce.14
  13.5 1.2 gather_fusion
  14.7 1.0 select_select_fusion
  15.7 8.5 %all-to-all-start = ((bf16[8,32,1024]{2,1,0:T(8,128)(2,1)}), bf16[8,32,1024]{2,1,0:T(8,128)(2,1)S(1)}, u32[]{:S(2)}, u32[]{:S(2)}) async-start(bf16[8,32,1024]{2,1,0:T(8,128)(2,1)} %select_select_fusion), calls=%async_computation | async-start | bytes 1048576 | tf_op jit(solution)/shard_map/all_to_all | solution.py:137
  24.3 2.8 gather_fusion.3
  28.1 13.6 %all-to-all-done = bf16[8,32,1024]{2,1,0:T(8,128)(2,1)S(1)} async-done(((bf16[8,32,1024]{2,1,0:T(8,128)(2,1)}), bf16[8,32,1024]{2,1,0:T(8,128)(2,1)S(1)}, u32[]{:S(2)}, u32[]{:S(2)}) %all-to-all-start) | async-done | bytes 524320 | tf_op jit(solution)/shard_map/all_to_all | solution.py:137
  42.3 30.2 %all-gather.2.cloned.1.call-done = bf16[1024,4224]{1,0:T(8,128)(2,1)} async-done(((bf16[32,4224]{1,0:T(8,128)(2,1)}), bf16[1024,4224]{1,0:T(8,128)(2,1)}) %all-gather.2.cloned.1.call-update) | async-done | bytes 8650768 | tf_op jit(solution)/shard_map/all_gather | solution.py:103
  72.4 1.1 convert_reduce_fusion.1
  73.5 1.3 fusion.38
  74.8 6.0 %fusion.6 = bf16[256,3072]{1,0:T(8,128)(2,1)} fusion(bf16[1024,4224]{1,0:T(8,128)(2,1)} %all-gather.2.cloned.1.call-done, f32[1024]{0:T(1024)S(1)} %convert_reduce_fusion.1, f32[256]{0:T(256)S(1)} %rsqrt.13, f32[256]{0:T(256)S(1)} %div.51, bf16[256,1024]{1,0:T(8,128)(2,1)S(1)} %gather_fusion.3, pred[256]{0:T(512)(128)(4,1)S(1)} %compare_and_fusion.4), kind=kOutput, calls=%fused_computation.14 | convolution fusion | flops 1612972032 | bytes 8395008 | tf_op jit(solution)/shard_map/dot_general | solution.py:30
  80.8 5.0 %reshape.372 = bf16[8,32,3,16,64]{4,3,2,1,0:T(8,128)(2,1)} reshape(bf16[256,3072]{1,0:T(8,128)(2,1)} %fusion.6) | data formatting | bytes 3145728 | tf_op jit(solution)/shard_map/reshape | solution.py:31
  85.8 2.7 copy.33
  88.5 2.9 slice.72
  91.4 1.3 fusion.32
  92.7 2.0 fusion.57
  94.8 3.9 %fusion.87 = (f32[16,8,32]{2,1,0:T(8,128)S(1)}, f32[16,8,32,32]{2,3,1,0:T(8,128)}) fusion(pred[8,32]{1,0:T(8,128)(4,1)S(1)} %iota_compare_fusion.3, bf16[3,16,8,32,64]{4,3,2,1,0:T(8,128)(2,1)} %bitcast.122), kind=kOutput, calls=%fused_computation.156 | convolution fusion | flops 17301536 | bytes 2638080 | tf_op jit(solution)/shard_map/sub | solution.py:36
  98.6 3.0 %fusion.25 = bf16[1,16,8,32,64]{4,3,2,1,0:T(8,128)(2,1)} fusion(bf16[16,8,32,64]{3,2,1,0:T(8,128)(2,1)S(1)} %fusion.32, f32[16,8,32,32]{2,3,1,0:T(8,128)} %get-tuple-element.34, f32[16,8,32]{2,1,0:T(8,128)S(1)} %get-tuple-element.33), kind=kOutput, calls=%fused_computation.31 | convolution fusion | flops 17301504 | bytes 1589248 | tf_op jit(solution)/shard_map/hgqk,hgqd->hgkd/dot_general | solution.py:49
  101.6 6.1 %fusion.29 = bf16[1,16,8,32,64]{4,3,2,1,0:T(8,128)(2,1)} fusion(f32[16,8,32,32]{2,3,1,0:T(8,128)} %fusion.57, bf16[3,16,8,32,64]{4,3,2,1,0:T(8,128)(2,1)} %bitcast.123, f32[16,8,32,32]{2,3,1,0:T(8,128)} %get-tuple-element.34, f32[16,8,32]{2,1,0:T(8,128)S(1)} %get-tuple-element.33), kind=kOutput, calls=%fused_computation.33 | convolution fusion | flops 17960992 | bytes 10092544 | tf_op jit(solution)/shard_map/hgqk,hgkd->hgqd/dot_general | solution.py:56
  107.8 5.9 %fusion.26 = bf16[1,16,8,32,64]{4,3,2,1,0:T(8,128)(2,1)} fusion(f32[16,8,32,32]{2,3,1,0:T(8,128)} %fusion.57, bf16[3,16,8,32,64]{4,3,2,1,0:T(8,128)(2,1)} %bitcast.124, f32[16,8,32,32]{2,3,1,0:T(8,128)} %get-tuple-element.34, f32[16,8,32]{2,1,0:T(8,128)S(1)} %get-tuple-element.33), kind=kOutput, calls=%fused_computation.32 | convolution fusion | flops 17960992 | bytes 10092544 | tf_op jit(solution)/shard_map/hgqk,hgqd->hgkd/dot_general | solution.py:59
  113.7 2.3 maximum_bitcast_fusion
  116.0 3.7 %copy.26 = bf16[8,32,3,16,64]{4,3,2,1,0:T(8,128)(2,1)} copy(bf16[8,32,3,16,64]{4,1,0,3,2:T(8,128)(2,1)S(1)} %maximum_bitcast_fusion) | data formatting | bytes 3145728 | tf_op jit(solution)/shard_map/transpose | solution.py:62
  119.7 4.2 %reshape.375 = bf16[256,3072]{1,0:T(8,128)(2,1)S(1)} reshape(bf16[8,32,3,16,64]{4,3,2,1,0:T(8,128)(2,1)} %copy.26) | data formatting | bytes 3145728 | tf_op jit(solution)/shard_map/reshape | solution.py:62
  124.0 5.6 %convolution_convert_fusion = bf16[1024,3072]{1,0:T(8,128)(2,1)} fusion(bf16[256,1024]{1,0:T(8,128)(2,1)} %bitcast.126, bf16[256,3072]{1,0:T(8,128)(2,1)S(1)} %reshape.375), kind=kOutput, calls=%fused_computation.8 | convolution fusion | flops 1613758464 | bytes 8388608 | tf_op jit(solution)/shard_map/dot_general | solution.py:92
  129.6 5.8 %fusion.50 = (bf16[1024]{0:T(1024)(128)(2,1)S(1)}, f32[256]{0:T(256)S(1)}, f32[256]{0:T(256)S(1)}, f32[256,1024]{1,0:T(8,128)}) fusion(f32[256]{0:T(256)S(1)} %rsqrt.13, f32[256]{0:T(256)S(1)} %div.51, bf16[256,1024]{1,0:T(8,128)(2,1)S(1)} %gather_fusion.3, pred[256]{0:T(512)(128)(4,1)S(1)} %compare_and_fusion.4, f32[1024]{0:T(1024)S(1)} %convert_reduce_fusion.1, ...), kind=kOutput, calls=%fused_computation.57 | convolution fusion | flops 1613232640 | bytes 9447680 | tf_op jit(solution)/shard_map/dot_general | solution.py:65
  135.5 2.5 convolution_convert_fusion.3
  137.9 1.0 copy-done.8
  138.9 0.8 bitcast_convert_fusion
  139.9 1.7 pad_maximum_fusion
  141.6 5.9 %all-to-all-start.2 = ((bf16[32,32,1152]{2,1,0:T(8,128)(2,1)}), bf16[32,32,1152]{2,1,0:T(8,128)(2,1)}, u32[]{:S(2)}, u32[]{:S(2)}) async-start(bf16[32,32,1152]{2,1,0:T(8,128)(2,1)} %pad_maximum_fusion), calls=%async_computation.3 | async-start | bytes 4718592 | tf_op jit(solution)/shard_map/all_to_all | solution.py:163
  148.4 1.0 copy-done.6
  149.4 2.1 fusion.33
  152.2 26.3 %all-to-all-done.2 = bf16[32,32,1152]{2,1,0:T(8,128)(2,1)} async-done(((bf16[32,32,1152]{2,1,0:T(8,128)(2,1)}), bf16[32,32,1152]{2,1,0:T(8,128)(2,1)}, u32[]{:S(2)}, u32[]{:S(2)}) %all-to-all-start.2) | async-done | bytes 2359328 | tf_op jit(solution)/shard_map/all_to_all | solution.py:163
  178.5 2.0 reduce_sum.147
  180.5 42.4 %reduce-scatter.2.cloned.1.call-done = bf16[32,3072]{1,0:T(8,128)(2,1)} async-done(((bf16[1024,3072]{1,0:T(8,128)(2,1)}), bf16[32,3072]{1,0:T(8,128)(2,1)}) %reduce-scatter.2.cloned.1.call-update) | async-done | bytes 196624 | tf_op jit(solution)/shard_map/reduce_scatter | solution.py:167
  222.9 0.9 pad_maximum_fusion.3
  224.6 7.0 %all-to-all-start.3 = ((bf16[8,4,4224]{2,1,0:T(4,128)(2,1)}), bf16[8,4,4224]{2,1,0:T(4,128)(2,1)S(1)}, u32[]{:S(2)}, u32[]{:S(2)}) async-start(bf16[8,4,4224]{2,1,0:T(4,128)(2,1)} %reshape.379), calls=%async_computation.4 | async-start | bytes 540672 | tf_op jit(solution)/shard_map/all_to_all | solution.py:171
  231.6 1.2 broadcast_select_fusion
  232.8 9.4 %all-to-all-done.3 = bf16[8,4,4224]{2,1,0:T(4,128)(2,1)S(1)} async-done(((bf16[8,4,4224]{2,1,0:T(4,128)(2,1)}), bf16[8,4,4224]{2,1,0:T(4,128)(2,1)S(1)}, u32[]{:S(2)}, u32[]{:S(2)}) %all-to-all-start.3) | async-done | bytes 270368 | tf_op jit(solution)/shard_map/all_to_all | solution.py:171
  242.2 3.6 %all-to-all-start.1 = ((bf16[8,32,2048]{2,1,0:T(8,128)(2,1)}), bf16[8,32,2048]{2,1,0:T(8,128)(2,1)S(1)}, u32[]{:S(2)}, u32[]{:S(2)}) async-start(bf16[8,32,2048]{2,1,0:T(8,128)(2,1)} %broadcast_select_fusion), calls=%async_computation.1 | async-start | bytes 2097152 | tf_op jit(solution)/shard_map/all_to_all | solution.py:144
  246.0 25.2 %all-to-all-done.1 = bf16[8,32,2048]{2,1,0:T(8,128)(2,1)S(1)} async-done(((bf16[8,32,2048]{2,1,0:T(8,128)(2,1)}), bf16[8,32,2048]{2,1,0:T(8,128)(2,1)S(1)}, u32[]{:S(2)}, u32[]{:S(2)}) %all-to-all-start.1) | async-done | bytes 1048608 | tf_op jit(solution)/shard_map/all_to_all | solution.py:144
  272.0 3.4 %all-to-all-start.4 = ((bf16[8,4,4224]{2,1,0:T(4,128)(2,1)}), bf16[8,4,4224]{2,1,0:T(4,128)(2,1)S(1)}, u32[]{:S(2)}, u32[]{:S(2)}) async-start(bf16[8,4,4224]{2,1,0:T(4,128)(2,1)} %broadcast_in_dim.188), calls=%async_computation.5 | async-start | bytes 540672 | tf_op jit(solution)/shard_map/all_to_all | solution.py:175
  275.5 0.9 gather_fusion.5
  276.4 0.9 gather_fusion.4
  277.2 0.9 select_bitcast_fusion
  278.2 7.8 %all-to-all-done.4 = bf16[8,4,4224]{2,1,0:T(4,128)(2,1)S(1)} async-done(((bf16[8,4,4224]{2,1,0:T(4,128)(2,1)}), bf16[8,4,4224]{2,1,0:T(4,128)(2,1)S(1)}, u32[]{:S(2)}, u32[]{:S(2)}) %all-to-all-start.4) | async-done | bytes 270368 | tf_op jit(solution)/shard_map/all_to_all | solution.py:175
  (75 shorter events, 8.6 us)
Async XLA Ops:
  7.2 17.2 %copy-start = (bf16[1,8,64,1024]{3,2,1,0:T(8,128)(2,1)S(1)}, bf16[1,8,64,1024]{3,2,1,0:T(8,128)(2,1)}, u32[]{:S(2)}) copy-start(bf16[1,8,64,1024]{3,2,1,0:T(8,128)(2,1)} %param.12) | copy-start | bytes 3145732
  7.2 6.3 %copy-start.1 = (bf16[1,128,1024]{2,1,0:T(8,128)(2,1)S(1)}, bf16[1,128,1024]{2,1,0:T(8,128)(2,1)}, u32[]{:S(2)}) copy-start(bf16[1,128,1024]{2,1,0:T(8,128)(2,1)} %param.19) | copy-start | bytes 786436
  7.2 65.2 %all-gather.2.cloned.1.call-start = ((), (), s32[]{:S(2)}) async-start(), calls=%async_computation.6 | async-start | bytes 8921088 | tf_op jit(solution)/shard_map/all_gather | solution.py:103
  14.6 9.6 %copy-start.10 = (s32[1,8,64]{2,1,0:T(8,128)S(1)}, s32[1,8,64]{2,1,0:T(8,128)}, u32[]{:S(2)}) copy-start(s32[1,8,64]{2,1,0:T(8,128)} %param.13) | copy-start | bytes 6148
  15.7 26.0 %all-to-all-start = ((bf16[8,32,1024]{2,1,0:T(8,128)(2,1)}), bf16[8,32,1024]{2,1,0:T(8,128)(2,1)S(1)}, u32[]{:S(2)}, u32[]{:S(2)}) async-start(bf16[8,32,1024]{2,1,0:T(8,128)(2,1)} %select_select_fusion), calls=%async_computation | async-start | bytes 1048576 | tf_op jit(solution)/shard_map/all_to_all | solution.py:137
  24.2 198.7 %reduce-scatter.2.cloned.1.call-start = ((), (), s32[]{:S(2)}) async-start(), calls=%async_computation.7 | async-start | bytes 6488064 | tf_op jit(solution)/shard_map/reduce_scatter | solution.py:167
  42.2 49.1 %copy-start.3 = (bf16[8,32,1024]{2,1,0:T(8,128)(2,1)}, bf16[8,32,1024]{2,1,0:T(8,128)(2,1)S(1)}, u32[]{:S(2)}) copy-start(bf16[8,32,1024]{2,1,0:T(8,128)(2,1)S(1)} %gather_fusion.1) | copy-start | bytes 1572868
  88.5 4.2 %copy-start.2 = (bf16[8,32,3,16,64]{4,1,0,3,2:T(8,128)(2,1)}, bf16[8,32,3,16,64]{4,1,0,3,2:T(8,128)(2,1)S(1)}, u32[]{:S(2)}) copy-start(bf16[8,32,3,16,64]{4,1,0,3,2:T(8,128)(2,1)S(1)} %copy.33) | copy-start | bytes 4718596
  91.4 1.3 copy-start.5
  107.8 5.9 %copy-start.9 = (bf16[1,16,8,32,64]{4,3,2,1,0:T(8,128)(2,1)S(1)}, bf16[1,16,8,32,64]{4,3,2,1,0:T(8,128)(2,1)}, u32[]{:S(2)}) copy-start(bf16[1,16,8,32,64]{4,3,2,1,0:T(8,128)(2,1)} %fusion.25) | copy-start | bytes 1572868
  135.5 3.5 %copy-start.4 = (bf16[8,32,1024]{2,1,0:T(8,128)(2,1)S(1)}, bf16[8,32,1024]{2,1,0:T(8,128)(2,1)}, u32[]{:S(2)}) copy-start(bf16[8,32,1024]{2,1,0:T(8,128)(2,1)} %copy-done.3) | copy-start | bytes 1572868
  137.9 1.0 copy-start.8
  141.6 6.3 %copy-start.7 = (f32[256,1024]{1,0:T(8,128)S(1)}, f32[256,1024]{1,0:T(8,128)}, u32[]{:S(2)}) copy-start(f32[256,1024]{1,0:T(8,128)} %get-tuple-element.35) | copy-start | bytes 3145732
  141.6 36.9 %all-to-all-start.2 = ((bf16[32,32,1152]{2,1,0:T(8,128)(2,1)}), bf16[32,32,1152]{2,1,0:T(8,128)(2,1)}, u32[]{:S(2)}, u32[]{:S(2)}) async-start(bf16[32,32,1152]{2,1,0:T(8,128)(2,1)} %pad_maximum_fusion), calls=%async_computation.3 | async-start | bytes 4718592 | tf_op jit(solution)/shard_map/all_to_all | solution.py:163
  147.7 1.7 copy-start.6
  224.6 17.6 %all-to-all-start.3 = ((bf16[8,4,4224]{2,1,0:T(4,128)(2,1)}), bf16[8,4,4224]{2,1,0:T(4,128)(2,1)S(1)}, u32[]{:S(2)}, u32[]{:S(2)}) async-start(bf16[8,4,4224]{2,1,0:T(4,128)(2,1)} %reshape.379), calls=%async_computation.4 | async-start | bytes 540672 | tf_op jit(solution)/shard_map/all_to_all | solution.py:171
  242.2 29.0 %all-to-all-start.1 = ((bf16[8,32,2048]{2,1,0:T(8,128)(2,1)}), bf16[8,32,2048]{2,1,0:T(8,128)(2,1)S(1)}, u32[]{:S(2)}, u32[]{:S(2)}) async-start(bf16[8,32,2048]{2,1,0:T(8,128)(2,1)} %broadcast_select_fusion), calls=%async_computation.1 | async-start | bytes 2097152 | tf_op jit(solution)/shard_map/all_to_all | solution.py:144
  272.0 13.9 %all-to-all-start.4 = ((bf16[8,4,4224]{2,1,0:T(4,128)(2,1)}), bf16[8,4,4224]{2,1,0:T(4,128)(2,1)S(1)}, u32[]{:S(2)}, u32[]{:S(2)}) async-start(bf16[8,4,4224]{2,1,0:T(4,128)(2,1)} %broadcast_in_dim.188), calls=%async_computation.5 | async-start | bytes 540672 | tf_op jit(solution)/shard_map/all_to_all | solution.py:175
Sparse Core Ops, SparseCore 0:
  11.1 61.2 all-gather.1
  129.7 93.1 reduce-scatter.1

commit v6 on v4

--- a/solution.py
+++ b/solution.py
@@ -153,14 +153,21 @@
     layer_out = jnp.take(came_out.reshape(batches * MAXVIS, width), flat_rows, axis=0)
     d_packed = jnp.take(came_grad.reshape(batches * MAXVIS, width), flat_rows, axis=0)
     partial = jnp.concatenate(
-        [
-            grad_qkv_part.astype(jnp.bfloat16),
-            grad_out_part.astype(jnp.bfloat16),
-            jnp.broadcast_to(gain_products.astype(jnp.bfloat16)[:, None], (width, 128)),
-        ],
-        axis=1,
+        [grad_qkv_part.astype(jnp.bfloat16), grad_out_part.astype(jnp.bfloat16)], axis=1
     )
     summed = lax.psum_scatter(partial, "replica", scatter_dimension=0, tiled=True)
+    replicas = lax.axis_size("replica")
+    gain_sum = lax.all_to_all(
+        gain_products.astype(jnp.bfloat16).reshape(replicas, -1),
+        "replica",
+        split_axis=0,
+        concat_axis=0,
+        tiled=True,
+    )
+    gain_sum = jnp.sum(gain_sum.astype(jnp.float32), axis=0).astype(jnp.bfloat16)
+    summed = jnp.concatenate(
+        [summed, jnp.broadcast_to(gain_sum[:, None], (gain_sum.shape[0], 128))], axis=1
+    )
     pieces = lax.all_to_all(
         summed.reshape(batches, -1, summed.shape[1]), "batch", split_axis=0, concat_axis=0, tiled=True
     )

time: 310 us -> 312 us (level)
  waiting for transfers between devices: 182 us -> 168 us
  other arithmetic: 16.7 us -> 22.9 us
  starting transfers between devices: 22.5 us -> 28.3 us
  matrix products: 40.6 us -> 45.1 us
    reduce_scatter x1, waiting for transfers between devices: 95.8 us -> 81.1 us  [on_device(): lax.psum_scatter(partial, 'replica', scatter_dimension=0, tiled=True)]
    all_to_all x0 -> x1, starting transfers between devices: none -> 5.77 us  [on_device(): lax.all_to_all(gain_products.astype(jnp.bfloat16).reshape(replicas, -1),...]
    concatenate x1, other arithmetic: 3.67 us -> 7.58 us  [on_device(): jnp.concatenate([grad_qkv_part.astype(jnp.bfloat16), grad_out_part.astype...]
  transfers between devices with their start and end apart: 6 -> 7, of which waited for: 6 -> 7; matrix products, arithmetic and copies ran while one was open for 6% -> 8% of each run, Pallas kernels for 0% -> 0%
where the time goes in v6:
time: 312 us; the launch traced here: 311 us
  waiting for transfers between devices  168 us (54%)
  matrix products  45.1 us (14%)
  local copies, waits for them, and re-layouts  31.7 us (10%)
  starting transfers between devices  28.3 us (9%)
  other arithmetic  22.9 us (7%)
  between operations  14.4 us (5%)
    reduce_scatter x1, waiting for transfers between devices, on_device(): lax.psum_scatter(partial, 'replica', scatter_dimension=0, tiled=True)  81.1 us
    all_gather x1, waiting for transfers between devices, on_device(): lax.all_gather(jnp.concatenate([qkv_weight, out_weight, gain_block], axis...  30.2 us
    all_to_all x1, waiting for transfers between devices, on_device(): lax.all_to_all(jnp.take(jnp.concatenate([result, d_tokens], axis=-1), to_...  25.2 us
    all_to_all x1, waiting for transfers between devices, on_device(): lax.all_to_all(backward_rows, 'batch', split_axis=0, concat_axis=0, tiled...  13.6 us
    all_to_all x1, waiting for transfers between devices, on_device(): lax.all_to_all(summed.reshape(batches, -1, summed.shape[1]), 'batch', spl...  9.42 us
    all_to_all x1, starting transfers between devices, on_device(): lax.all_to_all(backward_rows, 'batch', split_axis=0, concat_axis=0, tiled...  8.47 us
    all_to_all x1, waiting for transfers between devices, on_device(): lax.all_to_all(jnp.broadcast_to(reduced[None], (batches,) + reduced.shape...  7.76 us
    concatenate x1, other arithmetic, on_device(): jnp.concatenate([grad_qkv_part.astype(jnp.bfloat16), grad_out_part.astype...  7.58 us
  transfers between devices with their start and end apart: 7, of which 7 were waited for; matrix products, arithmetic and copies ran while one was open for 8% of the time, Pallas kernels for 0%

profile of v6, /device:TPU:2, one launch (start us, length us, event | category | flops | bytes accessed | tf_op | source)
XLA Modules:
  0.0 310.7 jit_solution(9063204625028089788)
XLA Ops:
  7.2 0.8 broadcast_in_dim.172
  8.1 1.7 pad_maximum_fusion.2
  10.3 1.3 reduce.16
  11.6 1.3 reduce.15
  13.5 1.2 gather_fusion
  14.7 1.0 select_select_fusion
  15.7 8.5 %all-to-all-start = ((bf16[8,32,1024]{2,1,0:T(8,128)(2,1)}), bf16[8,32,1024]{2,1,0:T(8,128)(2,1)S(1)}, u32[]{:S(2)}, u32[]{:S(2)}) async-start(bf16[8,32,1024]{2,1,0:T(8,128)(2,1)} %select_select_fusion), calls=%async_computation | async-start | bytes 1048576 | tf_op jit(solution)/shard_map/all_to_all | solution.py:137
  24.3 2.8 gather_fusion.3
  28.1 13.6 %all-to-all-done = bf16[8,32,1024]{2,1,0:T(8,128)(2,1)S(1)} async-done(((bf16[8,32,1024]{2,1,0:T(8,128)(2,1)}), bf16[8,32,1024]{2,1,0:T(8,128)(2,1)S(1)}, u32[]{:S(2)}, u32[]{:S(2)}) %all-to-all-start) | async-done | bytes 524320 | tf_op jit(solution)/shard_map/all_to_all | solution.py:137
  42.2 30.2 %all-gather.2.cloned.1.call-done = bf16[1024,4224]{1,0:T(8,128)(2,1)} async-done(((bf16[32,4224]{1,0:T(8,128)(2,1)}), bf16[1024,4224]{1,0:T(8,128)(2,1)}) %all-gather.2.cloned.1.call-update) | async-done | bytes 8650768 | tf_op jit(solution)/shard_map/all_gather | solution.py:103
  72.4 1.1 convert_reduce_fusion.1
  73.8 4.7 %fusion.6 = bf16[256,3072]{1,0:T(8,128)(2,1)S(1)} fusion(bf16[1024,4224]{1,0:T(8,128)(2,1)} %all-gather.2.cloned.1.call-done, f32[1024]{0:T(1024)S(1)} %convert_reduce_fusion.1, f32[256]{0:T(256)S(1)} %rsqrt.13, f32[256]{0:T(256)S(1)} %div.51, bf16[256,1024]{1,0:T(8,128)(2,1)S(1)} %gather_fusion.3, pred[256]{0:T(512)(128)(4,1)S(1)} %compare_and_fusion.4), kind=kOutput, calls=%fused_computation.15 | convolution fusion | flops 1612972032 | bytes 8395008 | tf_op jit(solution)/shard_map/dot_general | solution.py:30
  78.5 3.6 %reshape.374 = bf16[8,32,3,16,64]{4,3,2,1,0:T(8,128)(2,1)} reshape(bf16[256,3072]{1,0:T(8,128)(2,1)S(1)} %fusion.6) | data formatting | bytes 3145728 | tf_op jit(solution)/shard_map/reshape | solution.py:31
  82.1 2.7 copy.40
  84.8 2.9 slice.72
  87.7 1.3 fusion.32
  89.0 1.0 copy-done.6
  90.0 2.0 fusion.57
  92.0 3.9 %fusion.87 = (f32[16,8,32]{2,1,0:T(8,128)S(1)}, f32[16,8,32,32]{2,3,1,0:T(8,128)}) fusion(pred[8,32]{1,0:T(8,128)(4,1)S(1)} %iota_compare_fusion.3, bf16[3,16,8,32,64]{4,3,2,1,0:T(8,128)(2,1)} %bitcast.122), kind=kOutput, calls=%fused_computation.156 | convolution fusion | flops 17301536 | bytes 2638080 | tf_op jit(solution)/shard_map/sub | solution.py:36
  96.0 2.4 fusion.25
  98.5 2.8 convolution_convert_fusion.3
  101.3 5.9 %fusion.29 = bf16[1,16,8,32,64]{4,3,2,1,0:T(8,128)(2,1)} fusion(f32[16,8,32,32]{2,3,1,0:T(8,128)} %fusion.57, bf16[3,16,8,32,64]{4,3,2,1,0:T(8,128)(2,1)} %bitcast.124, f32[16,8,32,32]{2,3,1,0:T(8,128)} %get-tuple-element.34, f32[16,8,32]{2,1,0:T(8,128)S(1)} %get-tuple-element.33), kind=kOutput, calls=%fused_computation.33 | convolution fusion | flops 17960992 | bytes 10092544 | tf_op jit(solution)/shard_map/hgqk,hgkd->hgqd/dot_general | solution.py:56
  107.2 5.8 %fusion.26 = bf16[1,16,8,32,64]{4,3,2,1,0:T(8,128)(2,1)} fusion(f32[16,8,32,32]{2,3,1,0:T(8,128)} %fusion.57, bf16[3,16,8,32,64]{4,3,2,1,0:T(8,128)(2,1)} %bitcast.125, f32[16,8,32,32]{2,3,1,0:T(8,128)} %get-tuple-element.34, f32[16,8,32]{2,1,0:T(8,128)S(1)} %get-tuple-element.33), kind=kOutput, calls=%fused_computation.32 | convolution fusion | flops 17960992 | bytes 10092544 | tf_op jit(solution)/shard_map/hgqk,hgqd->hgkd/dot_general | solution.py:59
  113.0 2.3 maximum_bitcast_fusion
  115.3 3.7 %copy.32 = bf16[8,32,3,16,64]{4,3,2,1,0:T(8,128)(2,1)} copy(bf16[8,32,3,16,64]{4,1,0,3,2:T(8,128)(2,1)S(1)} %maximum_bitcast_fusion) | data formatting | bytes 3145728 | tf_op jit(solution)/shard_map/transpose | solution.py:62
  119.1 4.2 %reshape.377 = bf16[256,3072]{1,0:T(8,128)(2,1)S(1)} reshape(bf16[8,32,3,16,64]{4,3,2,1,0:T(8,128)(2,1)} %copy.32) | data formatting | bytes 3145728 | tf_op jit(solution)/shard_map/reshape | solution.py:62
  123.3 3.4 %bitcast_convert_fusion = bf16[16,64,1024]{2,1,0:T(8,128)(2,1)} fusion(bf16[16,8,32,64]{3,2,1,0:T(8,128)(2,1)} %convolution_convert_fusion.3, bf16[8,32,1024]{2,1,0:T(8,128)(2,1)S(1)} %gather_fusion.1, pred[8]{0:T(512)(128)(4,1)S(1)} %get-tuple-element.27), kind=kOutput, calls=%fused_computation.14 | convolution fusion | flops 538181632 | bytes 3145736 | tf_op jit(solution)/shard_map/hgqd,gqe->hde/dot_general | solution.py:79
  126.7 4.5 %convolution_convert_fusion = bf16[1024,3072]{1,0:T(8,128)(2,1)} fusion(bf16[256,1024]{1,0:T(8,128)(2,1)S(1)} %bitcast.126, bf16[256,3072]{1,0:T(8,128)(2,1)S(1)} %reshape.377), kind=kOutput, calls=%fused_computation.9 | convolution fusion | flops 1613758464 | bytes 8388608 | tf_op jit(solution)/shard_map/dot_general | solution.py:92
  131.2 7.6 %pad_maximum_fusion = bf16[1024,4096]{1,0:T(8,128)(2,1)} fusion(bf16[1024,1024]{1,0:T(8,128)(2,1)} %bitcast.120, bf16[1024,3072]{1,0:T(8,128)(2,1)} %convolution_convert_fusion), kind=kLoop, calls=%fused_computation.8 | loop fusion | flops 16777216 | bytes 16777216 | tf_op jit(solution)/shard_map/concatenate | solution.py:155
  139.1 5.9 %fusion.50 = (bf16[1024]{0:T(1024)(128)(2,1)S(1)}, f32[256]{0:T(256)S(1)}, f32[256]{0:T(256)S(1)}, f32[256,1024]{1,0:T(8,128)}) fusion(f32[256]{0:T(256)S(1)} %rsqrt.13, f32[256]{0:T(256)S(1)} %div.51, bf16[256,1024]{1,0:T(8,128)(2,1)S(1)} %gather_fusion.3, pred[256]{0:T(512)(128)(4,1)S(1)} %compare_and_fusion.4, f32[1024]{0:T(1024)S(1)} %convert_reduce_fusion.1, ...), kind=kOutput, calls=%fused_computation.57 | convolution fusion | flops 1613232640 | bytes 9447680 | tf_op jit(solution)/shard_map/dot_general | solution.py:65
  145.6 5.8 %all-to-all-start.2 = ((bf16[32,1,32]{2,1,0:T(2,128)(2,1)}), bf16[32,1,32]{2,1,0:T(2,128)(2,1)S(1)}, u32[]{:S(2)}, u32[]{:S(2)}) async-start(bf16[32,1,32]{2,1,0:T(2,128)(2,1)} %convert_element_type.141), calls=%async_computation.3 | async-start | bytes 32768 | tf_op jit(solution)/shard_map/all_to_all | solution.py:160
  151.4 1.8 fusion.49
  153.2 2.5 fusion.33
  156.4 1.1 all-to-all-done.2
  157.6 81.1 %reduce-scatter.2.cloned.1.call-done = bf16[32,4096]{1,0:T(8,128)(2,1)} async-done(((bf16[1024,4096]{1,0:T(8,128)(2,1)}), bf16[32,4096]{1,0:T(8,128)(2,1)}) %reduce-scatter.2.cloned.1.call-update) | async-done | bytes 262160 | tf_op jit(solution)/shard_map/reduce_scatter | solution.py:158
  238.7 1.0 pad_maximum_fusion.3
  239.7 0.8 reshape.381
  240.5 7.0 %all-to-all-start.3 = ((bf16[8,4,4224]{2,1,0:T(4,128)(2,1)}), bf16[8,4,4224]{2,1,0:T(4,128)(2,1)S(1)}, u32[]{:S(2)}, u32[]{:S(2)}) async-start(bf16[8,4,4224]{2,1,0:T(4,128)(2,1)} %reshape.381), calls=%async_computation.4 | async-start | bytes 540672 | tf_op jit(solution)/shard_map/all_to_all | solution.py:171
  247.5 1.2 broadcast_select_fusion
  248.6 9.4 %all-to-all-done.3 = bf16[8,4,4224]{2,1,0:T(4,128)(2,1)S(1)} async-done(((bf16[8,4,4224]{2,1,0:T(4,128)(2,1)}), bf16[8,4,4224]{2,1,0:T(4,128)(2,1)S(1)}, u32[]{:S(2)}, u32[]{:S(2)}) %all-to-all-start.3) | async-done | bytes 270368 | tf_op jit(solution)/shard_map/all_to_all | solution.py:171
  258.1 3.6 %all-to-all-start.1 = ((bf16[8,32,2048]{2,1,0:T(8,128)(2,1)}), bf16[8,32,2048]{2,1,0:T(8,128)(2,1)S(1)}, u32[]{:S(2)}, u32[]{:S(2)}) async-start(bf16[8,32,2048]{2,1,0:T(8,128)(2,1)} %broadcast_select_fusion), calls=%async_computation.1 | async-start | bytes 2097152 | tf_op jit(solution)/shard_map/all_to_all | solution.py:144
  261.9 25.2 %all-to-all-done.1 = bf16[8,32,2048]{2,1,0:T(8,128)(2,1)S(1)} async-done(((bf16[8,32,2048]{2,1,0:T(8,128)(2,1)}), bf16[8,32,2048]{2,1,0:T(8,128)(2,1)S(1)}, u32[]{:S(2)}, u32[]{:S(2)}) %all-to-all-start.1) | async-done | bytes 1048608 | tf_op jit(solution)/shard_map/all_to_all | solution.py:144
  287.1 0.8 broadcast_in_dim.188
  287.9 3.4 %all-to-all-start.4 = ((bf16[8,4,4224]{2,1,0:T(4,128)(2,1)}), bf16[8,4,4224]{2,1,0:T(4,128)(2,1)S(1)}, u32[]{:S(2)}, u32[]{:S(2)}) async-start(bf16[8,4,4224]{2,1,0:T(4,128)(2,1)} %broadcast_in_dim.188), calls=%async_computation.5 | async-start | bytes 540672 | tf_op jit(solution)/shard_map/all_to_all | solution.py:175
  291.4 0.9 gather_fusion.5
  292.3 0.9 gather_fusion.4
  293.1 0.9 select_bitcast_fusion
  294.0 7.8 %all-to-all-done.4 = bf16[8,4,4224]{2,1,0:T(4,128)(2,1)S(1)} async-done(((bf16[8,4,4224]{2,1,0:T(4,128)(2,1)}), bf16[8,4,4224]{2,1,0:T(4,128)(2,1)S(1)}, u32[]{:S(2)}, u32[]{:S(2)}) %all-to-all-start.4) | async-done | bytes 270368 | tf_op jit(solution)/shard_map/all_to_all | solution.py:175
  (71 shorter events, 7.4 us)
Async XLA Ops:
  7.2 17.2 %copy-start = (bf16[1,8,64,1024]{3,2,1,0:T(8,128)(2,1)S(1)}, bf16[1,8,64,1024]{3,2,1,0:T(8,128)(2,1)}, u32[]{:S(2)}) copy-start(bf16[1,8,64,1024]{3,2,1,0:T(8,128)(2,1)} %param.12) | copy-start | bytes 3145732
  7.2 6.3 %copy-start.2 = (bf16[1,128,1024]{2,1,0:T(8,128)(2,1)S(1)}, bf16[1,128,1024]{2,1,0:T(8,128)(2,1)}, u32[]{:S(2)}) copy-start(bf16[1,128,1024]{2,1,0:T(8,128)(2,1)} %param.19) | copy-start | bytes 786436
  7.2 65.2 %all-gather.2.cloned.1.call-start = ((), (), s32[]{:S(2)}) async-start(), calls=%async_computation.6 | async-start | bytes 8921088 | tf_op jit(solution)/shard_map/all_gather | solution.py:103
  14.6 9.6 %copy-start.7 = (s32[1,8,64]{2,1,0:T(8,128)S(1)}, s32[1,8,64]{2,1,0:T(8,128)}, u32[]{:S(2)}) copy-start(s32[1,8,64]{2,1,0:T(8,128)} %param.13) | copy-start | bytes 6148
  15.7 26.0 %all-to-all-start = ((bf16[8,32,1024]{2,1,0:T(8,128)(2,1)}), bf16[8,32,1024]{2,1,0:T(8,128)(2,1)S(1)}, u32[]{:S(2)}, u32[]{:S(2)}) async-start(bf16[8,32,1024]{2,1,0:T(8,128)(2,1)} %select_select_fusion), calls=%async_computation | async-start | bytes 1048576 | tf_op jit(solution)/shard_map/all_to_all | solution.py:137
  24.2 214.5 %reduce-scatter.2.cloned.1.call-start = ((), (), s32[]{:S(2)}) async-start(), calls=%async_computation.7 | async-start | bytes 8650752 | tf_op jit(solution)/shard_map/reduce_scatter | solution.py:158
  84.8 4.3 %copy-start.3 = (bf16[8,32,3,16,64]{4,1,0,3,2:T(8,128)(2,1)}, bf16[8,32,3,16,64]{4,1,0,3,2:T(8,128)(2,1)S(1)}, u32[]{:S(2)}) copy-start(bf16[8,32,3,16,64]{4,1,0,3,2:T(8,128)(2,1)S(1)} %copy.40) | copy-start | bytes 4718596
  87.7 1.3 copy-start.4
  89.0 1.0 copy-start.6
  96.0 2.5 copy-start.8
  144.9 8.3 %copy-start.5 = (bf16[16,8,32,64]{3,2,1,0:T(8,128)(2,1)S(1)}, bf16[16,8,32,64]{3,2,1,0:T(8,128)(2,1)}, u32[]{:S(2)}) copy-start(bf16[16,8,32,64]{3,2,1,0:T(8,128)(2,1)} %convolution_convert_fusion.3) | copy-start | bytes 1572868
  145.6 11.9 %all-to-all-start.2 = ((bf16[32,1,32]{2,1,0:T(2,128)(2,1)}), bf16[32,1,32]{2,1,0:T(2,128)(2,1)S(1)}, u32[]{:S(2)}, u32[]{:S(2)}) async-start(bf16[32,1,32]{2,1,0:T(2,128)(2,1)} %convert_element_type.141), calls=%async_computation.3 | async-start | bytes 32768 | tf_op jit(solution)/shard_map/all_to_all | solution.py:160
  240.5 17.6 %all-to-all-start.3 = ((bf16[8,4,4224]{2,1,0:T(4,128)(2,1)}), bf16[8,4,4224]{2,1,0:T(4,128)(2,1)S(1)}, u32[]{:S(2)}, u32[]{:S(2)}) async-start(bf16[8,4,4224]{2,1,0:T(4,128)(2,1)} %reshape.381), calls=%async_computation.4 | async-start | bytes 540672 | tf_op jit(solution)/shard_map/all_to_all | solution.py:171
  258.1 29.1 %all-to-all-start.1 = ((bf16[8,32,2048]{2,1,0:T(8,128)(2,1)}), bf16[8,32,2048]{2,1,0:T(8,128)(2,1)S(1)}, u32[]{:S(2)}, u32[]{:S(2)}) async-start(bf16[8,32,2048]{2,1,0:T(8,128)(2,1)} %broadcast_select_fusion), calls=%async_computation.1 | async-start | bytes 2097152 | tf_op jit(solution)/shard_map/all_to_all | solution.py:144
  287.9 13.9 %all-to-all-start.4 = ((bf16[8,4,4224]{2,1,0:T(4,128)(2,1)}), bf16[8,4,4224]{2,1,0:T(4,128)(2,1)S(1)}, u32[]{:S(2)}, u32[]{:S(2)}) async-start(bf16[8,4,4224]{2,1,0:T(4,128)(2,1)} %broadcast_in_dim.188), calls=%async_computation.5 | async-start | bytes 540672 | tf_op jit(solution)/shard_map/all_to_all | solution.py:175
  292.3 11.6 %copy-start.1 = (bf16[1,8,64,1024]{3,2,1,0:T(8,128)(2,1)S(1)}, bf16[1,8,64,1024]{3,2,1,0:T(8,128)(2,1)}, u32[]{:S(2)}) copy-start(bf16[1,8,64,1024]{3,2,1,0:T(8,128)(2,1)} %param.12) | copy-start | bytes 3145732
Sparse Core Ops, SparseCore 0:
  11.1 61.2 all-gather.1
  138.9 99.7 reduce-scatter.1

commit v7 on v4

--- a/solution.py
+++ b/solution.py
@@ -39,13 +39,13 @@
     context = jnp.einsum("hgqk,hgkd->hgqd", weights, values, preferred_element_type=f32).astype(
         jnp.bfloat16
     )
-    wout3 = wout.reshape(HEADS, head_dim, width)
-    projected = jnp.einsum("hgqd,hde->gqe", context, wout3, preferred_element_type=f32)
-    result = (x32 + projected.reshape(rows, width)).astype(jnp.bfloat16)
-    up3 = upward.reshape(groups, length, width)
-    d_context = jnp.einsum("gqe,hde->hgqd", up3, wout3, preferred_element_type=f32).astype(
-        jnp.bfloat16
-    )
+    context_rows = jnp.transpose(context, (1, 2, 0, 3)).reshape(rows, width)
+    result = (x32 + jnp.dot(context_rows, wout, preferred_element_type=f32)).astype(jnp.bfloat16)
+    up_rows = upward.reshape(rows, width)
+    d_context = lax.dot_general(
+        up_rows, wout, (((1,), (1,)), ((), ())), preferred_element_type=f32
+    ).astype(jnp.bfloat16)
+    d_context = jnp.transpose(d_context.reshape(groups, length, HEADS, head_dim), (2, 0, 1, 3))
     d_values = jnp.einsum(
         "hgqk,hgqd->hgkd", weights, d_context, preferred_element_type=f32
     ).astype(jnp.bfloat16)
@@ -73,12 +73,9 @@
         - standardized_rows
         * jnp.mean(normalized_gradient * standardized_rows, axis=1, keepdims=True)
     )
-    up_rows = upward.reshape(rows, width)
     d_tokens = (up_rows.astype(jnp.float32) + input_gradient).astype(jnp.bfloat16)
     grad_qkv_part = left_product(layernorm_output, d_qkv)
-    grad_out_part = jnp.einsum(
-        "hgqd,gqe->hde", context, up3, preferred_element_type=f32
-    ).reshape(width, width)
+    grad_out_part = left_product(context_rows, up_rows)
     return (
         result.reshape(tokens.shape),
         d_tokens.reshape(tokens.shape),

time: 310 us -> 314 us (1.013)
  no operation moved by 1% of the time
where the time goes in v7:
time: 314 us; the launch traced here: 313 us
  waiting for transfers between devices  181 us (58%)
  matrix products  42.6 us (14%)
  local copies, waits for them, and re-layouts  34.8 us (11%)
  starting transfers between devices  22.5 us (7%)
  other arithmetic  18.2 us (6%)
  between operations  14.4 us (5%)
    reduce_scatter x1, waiting for transfers between devices, on_device(): lax.psum_scatter(partial, 'replica', scatter_dimension=0, tiled=True)  96.1 us
    all_gather x1, waiting for transfers between devices, on_device(): lax.all_gather(jnp.concatenate([qkv_weight, out_weight, gain_block], axis...  29.1 us
    all_to_all x1, waiting for transfers between devices, on_device(): lax.all_to_all(jnp.take(jnp.concatenate([result, d_tokens], axis=-1), to_...  25.2 us
    all_to_all x1, waiting for transfers between devices, on_device(): lax.all_to_all(backward_rows, 'batch', split_axis=0, concat_axis=0, tiled...  13.4 us
    all_to_all x1, waiting for transfers between devices, on_device(): lax.all_to_all(summed.reshape(batches, -1, summed.shape[1]), 'batch', spl...  9.42 us
    all_to_all x1, starting transfers between devices, on_device(): lax.all_to_all(backward_rows, 'batch', split_axis=0, concat_axis=0, tiled...  8.47 us
    all_to_all x1, waiting for transfers between devices, on_device(): lax.all_to_all(jnp.broadcast_to(reduced[None], (batches,) + reduced.shape...  7.74 us
    reshape x2, local copies, waits for them, and re-layouts, layer_core(): qkv.reshape(groups, length, 3, HEADS, head_dim)  7.55 us
  transfers between devices with their start and end apart: 6, of which 6 were waited for; matrix products, arithmetic and copies ran while one was open for 6% of the time, Pallas kernels for 0%

profile of v7, /device:TPU:2, one launch (start us, length us, event | category | flops | bytes accessed | tf_op | source)
XLA Modules:
  0.0 313.5 jit_solution(3089579909730180930)
XLA Ops:
  7.2 0.8 broadcast_in_dim.172
  8.1 1.7 pad_maximum_fusion.2
  10.3 1.3 reduce.14
  11.6 1.3 reduce.13
  13.5 1.2 gather_fusion
  14.7 1.0 select_select_fusion
  15.7 8.5 %all-to-all-start = ((bf16[8,32,1024]{2,1,0:T(8,128)(2,1)}), bf16[8,32,1024]{2,1,0:T(8,128)(2,1)S(1)}, u32[]{:S(2)}, u32[]{:S(2)}) async-start(bf16[8,32,1024]{2,1,0:T(8,128)(2,1)} %select_select_fusion), calls=%async_computation | async-start | bytes 1048576 | tf_op jit(solution)/shard_map/all_to_all | solution.py:134
  24.3 2.8 gather_fusion.3
  28.2 13.4 %all-to-all-done = bf16[8,32,1024]{2,1,0:T(8,128)(2,1)S(1)} async-done(((bf16[8,32,1024]{2,1,0:T(8,128)(2,1)}), bf16[8,32,1024]{2,1,0:T(8,128)(2,1)S(1)}, u32[]{:S(2)}, u32[]{:S(2)}) %all-to-all-start) | async-done | bytes 524320 | tf_op jit(solution)/shard_map/all_to_all | solution.py:134
  42.2 1.0 broadcast_select_fusion.1
  43.3 29.1 %all-gather.2.cloned.1.call-done = bf16[1024,4224]{1,0:T(8,128)(2,1)} async-done(((bf16[32,4224]{1,0:T(8,128)(2,1)}), bf16[1024,4224]{1,0:T(8,128)(2,1)}) %all-gather.2.cloned.1.call-update) | async-done | bytes 8650768 | tf_op jit(solution)/shard_map/all_gather | solution.py:100
  72.4 1.1 convert_reduce_fusion.1
  73.8 2.3 fusion.43
  76.8 6.0 %fusion.6 = bf16[256,3072]{1,0:T(8,128)(2,1)} fusion(bf16[1024,4224]{1,0:T(8,128)(2,1)} %all-gather.2.cloned.1.call-done, f32[1024]{0:T(1024)S(1)} %convert_reduce_fusion.1, f32[256]{0:T(256)S(1)} %rsqrt.13, f32[256]{0:T(256)S(1)} %div.51, bf16[256,1024]{1,0:T(8,128)(2,1)S(1)} %gather_fusion.3, pred[256]{0:T(512)(128)(4,1)S(1)} %compare_and_fusion.4), kind=kOutput, calls=%fused_computation.14 | convolution fusion | flops 1612972032 | bytes 8395008 | tf_op jit(solution)/shard_map/dot_general | solution.py:30
  82.8 4.9 %reshape.390 = bf16[8,32,3,16,64]{4,3,2,1,0:T(8,128)(2,1)} reshape(bf16[256,3072]{1,0:T(8,128)(2,1)} %fusion.6) | data formatting | bytes 3145728 | tf_op jit(solution)/shard_map/reshape | solution.py:31
  87.6 2.7 copy.44
  90.3 1.6 copy-done.3
  91.9 2.0 fusion.64
  94.0 3.8 %fusion.99 = (f32[16,8,32]{2,1,0:T(8,128)S(1)}, f32[16,8,32,32]{2,3,1,0:T(8,128)}) fusion(pred[8,32]{1,0:T(8,128)(4,1)S(1)} %iota_compare_fusion.3, bf16[3,16,8,32,64]{4,3,2,1,0:T(8,128)(2,1)} %bitcast.104), kind=kOutput, calls=%fused_computation.158 | convolution fusion | flops 17301536 | bytes 2638080 | tf_op jit(solution)/shard_map/sub | solution.py:36
  97.7 3.2 %fusion.30 = bf16[1,16,8,32,64]{4,3,2,1,0:T(8,128)(2,1)} fusion(bf16[8,32,16,64]{3,2,1,0:T(8,128)(2,1)S(1)} %reshape.393, f32[16,8,32,32]{2,3,1,0:T(8,128)} %get-tuple-element.34, f32[16,8,32]{2,1,0:T(8,128)S(1)} %get-tuple-element.33), kind=kOutput, calls=%fused_computation.35 | convolution fusion | flops 17301504 | bytes 1589248 | tf_op jit(solution)/shard_map/hgqk,hgqd->hgkd/dot_general | solution.py:49
  100.9 5.6 %fusion.34 = bf16[1,16,8,32,64]{4,3,2,1,0:T(8,128)(2,1)} fusion(f32[16,8,32,32]{2,3,1,0:T(8,128)} %fusion.64, bf16[3,16,8,32,64]{4,3,2,1,0:T(8,128)(2,1)} %bitcast.105, f32[16,8,32,32]{2,3,1,0:T(8,128)} %get-tuple-element.34, f32[16,8,32]{2,1,0:T(8,128)S(1)} %get-tuple-element.33), kind=kOutput, calls=%fused_computation.37 | convolution fusion | flops 17960992 | bytes 10092544 | tf_op jit(solution)/shard_map/hgqk,hgkd->hgqd/dot_general | solution.py:56
  106.5 5.5 %fusion.31 = bf16[1,16,8,32,64]{4,3,2,1,0:T(8,128)(2,1)} fusion(f32[16,8,32,32]{2,3,1,0:T(8,128)} %fusion.64, bf16[3,16,8,32,64]{4,3,2,1,0:T(8,128)(2,1)} %bitcast.106, f32[16,8,32,32]{2,3,1,0:T(8,128)} %get-tuple-element.34, f32[16,8,32]{2,1,0:T(8,128)S(1)} %get-tuple-element.33), kind=kOutput, calls=%fused_computation.36 | convolution fusion | flops 17960992 | bytes 10092544 | tf_op jit(solution)/shard_map/hgqk,hgqd->hgkd/dot_general | solution.py:59
  112.0 2.4 fusion.29
  114.4 0.7 copy.27
  115.0 1.5 reshape.391
  116.6 2.6 maximum_bitcast_fusion
  119.2 3.7 %copy.30 = bf16[8,32,3,16,64]{4,3,2,1,0:T(8,128)(2,1)} copy(bf16[8,32,3,16,64]{4,1,0,3,2:T(8,128)(2,1)S(1)} %maximum_bitcast_fusion) | data formatting | bytes 3145728 | tf_op jit(solution)/shard_map/transpose | solution.py:62
  122.9 4.2 %reshape.394 = bf16[256,3072]{1,0:T(8,128)(2,1)S(1)} reshape(bf16[8,32,3,16,64]{4,3,2,1,0:T(8,128)(2,1)} %copy.30) | data formatting | bytes 3145728 | tf_op jit(solution)/shard_map/reshape | solution.py:62
  127.1 1.9 convolution_convert_fusion.1
  129.1 1.8 convolution_convert_fusion
  130.9 5.7 %fusion.62 = (bf16[1024]{0:T(1024)(128)(2,1)S(1)}, f32[256]{0:T(256)S(1)}, f32[256]{0:T(256)S(1)}, f32[256,1024]{1,0:T(8,128)}) fusion(f32[256]{0:T(256)S(1)} %rsqrt.13, f32[256]{0:T(256)S(1)} %div.51, bf16[256,1024]{1,0:T(8,128)(2,1)S(1)} %gather_fusion.3, pred[256]{0:T(512)(128)(4,1)S(1)} %compare_and_fusion.4, f32[1024]{0:T(1024)S(1)} %convert_reduce_fusion.1, ...), kind=kOutput, calls=%fused_computation.60 | convolution fusion | flops 1613232640 | bytes 9447680 | tf_op jit(solution)/shard_map/dot_general | solution.py:65
  136.8 3.8 %pad_maximum_fusion = bf16[1024,4224]{1,0:T(8,128)(2,1)} fusion(bf16[1024,128]{1,0:T(8,128)(2,1)S(1)} %broadcast_in_dim.187, bf16[1024,1024]{1,0:T(8,128)(2,1)S(1)} %convolution_convert_fusion.1, bf16[1024,3072]{1,0:T(8,128)(2,1)S(1)} %convolution_convert_fusion), kind=kLoop, calls=%fused_computation.8 | loop fusion | flops 25952256 | bytes 17301504 | tf_op jit(solution)/shard_map/concatenate | solution.py:152
  140.8 1.0 copy-done.5
  142.4 2.3 fusion.40
  145.4 96.1 %reduce-scatter.2.cloned.1.call-done = bf16[32,4224]{1,0:T(8,128)(2,1)} async-done(((bf16[1024,4224]{1,0:T(8,128)(2,1)}), bf16[32,4224]{1,0:T(8,128)(2,1)}) %reduce-scatter.2.cloned.1.call-update) | async-done | bytes 270352 | tf_op jit(solution)/shard_map/reduce_scatter | solution.py:160
  241.5 1.7 reshape.398
  243.2 7.0 %all-to-all-start.2 = ((bf16[8,4,4224]{2,1,0:T(4,128)(2,1)}), bf16[8,4,4224]{2,1,0:T(4,128)(2,1)S(1)}, u32[]{:S(2)}, u32[]{:S(2)}) async-start(bf16[8,4,4224]{2,1,0:T(4,128)(2,1)} %reshape.398), calls=%async_computation.3 | async-start | bytes 540672 | tf_op jit(solution)/shard_map/all_to_all | solution.py:161
  250.2 1.2 broadcast_select_fusion
  251.4 9.4 %all-to-all-done.2 = bf16[8,4,4224]{2,1,0:T(4,128)(2,1)S(1)} async-done(((bf16[8,4,4224]{2,1,0:T(4,128)(2,1)}), bf16[8,4,4224]{2,1,0:T(4,128)(2,1)S(1)}, u32[]{:S(2)}, u32[]{:S(2)}) %all-to-all-start.2) | async-done | bytes 270368 | tf_op jit(solution)/shard_map/all_to_all | solution.py:161
  260.8 3.6 %all-to-all-start.1 = ((bf16[8,32,2048]{2,1,0:T(8,128)(2,1)}), bf16[8,32,2048]{2,1,0:T(8,128)(2,1)S(1)}, u32[]{:S(2)}, u32[]{:S(2)}) async-start(bf16[8,32,2048]{2,1,0:T(8,128)(2,1)} %broadcast_select_fusion), calls=%async_computation.1 | async-start | bytes 2097152 | tf_op jit(solution)/shard_map/all_to_all | solution.py:141
  264.6 25.2 %all-to-all-done.1 = bf16[8,32,2048]{2,1,0:T(8,128)(2,1)S(1)} async-done(((bf16[8,32,2048]{2,1,0:T(8,128)(2,1)}), bf16[8,32,2048]{2,1,0:T(8,128)(2,1)S(1)}, u32[]{:S(2)}, u32[]{:S(2)}) %all-to-all-start.1) | async-done | bytes 1048608 | tf_op jit(solution)/shard_map/all_to_all | solution.py:141
  289.8 0.8 broadcast_in_dim.188
  290.6 3.4 %all-to-all-start.3 = ((bf16[8,4,4224]{2,1,0:T(4,128)(2,1)}), bf16[8,4,4224]{2,1,0:T(4,128)(2,1)S(1)}, u32[]{:S(2)}, u32[]{:S(2)}) async-start(bf16[8,4,4224]{2,1,0:T(4,128)(2,1)} %broadcast_in_dim.188), calls=%async_computation.4 | async-start | bytes 540672 | tf_op jit(solution)/shard_map/all_to_all | solution.py:165
  294.1 0.9 gather_fusion.5
  295.0 0.9 gather_fusion.4
  295.9 0.9 select_bitcast_fusion
  296.8 7.7 %all-to-all-done.3 = bf16[8,4,4224]{2,1,0:T(4,128)(2,1)S(1)} async-done(((bf16[8,4,4224]{2,1,0:T(4,128)(2,1)}), bf16[8,4,4224]{2,1,0:T(4,128)(2,1)S(1)}, u32[]{:S(2)}, u32[]{:S(2)}) %all-to-all-start.3) | async-done | bytes 270368 | tf_op jit(solution)/shard_map/all_to_all | solution.py:165
  305.9 0.8 slice.75
  (66 shorter events, 7.2 us)
Async XLA Ops:
  7.2 17.2 %copy-start = (bf16[1,8,64,1024]{3,2,1,0:T(8,128)(2,1)S(1)}, bf16[1,8,64,1024]{3,2,1,0:T(8,128)(2,1)}, u32[]{:S(2)}) copy-start(bf16[1,8,64,1024]{3,2,1,0:T(8,128)(2,1)} %param.12) | copy-start | bytes 3145732
  7.2 6.3 %copy-start.2 = (bf16[1,128,1024]{2,1,0:T(8,128)(2,1)S(1)}, bf16[1,128,1024]{2,1,0:T(8,128)(2,1)}, u32[]{:S(2)}) copy-start(bf16[1,128,1024]{2,1,0:T(8,128)(2,1)} %param.19) | copy-start | bytes 786436
  7.2 65.2 %all-gather.2.cloned.1.call-start = ((), (), s32[]{:S(2)}) async-start(), calls=%async_computation.5 | async-start | bytes 8921088 | tf_op jit(solution)/shard_map/all_gather | solution.py:100
  14.6 9.6 %copy-start.6 = (s32[1,8,64]{2,1,0:T(8,128)S(1)}, s32[1,8,64]{2,1,0:T(8,128)}, u32[]{:S(2)}) copy-start(s32[1,8,64]{2,1,0:T(8,128)} %param.13) | copy-start | bytes 6148
  15.7 26.0 %all-to-all-start = ((bf16[8,32,1024]{2,1,0:T(8,128)(2,1)}), bf16[8,32,1024]{2,1,0:T(8,128)(2,1)S(1)}, u32[]{:S(2)}, u32[]{:S(2)}) async-start(bf16[8,32,1024]{2,1,0:T(8,128)(2,1)} %select_select_fusion), calls=%async_computation | async-start | bytes 1048576 | tf_op jit(solution)/shard_map/all_to_all | solution.py:134
  24.2 217.3 %reduce-scatter.2.cloned.1.call-start = ((), (), s32[]{:S(2)}) async-start(), calls=%async_computation.6 | async-start | bytes 8921088 | tf_op jit(solution)/shard_map/reduce_scatter | solution.py:160
  90.3 1.6 copy-start.3
  140.6 1.2 copy-start.5
  140.7 1.7 copy-start.4
  243.2 17.6 %all-to-all-start.2 = ((bf16[8,4,4224]{2,1,0:T(4,128)(2,1)}), bf16[8,4,4224]{2,1,0:T(4,128)(2,1)S(1)}, u32[]{:S(2)}, u32[]{:S(2)}) async-start(bf16[8,4,4224]{2,1,0:T(4,128)(2,1)} %reshape.398), calls=%async_computation.3 | async-start | bytes 540672 | tf_op jit(solution)/shard_map/all_to_all | solution.py:161
  260.8 29.0 %all-to-all-start.1 = ((bf16[8,32,2048]{2,1,0:T(8,128)(2,1)}), bf16[8,32,2048]{2,1,0:T(8,128)(2,1)S(1)}, u32[]{:S(2)}, u32[]{:S(2)}) async-start(bf16[8,32,2048]{2,1,0:T(8,128)(2,1)} %broadcast_select_fusion), calls=%async_computation.1 | async-start | bytes 2097152 | tf_op jit(solution)/shard_map/all_to_all | solution.py:141
  290.6 13.9 %all-to-all-start.3 = ((bf16[8,4,4224]{2,1,0:T(4,128)(2,1)}), bf16[8,4,4224]{2,1,0:T(4,128)(2,1)S(1)}, u32[]{:S(2)}, u32[]{:S(2)}) async-start(bf16[8,4,4224]{2,1,0:T(4,128)(2,1)} %broadcast_in_dim.188), calls=%async_computation.4 | async-start | bytes 540672 | tf_op jit(solution)/shard_map/all_to_all | solution.py:165
  295.0 11.6 %copy-start.1 = (bf16[1,8,64,1024]{3,2,1,0:T(8,128)(2,1)S(1)}, bf16[1,8,64,1024]{3,2,1,0:T(8,128)(2,1)}, u32[]{:S(2)}) copy-start(bf16[1,8,64,1024]{3,2,1,0:T(8,128)(2,1)} %param.12) | copy-start | bytes 3145732
Sparse Core Ops, SparseCore 0:
  11.1 61.2 all-gather.1
  140.8 100.6 reduce-scatter.1

commit v8 on v4

--- a/solution.py
+++ b/solution.py
@@ -172,10 +172,10 @@
         concat_axis=0,
         tiled=True,
     )
-    summed = summed.reshape(-1, summed.shape[2]).astype(jnp.float32)
-    grad_q = summed[:, :qkv_cols]
-    grad_o = summed[:, qkv_cols : qkv_cols + out_cols]
-    grad_g = summed[:, qkv_cols + out_cols]
+    summed = summed.reshape(-1, summed.shape[2])
+    grad_q = summed[:, :qkv_cols].astype(jnp.float32)
+    grad_o = summed[:, qkv_cols : qkv_cols + out_cols].astype(jnp.float32)
+    grad_g = summed[:, qkv_cols + out_cols].astype(jnp.float32)
     return (layer_out[None], d_packed[None], grad_q, grad_o, grad_g)
 
 

time: 310 us -> 310 us (level)
  no operation moved by 1% of the time
where the time goes in v8:
time: 310 us; the launch traced here: 309 us
  waiting for transfers between devices  182 us (59%)
  matrix products  40.6 us (13%)
  local copies, waits for them, and re-layouts  31 us (10%)
  starting transfers between devices  22.5 us (7%)
  other arithmetic  18.8 us (6%)
  between operations  14.4 us (5%)
    reduce_scatter x1, waiting for transfers between devices, on_device(): lax.psum_scatter(partial, 'replica', scatter_dimension=0, tiled=True)  95.8 us
    all_gather x1, waiting for transfers between devices, on_device(): lax.all_gather(jnp.concatenate([qkv_weight, out_weight, gain_block], axis...  30.2 us
    all_to_all x1, waiting for transfers between devices, on_device(): lax.all_to_all(jnp.take(jnp.concatenate([result, d_tokens], axis=-1), to_...  25.2 us
    all_to_all x1, waiting for transfers between devices, on_device(): lax.all_to_all(backward_rows, 'batch', split_axis=0, concat_axis=0, tiled...  13.6 us
    all_to_all x1, waiting for transfers between devices, on_device(): lax.all_to_all(summed.reshape(batches, -1, summed.shape[1]), 'batch', spl...  9.42 us
    all_to_all x1, starting transfers between devices, on_device(): lax.all_to_all(backward_rows, 'batch', split_axis=0, concat_axis=0, tiled...  8.47 us
    all_to_all x1, waiting for transfers between devices, on_device(): lax.all_to_all(jnp.broadcast_to(reduced[None], (batches,) + reduced.shape...  7.74 us
    all_to_all x1, starting transfers between devices, on_device(): lax.all_to_all(summed.reshape(batches, -1, summed.shape[1]), 'batch', spl...  7.01 us
  transfers between devices with their start and end apart: 6, of which 6 were waited for; matrix products, arithmetic and copies ran while one was open for 6% of the time, Pallas kernels for 0%

profile of v8, /device:TPU:2, one launch (start us, length us, event | category | flops | bytes accessed | tf_op | source)
XLA Modules:
  0.0 309.2 jit_solution(4680725117098277309)
XLA Ops:
  7.2 0.8 broadcast_in_dim.172
  8.1 1.7 pad_maximum_fusion.2
  10.3 1.3 reduce.14
  11.6 1.3 reduce.13
  13.5 1.2 gather_fusion
  14.7 1.0 select_select_fusion
  15.7 8.5 %all-to-all-start = ((bf16[8,32,1024]{2,1,0:T(8,128)(2,1)}), bf16[8,32,1024]{2,1,0:T(8,128)(2,1)S(1)}, u32[]{:S(2)}, u32[]{:S(2)}) async-start(bf16[8,32,1024]{2,1,0:T(8,128)(2,1)} %select_select_fusion), calls=%async_computation | async-start | bytes 1048576 | tf_op jit(solution)/shard_map/all_to_all | solution.py:137
  24.3 2.8 gather_fusion.3
  28.1 13.6 %all-to-all-done = bf16[8,32,1024]{2,1,0:T(8,128)(2,1)S(1)} async-done(((bf16[8,32,1024]{2,1,0:T(8,128)(2,1)}), bf16[8,32,1024]{2,1,0:T(8,128)(2,1)S(1)}, u32[]{:S(2)}, u32[]{:S(2)}) %all-to-all-start) | async-done | bytes 524320 | tf_op jit(solution)/shard_map/all_to_all | solution.py:137
  42.2 30.2 %all-gather.2.cloned.1.call-done = bf16[1024,4224]{1,0:T(8,128)(2,1)} async-done(((bf16[32,4224]{1,0:T(8,128)(2,1)}), bf16[1024,4224]{1,0:T(8,128)(2,1)}) %all-gather.2.cloned.1.call-update) | async-done | bytes 8650768 | tf_op jit(solution)/shard_map/all_gather | solution.py:103
  72.4 1.1 convert_reduce_fusion.1
  73.8 4.7 %fusion.6 = bf16[256,3072]{1,0:T(8,128)(2,1)S(1)} fusion(bf16[1024,4224]{1,0:T(8,128)(2,1)} %all-gather.2.cloned.1.call-done, f32[1024]{0:T(1024)S(1)} %convert_reduce_fusion.1, f32[256]{0:T(256)S(1)} %rsqrt.13, f32[256]{0:T(256)S(1)} %div.51, bf16[256,1024]{1,0:T(8,128)(2,1)S(1)} %gather_fusion.3, pred[256]{0:T(512)(128)(4,1)S(1)} %compare_and_fusion.4), kind=kOutput, calls=%fused_computation.15 | convolution fusion | flops 1612972032 | bytes 8395008 | tf_op jit(solution)/shard_map/dot_general | solution.py:30
  78.5 3.6 %reshape.363 = bf16[8,32,3,16,64]{4,3,2,1,0:T(8,128)(2,1)} reshape(bf16[256,3072]{1,0:T(8,128)(2,1)S(1)} %fusion.6) | data formatting | bytes 3145728 | tf_op jit(solution)/shard_map/reshape | solution.py:31
  82.1 2.7 copy.33
  84.8 2.9 slice.72
  87.7 1.3 fusion.32
  89.2 1.0 copy-done.6
  90.2 2.0 fusion.57
  92.2 3.8 %fusion.87 = (f32[16,8,32]{2,1,0:T(8,128)S(1)}, f32[16,8,32,32]{2,3,1,0:T(8,128)}) fusion(pred[8,32]{1,0:T(8,128)(4,1)S(1)} %iota_compare_fusion.3, bf16[3,16,8,32,64]{4,3,2,1,0:T(8,128)(2,1)} %bitcast.122), kind=kOutput, calls=%fused_computation.157 | convolution fusion | flops 17301536 | bytes 2638080 | tf_op jit(solution)/shard_map/sub | solution.py:36
  95.9 2.4 fusion.25
  98.5 2.8 convolution_convert_fusion.3
  101.3 5.6 %fusion.29 = bf16[1,16,8,32,64]{4,3,2,1,0:T(8,128)(2,1)} fusion(f32[16,8,32,32]{2,3,1,0:T(8,128)} %fusion.57, bf16[3,16,8,32,64]{4,3,2,1,0:T(8,128)(2,1)} %bitcast.124, f32[16,8,32,32]{2,3,1,0:T(8,128)} %get-tuple-element.34, f32[16,8,32]{2,1,0:T(8,128)S(1)} %get-tuple-element.33), kind=kOutput, calls=%fused_computation.33 | convolution fusion | flops 17960992 | bytes 10092544 | tf_op jit(solution)/shard_map/hgqk,hgkd->hgqd/dot_general | solution.py:56
  106.9 5.6 %fusion.26 = bf16[1,16,8,32,64]{4,3,2,1,0:T(8,128)(2,1)} fusion(f32[16,8,32,32]{2,3,1,0:T(8,128)} %fusion.57, bf16[3,16,8,32,64]{4,3,2,1,0:T(8,128)(2,1)} %bitcast.125, f32[16,8,32,32]{2,3,1,0:T(8,128)} %get-tuple-element.34, f32[16,8,32]{2,1,0:T(8,128)S(1)} %get-tuple-element.33), kind=kOutput, calls=%fused_computation.32 | convolution fusion | flops 17960992 | bytes 10092544 | tf_op jit(solution)/shard_map/hgqk,hgqd->hgkd/dot_general | solution.py:59
  112.5 2.3 maximum_bitcast_fusion
  114.8 3.7 %copy.26 = bf16[8,32,3,16,64]{4,3,2,1,0:T(8,128)(2,1)} copy(bf16[8,32,3,16,64]{4,1,0,3,2:T(8,128)(2,1)S(1)} %maximum_bitcast_fusion) | data formatting | bytes 3145728 | tf_op jit(solution)/shard_map/transpose | solution.py:62
  118.5 4.2 %reshape.366 = bf16[256,3072]{1,0:T(8,128)(2,1)S(1)} reshape(bf16[8,32,3,16,64]{4,3,2,1,0:T(8,128)(2,1)} %copy.26) | data formatting | bytes 3145728 | tf_op jit(solution)/shard_map/reshape | solution.py:62
  122.7 2.0 bitcast_convert_fusion
  124.8 1.8 convolution_convert_fusion
  126.6 5.9 %fusion.50 = (bf16[1024]{0:T(1024)(128)(2,1)S(1)}, f32[256]{0:T(256)S(1)}, f32[256]{0:T(256)S(1)}, f32[256,1024]{1,0:T(8,128)}) fusion(f32[256]{0:T(256)S(1)} %rsqrt.13, f32[256]{0:T(256)S(1)} %div.51, bf16[256,1024]{1,0:T(8,128)(2,1)S(1)} %gather_fusion.3, pred[256]{0:T(512)(128)(4,1)S(1)} %compare_and_fusion.4, f32[1024]{0:T(1024)S(1)} %convert_reduce_fusion.1, ...), kind=kOutput, calls=%fused_computation.57 | convolution fusion | flops 1613232640 | bytes 9447680 | tf_op jit(solution)/shard_map/dot_general | solution.py:65
  132.7 3.7 %pad_maximum_fusion = bf16[1024,4224]{1,0:T(8,128)(2,1)} fusion(bf16[1024,128]{1,0:T(8,128)(2,1)S(1)} %broadcast_in_dim.187, bf16[1024,1024]{1,0:T(8,128)(2,1)S(1)} %bitcast.120, bf16[1024,3072]{1,0:T(8,128)(2,1)S(1)} %convolution_convert_fusion), kind=kLoop, calls=%fused_computation.8 | loop fusion | flops 25952256 | bytes 17301504 | tf_op jit(solution)/shard_map/concatenate | solution.py:155
  136.7 0.9 copy-done.5
  138.1 2.7 fusion.33
  141.5 95.8 %reduce-scatter.2.cloned.1.call-done = bf16[32,4224]{1,0:T(8,128)(2,1)} async-done(((bf16[1024,4224]{1,0:T(8,128)(2,1)}), bf16[32,4224]{1,0:T(8,128)(2,1)}) %reduce-scatter.2.cloned.1.call-update) | async-done | bytes 270352 | tf_op jit(solution)/shard_map/reduce_scatter | solution.py:163
  237.2 1.7 reshape.370
  239.0 7.0 %all-to-all-start.2 = ((bf16[8,4,4224]{2,1,0:T(4,128)(2,1)}), bf16[8,4,4224]{2,1,0:T(4,128)(2,1)S(1)}, u32[]{:S(2)}, u32[]{:S(2)}) async-start(bf16[8,4,4224]{2,1,0:T(4,128)(2,1)} %reshape.370), calls=%async_computation.3 | async-start | bytes 540672 | tf_op jit(solution)/shard_map/all_to_all | solution.py:164
  246.0 1.2 broadcast_select_fusion
  247.1 9.4 %all-to-all-done.2 = bf16[8,4,4224]{2,1,0:T(4,128)(2,1)S(1)} async-done(((bf16[8,4,4224]{2,1,0:T(4,128)(2,1)}), bf16[8,4,4224]{2,1,0:T(4,128)(2,1)S(1)}, u32[]{:S(2)}, u32[]{:S(2)}) %all-to-all-start.2) | async-done | bytes 270368 | tf_op jit(solution)/shard_map/all_to_all | solution.py:164
  256.5 3.6 %all-to-all-start.1 = ((bf16[8,32,2048]{2,1,0:T(8,128)(2,1)}), bf16[8,32,2048]{2,1,0:T(8,128)(2,1)S(1)}, u32[]{:S(2)}, u32[]{:S(2)}) async-start(bf16[8,32,2048]{2,1,0:T(8,128)(2,1)} %broadcast_select_fusion), calls=%async_computation.1 | async-start | bytes 2097152 | tf_op jit(solution)/shard_map/all_to_all | solution.py:144
  260.3 25.2 %all-to-all-done.1 = bf16[8,32,2048]{2,1,0:T(8,128)(2,1)S(1)} async-done(((bf16[8,32,2048]{2,1,0:T(8,128)(2,1)}), bf16[8,32,2048]{2,1,0:T(8,128)(2,1)S(1)}, u32[]{:S(2)}, u32[]{:S(2)}) %all-to-all-start.1) | async-done | bytes 1048608 | tf_op jit(solution)/shard_map/all_to_all | solution.py:144
  285.6 0.8 broadcast_in_dim.188
  286.4 3.4 %all-to-all-start.3 = ((bf16[8,4,4224]{2,1,0:T(4,128)(2,1)}), bf16[8,4,4224]{2,1,0:T(4,128)(2,1)S(1)}, u32[]{:S(2)}, u32[]{:S(2)}) async-start(bf16[8,4,4224]{2,1,0:T(4,128)(2,1)} %broadcast_in_dim.188), calls=%async_computation.4 | async-start | bytes 540672 | tf_op jit(solution)/shard_map/all_to_all | solution.py:168
  289.9 0.9 gather_fusion.5
  290.7 0.9 gather_fusion.4
  291.6 0.9 select_bitcast_fusion
  292.5 7.7 %all-to-all-done.3 = bf16[8,4,4224]{2,1,0:T(4,128)(2,1)S(1)} async-done(((bf16[8,4,4224]{2,1,0:T(4,128)(2,1)}), bf16[8,4,4224]{2,1,0:T(4,128)(2,1)S(1)}, u32[]{:S(2)}, u32[]{:S(2)}) %all-to-all-start.3) | async-done | bytes 270368 | tf_op jit(solution)/shard_map/all_to_all | solution.py:168
  300.3 0.6 convert_reduce_fusion.2
  301.0 0.7 slice_convert_fusion.1
  301.6 0.8 slice_convert_fusion
  (66 shorter events, 5.4 us)
Async XLA Ops:
  7.2 17.2 %copy-start = (bf16[1,8,64,1024]{3,2,1,0:T(8,128)(2,1)S(1)}, bf16[1,8,64,1024]{3,2,1,0:T(8,128)(2,1)}, u32[]{:S(2)}) copy-start(bf16[1,8,64,1024]{3,2,1,0:T(8,128)(2,1)} %param.12) | copy-start | bytes 3145732
  7.2 6.3 %copy-start.2 = (bf16[1,128,1024]{2,1,0:T(8,128)(2,1)S(1)}, bf16[1,128,1024]{2,1,0:T(8,128)(2,1)}, u32[]{:S(2)}) copy-start(bf16[1,128,1024]{2,1,0:T(8,128)(2,1)} %param.19) | copy-start | bytes 786436
  7.2 65.2 %all-gather.2.cloned.1.call-start = ((), (), s32[]{:S(2)}) async-start(), calls=%async_computation.5 | async-start | bytes 8921088 | tf_op jit(solution)/shard_map/all_gather | solution.py:103
  14.6 9.6 %copy-start.7 = (s32[1,8,64]{2,1,0:T(8,128)S(1)}, s32[1,8,64]{2,1,0:T(8,128)}, u32[]{:S(2)}) copy-start(s32[1,8,64]{2,1,0:T(8,128)} %param.13) | copy-start | bytes 6148
  15.7 26.0 %all-to-all-start = ((bf16[8,32,1024]{2,1,0:T(8,128)(2,1)}), bf16[8,32,1024]{2,1,0:T(8,128)(2,1)S(1)}, u32[]{:S(2)}, u32[]{:S(2)}) async-start(bf16[8,32,1024]{2,1,0:T(8,128)(2,1)} %select_select_fusion), calls=%async_computation | async-start | bytes 1048576 | tf_op jit(solution)/shard_map/all_to_all | solution.py:137
  24.2 213.1 %reduce-scatter.2.cloned.1.call-start = ((), (), s32[]{:S(2)}) async-start(), calls=%async_computation.6 | async-start | bytes 8921088 | tf_op jit(solution)/shard_map/reduce_scatter | solution.py:163
  84.8 4.4 %copy-start.3 = (bf16[8,32,3,16,64]{4,1,0,3,2:T(8,128)(2,1)}, bf16[8,32,3,16,64]{4,1,0,3,2:T(8,128)(2,1)S(1)}, u32[]{:S(2)}) copy-start(bf16[8,32,3,16,64]{4,1,0,3,2:T(8,128)(2,1)S(1)} %copy.33) | copy-start | bytes 4718596
  87.7 1.5 copy-start.4
  89.2 1.0 copy-start.6
  95.9 2.5 copy-start.8
  136.3 1.2 copy-start.5
  239.0 17.6 %all-to-all-start.2 = ((bf16[8,4,4224]{2,1,0:T(4,128)(2,1)}), bf16[8,4,4224]{2,1,0:T(4,128)(2,1)S(1)}, u32[]{:S(2)}, u32[]{:S(2)}) async-start(bf16[8,4,4224]{2,1,0:T(4,128)(2,1)} %reshape.370), calls=%async_computation.3 | async-start | bytes 540672 | tf_op jit(solution)/shard_map/all_to_all | solution.py:164
  256.5 29.0 %all-to-all-start.1 = ((bf16[8,32,2048]{2,1,0:T(8,128)(2,1)}), bf16[8,32,2048]{2,1,0:T(8,128)(2,1)S(1)}, u32[]{:S(2)}, u32[]{:S(2)}) async-start(bf16[8,32,2048]{2,1,0:T(8,128)(2,1)} %broadcast_select_fusion), calls=%async_computation.1 | async-start | bytes 2097152 | tf_op jit(solution)/shard_map/all_to_all | solution.py:144
  286.4 13.9 %all-to-all-start.3 = ((bf16[8,4,4224]{2,1,0:T(4,128)(2,1)}), bf16[8,4,4224]{2,1,0:T(4,128)(2,1)S(1)}, u32[]{:S(2)}, u32[]{:S(2)}) async-start(bf16[8,4,4224]{2,1,0:T(4,128)(2,1)} %broadcast_in_dim.188), calls=%async_computation.4 | async-start | bytes 540672 | tf_op jit(solution)/shard_map/all_to_all | solution.py:168
  290.7 11.7 %copy-start.1 = (bf16[1,8,64,1024]{3,2,1,0:T(8,128)(2,1)S(1)}, bf16[1,8,64,1024]{3,2,1,0:T(8,128)(2,1)}, u32[]{:S(2)}) copy-start(bf16[1,8,64,1024]{3,2,1,0:T(8,128)(2,1)} %param.12) | copy-start | bytes 3145732
Sparse Core Ops, SparseCore 0:
  11.1 61.2 all-gather.1
  136.5 100.6 reduce-scatter.1
